TPU v7x, 32 devices: a whole 2x2x4 slice. The times are simulated.
32 devices in a mesh: grp: 2 (over x), tile: 16 (over z, y, core).
Axes of the slice: x: 2, y: 2, z: 4, core: 2. Of those that a mesh axis runs over, the one named last changes fastest.
Arguments:
- latents: bfloat16 [384, 16, 8, 256], P(('grp', 'tile')), parts along dimension 0, may hold values from -6 to 6
- frame_counts: int32 [32], P('grp'), parts along dimension 0, may hold values from 1 to 12, 64 in all
- clip_order: int32 [32], P('grp'), parts along dimension 0, may hold values from 0 to 15, each once
- norm_scale: float32 [256], replicated, may hold values from 0.25 to 1.75
- norm_offset: float32 [256], replicated, may hold values from -3 to 3
- conv_weight: bfloat16 [3, 3, 3, 256, 256], replicated, may hold values from -0.078125 to 0.078125
- conv_bias: float32 [256], replicated, may hold values from -3 to 3
- out_scale: float32 [256], replicated, may hold values from 0.25 to 1.75
- out_offset: float32 [256], replicated, may hold values from -3 to 3
Outputs:
- block_out: bfloat16 [2, 1024, 8, 256], P(None, ('grp', 'tile')), parts along dimension 1
- normed: bfloat16 [2, 1024, 8, 256], P(None, ('grp', 'tile')), parts along dimension 1
There are 2 independent parts, one for each index of `grp`. A program takes and returns all parts, laid end to end along the dimension named above; an argument that names none is the same for every part. Nothing has to cross between parts.
Inputs may be any that keep to these rules, and one draw needn't show every extreme that they name: `frame_counts`: they sum to 64; the largest is exactly 12. `clip_order`: A permutation of the clips.
All inputs are finite; a program needn't handle non-finite values.
Results may differ from a plain program's by a relative error of at most 0.0057.
Values may be sent and summed in bfloat16 or wider, within the bound.
No kernel may reach another device: no remote copies, remote signals or barrier semaphores. Data moves between devices by JAX's collectives and lax.ppermute only.
A program may use at most 64 MiB of HBM per device.

v0:
```python
import jax
import jax.numpy as jnp
from jax import lax
from jax.sharding import PartitionSpec as P

GROUPS = 32
MEANF = 4
NRB = 8


eps = 1e-06


def normalize(values, frame_count, scaling, offsets):
    frames = values.shape[0]
    channels = values.shape[-1]
    grouped = values.reshape(frames, -1, GROUPS, channels // GROUPS)
    live_mask = (jnp.arange(frames) < frame_count).astype(jnp.float32)[:, None, None, None]
    members = frame_count.astype(jnp.float32) * grouped.shape[1] * grouped.shape[3]
    group_mean = jnp.sum(grouped * live_mask, axis=(0, 1, 3)) / members
    spread = (
        jnp.sum(grouped * grouped * live_mask, axis=(0, 1, 3)) / members - group_mean * group_mean
    )
    inverse = lax.rsqrt(spread + eps)
    normed = (grouped - group_mean[:, None]) * inverse[:, None] * scaling.reshape(
        GROUPS, -1
    ) + offsets.reshape(GROUPS, -1)
    return jax.nn.silu(normed).reshape(values.shape)


def convolve(stacked, kernel, offsets):
    tile_rows = stacked.shape[1] - 2
    columns = stacked.shape[3]
    channels = stacked.shape[4]
    padded = jnp.pad(stacked, ((0, 0), (0, 0), (0, 0), (1, 1), (0, 0)))
    tap_list = [
        padded[frame_lag, row_tap : row_tap + tile_rows, :, col_tap : col_tap + columns]
        for frame_lag in range(3)
        for row_tap in range(3)
        for col_tap in range(3)
    ]
    unfolded = jnp.concatenate(tap_list, axis=-1)
    result = jnp.dot(
        unfolded.reshape(-1, 27 * channels),
        kernel.reshape(27 * channels, -1),
        preferred_element_type=jnp.float32,
    )
    return (result + offsets).reshape(tile_rows, stacked.shape[2], columns, -1)


def local(
    latents,
    frame_counts,
    clip_order,
    norm_scale,
    norm_offset,
    conv_weight,
    conv_bias,
    out_scale,
    out_offset,
):
    devices = lax.axis_size("tile")
    device = lax.axis_index("tile")
    frames, frame_rows, columns, channels = latents.shape
    tile_rows = frame_rows // NRB
    own_tiles = frames * NRB
    capacity = (own_tiles + devices - 1) // devices
    slots_all = devices * capacity
    worker_tiles = MEANF * NRB
    positions = jnp.arange(frame_counts.shape[0], dtype=jnp.int32)
    chosen = clip_order[:, None] == positions[None, :]
    ordered = jnp.sum(jnp.where(chosen, frame_counts[None, :], 0), axis=1)
    starts = (jnp.cumsum(ordered) - ordered) * NRB
    own_start = jnp.sum(jnp.where(clip_order == device, starts, 0))
    own_count = jnp.sum(jnp.where(positions == device, frame_counts, 0))
    active = normalize(latents.astype(jnp.float32), own_count, norm_scale, norm_offset).astype(
        jnp.bfloat16
    )
    outgoing_slot = jnp.arange(slots_all, dtype=jnp.int32)
    target = outgoing_slot // capacity
    source_tile = outgoing_slot % capacity * devices + (target - own_start) % devices
    sendable = source_tile < own_count * NRB
    source_tile = jnp.minimum(source_tile, own_tiles - 1)
    local_slot = jnp.arange(worker_tiles, dtype=jnp.int32)
    tile_id = local_slot * devices + device
    placed = jnp.sum((starts[None, :] <= tile_id[:, None]).astype(jnp.int32), axis=1) - 1
    at_place = placed[:, None] == positions[None, :]
    clip_id = jnp.sum(jnp.where(at_place, clip_order[None, :], 0), axis=1)
    within = tile_id - jnp.sum(jnp.where(at_place, starts[None, :], 0), axis=1)
    take_from = clip_id * capacity + within // devices
    padded = jnp.pad(active, ((2, 0), (1, 1), (0, 0), (0, 0)))
    lagged = []
    for frame_lag in range(3):
        window = padded[frame_lag : frame_lag + frames]
        row_bands = [
            window[:, row_start : row_start + NRB * tile_rows : tile_rows]
            for row_start in range(tile_rows + 2)
        ]
        lagged.append(jnp.stack(row_bands, 0))
    pieces = jnp.stack(lagged, 0).reshape(3, tile_rows + 2, own_tiles, columns, channels)
    outgoing = jnp.where(
        sendable[None, None, :, None, None], jnp.take(pieces, source_tile, axis=2), 0
    )
    received = lax.all_to_all(outgoing, "tile", split_axis=2, concat_axis=2, tiled=True)
    stacked = jnp.take(received, take_from, axis=2)
    block_out = convolve(stacked, conv_weight, conv_bias).astype(jnp.bfloat16)
    per_group = channels // GROUPS
    grouped = block_out.astype(jnp.float32).reshape(
        tile_rows, worker_tiles, columns, GROUPS, per_group
    )
    first_sum = jnp.sum(grouped, axis=(0, 2, 4))
    second_sum = jnp.sum(grouped * grouped, axis=(0, 2, 4))
    belongs = (clip_id[:, None] == positions[None, :]).astype(jnp.float32)
    totals = lax.psum(
        (
            jnp.dot(belongs.T, first_sum, precision=lax.Precision.HIGHEST),
            jnp.dot(belongs.T, second_sum, precision=lax.Precision.HIGHEST),
        ),
        "tile",
    )
    members = frame_counts.astype(jnp.float32) * (frame_rows * columns * per_group)
    clip_mean = totals[0] / members[:, None]
    clip_spread = totals[1] / members[:, None] - clip_mean * clip_mean
    clip_inverse = lax.rsqrt(clip_spread + eps)
    tile_mean = jnp.dot(belongs, clip_mean, precision=lax.Precision.HIGHEST)
    tile_inverse = jnp.dot(belongs, clip_inverse, precision=lax.Precision.HIGHEST)
    normed = (grouped - tile_mean[None, :, None, :, None]) * tile_inverse[
        None, :, None, :, None
    ] * out_scale.reshape(GROUPS, per_group) + out_offset.reshape(GROUPS, per_group)
    normed = jax.nn.silu(normed).astype(jnp.bfloat16).reshape(block_out.shape)
    return (block_out, normed)


def solution(mesh):
    in_specs = (
        P(("grp", "tile"), None, None, None),
        P("grp"),
        P("grp"),
        P(),
        P(),
        P(),
        P(),
        P(),
        P(),
    )
    out_specs = (P(None, ("grp", "tile"), None, None), P(None, ("grp", "tile"), None, None))
    return jax.shard_map(local, mesh=mesh, in_specs=in_specs, out_specs=out_specs, check_vma=False)
```

profile of v0, /device:TPU:0, one launch (start us, length us, event | category | flops | bytes accessed | tf_op | source)
XLA Modules:
  0.0 250.5 jit_solution(12813425869111469504)
XLA Ops:
  2.4 2.0 fusion.32
  5.5 1.2 fusion.39
  6.7 1.3 compare_and_fusion
  8.0 2.2 fusion.11
  11.0 1.4 reduce_sum.116
  17.1 1.7 fusion.9
  19.1 1.3 fusion.44
  20.3 1.2 fusion.46
  24.0 5.2 %maximum_maximum_fusion = bf16[3,4,96,8,256]{4,3,2,1,0:T(8,128)(2,1)} fusion(bf16[1,1,96,8,256]{4,3,2,1,0:T(8,128)(2,1)} %bitcast.72, bf16[1,1,96,8,256]{4,3,2,1,0:T(8,128)(2,1)} %bitcast.73, bf16[1,1,96,8,256]{4,3,2,1,0:T(8,128)(2,1)} %bitcast.74, bf16[1,1,96,8,256]{4,3,2,1,0:T(8,128)(2,1)} %bitcast.71, bf16[1,1,96,8,256]{4,3,2,1,0:T(8,128)(2,1)} %bitcast.76, ...), kind=kLoop, calls=%fused_computation.21 | loop fusion | flops 25952256 | bytes 9437184 | tf_op jit(solution)/shard_map/stack | solution.py:100
  29.2 5.9 %gather_fusion = bf16[96,3,4,8,256]{4,3,2,1,0:T(8,128)(2,1)} fusion(bf16[3,4,96,8,256]{4,3,2,1,0:T(8,128)(2,1)} %maximum_maximum_fusion, s32[1024]{0:T(1024)S(1)} %pad_clamp_fusion.1), kind=kCustom, calls=%fused_computation | custom fusion | bytes 9437568 | tf_op jit(solution)/shard_map/jit(_take)/gather | solution.py:102
  35.1 5.1 %select_bitcast_fusion = bf16[3,4,96,8,256]{4,3,1,0,2:T(8,128)(2,1)} fusion(bf16[96,3,4,8,256]{4,3,2,1,0:T(8,128)(2,1)} %gather_fusion, pred[96]{0:T(512)(128)(4,1)S(1)} %broadcast_compare_fusion, pred[96]{0:T(512)(128)(4,1)S(1)} %copy-done.5), kind=kLoop, calls=%fused_computation.22 | loop fusion | flops 4718592 | bytes 9437376 | tf_op jit(solution)/shard_map/jit(_where)/select_n | solution.py:101
  40.2 7.6 %all-to-all-start = ((bf16[3,4,96,8,256]{4,3,1,0,2:T(8,128)(2,1)}), bf16[3,4,96,8,256]{4,3,1,0,2:T(8,128)(2,1)}, u32[]{:S(2)}, u32[]{:S(2)}) async-start(bf16[3,4,96,8,256]{4,3,1,0,2:T(8,128)(2,1)} %select_bitcast_fusion), calls=%async_computation | async-start | bytes 9437184 | tf_op jit(solution)/shard_map/all_to_all | solution.py:104
  48.1 1.2 convert_multiply_fusion.2
  49.3 85.3 %all-to-all-done = bf16[3,4,96,8,256]{4,3,1,0,2:T(8,128)(2,1)} async-done(((bf16[3,4,96,8,256]{4,3,1,0,2:T(8,128)(2,1)}), bf16[3,4,96,8,256]{4,3,1,0,2:T(8,128)(2,1)}, u32[]{:S(2)}, u32[]{:S(2)}) %all-to-all-start) | async-done | bytes 4718624 | tf_op jit(solution)/shard_map/all_to_all | solution.py:104
  134.6 4.9 %copy.83 = bf16[3,4,96,8,256]{4,3,2,1,0:T(8,128)(2,1)} copy(bf16[3,4,96,8,256]{4,3,1,0,2:T(8,128)(2,1)} %all-to-all-done) | data formatting | bytes 9437184 | tf_op jit(solution)/shard_map/all_to_all | solution.py:104
  139.5 4.2 %gather_fusion.1 = bf16[32,3,4,8,256]{4,3,2,1,0:T(8,128)(2,1)} fusion(bf16[3,4,96,8,256]{4,3,2,1,0:T(8,128)(2,1)} %copy.83, s32[1024]{0:T(1024)S(1)} %pad_clamp_fusion), kind=kCustom, calls=%fused_computation.1 | custom fusion | bytes 3145856 | tf_op jit(solution)/shard_map/jit(_take)/gather | solution.py:105
  143.8 1.6 select_bitcast_fusion.1
  148.5 2.7 %fusion.12 = bf16[512,256]{1,0:T(8,128)(2,1)} fusion(bf16[512,6912]{1,0:T(8,128)(2,1)S(1)} %constant_dynamic-update-slice_fusion, bf16[6912,256]{1,0:T(8,128)(2,1)S(1)} %bitcast.66, f32[256]{0:T(256)S(1)} %copy-done.7), kind=kOutput, calls=%fused_computation.40 | convolution fusion | flops 1812201472 | bytes 10880000 | tf_op jit(solution)/shard_map/dot_general | solution.py:43
  151.2 7.0 %reshape.406 = f32[2,32,8,32,8]{4,3,2,1,0:T(8,128)} reshape(bf16[512,256]{1,0:T(8,128)(2,1)} %fusion.12) | data formatting | bytes 786432 | tf_op jit(solution)/shard_map/convert_element_type | solution.py:108
  158.2 5.0 %fusion.42 = (f32[32,32]{1,0:T(8,128)S(1)}, f32[32,32]{1,0:T(8,128)S(1)}) fusion(f32[2,32,8,32,8]{4,3,2,1,0:T(8,128)} %reshape.406), kind=kLoop, calls=%fused_computation.154 | loop fusion | flops 391168 | bytes 532480 | tf_op jit(solution)/shard_map/reduce_sum | solution.py:111
  164.4 77.8 %all-reduce.2 = (f32[16,32]{1,0:T(8,128)}, f32[16,32]{1,0:T(8,128)}) all-reduce(f32[16,32]{1,0:T(8,128)S(1)} %fusion.14, f32[16,32]{1,0:T(8,128)S(1)} %fusion.16), channel_id=1, replica_groups=mesh['grp'=2,'tile'=16] {'tile'}, use_global_device_ids=true, to_apply=%region_14.15 | all-reduce | flops 1024 | bytes 8192 | tf_op jit(solution)/shard_map/psum | solution.py:114
  243.8 1.6 copy.112
  247.1 1.6 copy.114
  248.7 1.9 multiply_convert_fusion
  (102 shorter events, 17.3 us)
Async XLA Ops:
  0.6 147.7 %copy-start = (bf16[3,3,3,256,256]{4,3,2,1,0:T(8,128)(2,1)S(1)}, bf16[3,3,3,256,256]{4,3,2,1,0:T(8,128)(2,1)}, u32[]{:S(2)}) copy-start(bf16[3,3,3,256,256]{4,3,2,1,0:T(8,128)(2,1)} %param.14) | copy-start | bytes 10616836
  1.7 0.5 copy-start.4
  19.1 3.7 %copy-start.6 = (s32[96]{0:T(128)S(1)}, s32[96]{0:T(128)}, u32[]{:S(2)}) copy-start(s32[96]{0:T(128)} %fusion.39) | copy-start | bytes 1156
  29.2 5.9 %copy-start.5 = (pred[96]{0:T(512)(128)(4,1)S(1)}, pred[96]{0:T(512)(128)(4,1)}, u32[]{:S(2)}) copy-start(pred[96]{0:T(512)(128)(4,1)} %compare_and_fusion) | copy-start | bytes 292
  40.2 7.6 %copy-start.3 = (s32[16]{0:T(128)S(1)}, s32[16]{0:T(128)}, u32[]{:S(2)}) copy-start(s32[16]{0:T(128)} %get-tuple-element.11) | copy-start | bytes 196
  40.2 7.7 %copy-start.2 = (s32[16]{0:T(128)S(1)}, s32[16]{0:T(128)}, u32[]{:S(2)}) copy-start(s32[16]{0:T(128)} %param.11) | copy-start | bytes 196
  40.2 94.4 %all-to-all-start = ((bf16[3,4,96,8,256]{4,3,1,0,2:T(8,128)(2,1)}), bf16[3,4,96,8,256]{4,3,1,0,2:T(8,128)(2,1)}, u32[]{:S(2)}, u32[]{:S(2)}) async-start(bf16[3,4,96,8,256]{4,3,1,0,2:T(8,128)(2,1)} %select_bitcast_fusion), calls=%async_computation | async-start | bytes 9437184 | tf_op jit(solution)/shard_map/all_to_all | solution.py:104
  48.0 115.2 %copy-start.1 = (s32[32]{0:T(128)}, s32[32]{0:T(128)S(1)}, u32[]{:S(2)}) copy-start(s32[32]{0:T(128)S(1)} %get-tuple-element.6) | copy-start | bytes 388
  147.8 0.7 copy-start.7
where the time goes:
time: 252 us; the launch traced here: 251 us
  waiting for transfers between devices  85.3 us (34%)
  blocking collectives  77.8 us (31%)
  local copies, waits for them, and re-layouts  37.9 us (15%)
  other arithmetic  33.9 us (13%)
  starting transfers between devices  7.56 us (3%)
  matrix products  5.83 us (2%)
    all_to_all x1, waiting for transfers between devices, local(): lax.all_to_all(outgoing, 'tile', split_axis=2, concat_axis=2, tiled=True)  85.3 us
    psum x1, blocking collectives, local(): lax.psum((jnp.dot(belongs.T, first_sum, precision=lax.Precision.HIGHEST),...  77.8 us
    all_to_all x1, starting transfers between devices, local(): lax.all_to_all(outgoing, 'tile', split_axis=2, concat_axis=2, tiled=True)  7.56 us
    convert_element_type x1, local copies, waits for them, and re-layouts, local(): block_out.astype(jnp.float32)  7 us
    gather x1, local copies, waits for them, and re-layouts, local(): jnp.take(pieces, source_tile, axis=2)  5.85 us
    another operation x1, other arithmetic, local(): jnp.stack(lagged, 0).reshape(3, tile_rows + 2, own_tiles, columns, channels)  5.21 us
    select_n x1, other arithmetic, local(): jnp.where(sendable[None, None, :, None, None], jnp.take(pieces, source_ti...  5.14 us
  transfers between devices with their start and end apart: 1, of which 1 were waited for; matrix products, arithmetic and copies ran while one was open for 1% of the time, Pallas kernels for 0%

commit v1 on v0

v1 whole, which is shorter than its diff:
```python
import jax
import jax.numpy as jnp
from jax import lax
from jax.sharding import PartitionSpec as P

GROUPS = 32
MEANF = 4
NRB = 8


eps = 1e-06


def normalize(values, frame_count, scaling, offsets):
    frames = values.shape[0]
    channels = values.shape[-1]
    grouped = values.reshape(frames, -1, GROUPS, channels // GROUPS)
    live_mask = (jnp.arange(frames) < frame_count).astype(jnp.float32)[:, None, None, None]
    members = frame_count.astype(jnp.float32) * grouped.shape[1] * grouped.shape[3]
    group_mean = jnp.sum(grouped * live_mask, axis=(0, 1, 3)) / members
    spread = (
        jnp.sum(grouped * grouped * live_mask, axis=(0, 1, 3)) / members - group_mean * group_mean
    )
    inverse = lax.rsqrt(spread + eps)
    normed = (grouped - group_mean[:, None]) * inverse[:, None] * scaling.reshape(
        GROUPS, -1
    ) + offsets.reshape(GROUPS, -1)
    return jax.nn.silu(normed).reshape(values.shape)


def local(
    latents,
    frame_counts,
    clip_order,
    norm_scale,
    norm_offset,
    conv_weight,
    conv_bias,
    out_scale,
    out_offset,
):
    devices = lax.axis_size("tile")
    device = lax.axis_index("tile")
    frames, frame_rows, columns, channels = latents.shape
    tile_rows = frame_rows // NRB
    classes = devices // NRB
    per_dest = (frames + classes - 1) // classes
    worker_tiles = MEANF * NRB
    positions = jnp.arange(frame_counts.shape[0], dtype=jnp.int32)
    chosen = clip_order[:, None] == positions[None, :]
    ordered = jnp.sum(jnp.where(chosen, frame_counts[None, :], 0), axis=1)
    starts = (jnp.cumsum(ordered) - ordered) * NRB
    own_start = jnp.sum(jnp.where(clip_order == device, starts, 0))
    own_count = jnp.sum(jnp.where(positions == device, frame_counts, 0))

    active = normalize(latents.astype(jnp.float32), own_count, norm_scale, norm_offset).astype(
        jnp.bfloat16
    )
    conv = lax.conv_general_dilated(
        active[None],
        conv_weight,
        window_strides=(1, 1, 1),
        padding=((2, 0), (1, 1), (1, 1)),
        dimension_numbers=("NDHWC", "DHWIO", "NDHWC"),
        preferred_element_type=jnp.float32,
    )[0]
    block_out = (conv + conv_bias).astype(jnp.bfloat16)
    per_group = channels // GROUPS
    grouped = block_out.astype(jnp.float32).reshape(frames, frame_rows * columns, GROUPS, per_group)
    live_mask = (jnp.arange(frames) < own_count).astype(jnp.float32)[:, None, None, None]
    members = own_count.astype(jnp.float32) * (frame_rows * columns * per_group)
    first_sum = jnp.sum(grouped * live_mask, axis=(0, 1, 3))
    second_sum = jnp.sum(grouped * grouped * live_mask, axis=(0, 1, 3))
    clip_mean = first_sum / members
    clip_spread = second_sum / members - clip_mean * clip_mean
    clip_inverse = lax.rsqrt(clip_spread + eps)
    normed = (grouped - clip_mean[:, None]) * clip_inverse[:, None] * out_scale.reshape(
        GROUPS, per_group
    ) + out_offset.reshape(GROUPS, per_group)
    normed = jax.nn.silu(normed).astype(jnp.bfloat16).reshape(block_out.shape)

    both = jnp.stack([block_out, normed], 0).reshape(
        2, frames, NRB, tile_rows, columns, channels
    )
    both = jnp.pad(both, ((0, 0), (0, per_dest * classes - frames), (0, 0), (0, 0), (0, 0), (0, 0)))
    both = both.reshape(2, per_dest, classes, NRB, tile_rows, columns, channels)
    shift = own_start // NRB
    pick = (jnp.arange(classes, dtype=jnp.int32) - shift) % classes
    both = jnp.take(both, pick, axis=2)
    outgoing = jnp.transpose(both, (2, 3, 1, 0, 4, 5, 6)).reshape(
        devices, per_dest, 2, tile_rows, columns, channels
    )
    received = lax.all_to_all(outgoing, "tile", split_axis=0, concat_axis=0, tiled=True)
    received = received.reshape(devices * per_dest, 2, tile_rows, columns, channels)

    local_slot = jnp.arange(worker_tiles, dtype=jnp.int32)
    tile_id = local_slot * devices + device
    placed = jnp.sum((starts[None, :] <= tile_id[:, None]).astype(jnp.int32), axis=1) - 1
    at_place = placed[:, None] == positions[None, :]
    clip_id = jnp.sum(jnp.where(at_place, clip_order[None, :], 0), axis=1)
    within = tile_id - jnp.sum(jnp.where(at_place, starts[None, :], 0), axis=1)
    take_from = clip_id * per_dest + within // NRB // classes
    mine = jnp.take(received, take_from, axis=0)
    mine = jnp.transpose(mine, (1, 2, 0, 3, 4))
    return (mine[0], mine[1])


def solution(mesh):
    in_specs = (
        P(("grp", "tile"), None, None, None),
        P("grp"),
        P("grp"),
        P(),
        P(),
        P(),
        P(),
        P(),
        P(),
    )
    out_specs = (P(None, ("grp", "tile"), None, None), P(None, ("grp", "tile"), None, None))
    return jax.shard_map(local, mesh=mesh, in_specs=in_specs, out_specs=out_specs, check_vma=False)
```

time: 252 us -> 115 us (0.46)
  the two profiles are of different devices: /device:TPU:0 before, /device:TPU:9 now
where the time goes in v1:
time: 115 us; the launch traced here: 113 us
  waiting for transfers between devices  35.3 us (31%)
  matrix products  27.4 us (24%)
  other arithmetic  22.5 us (20%)
  local copies, waits for them, and re-layouts  17.3 us (15%)
  starting transfers between devices  6.74 us (6%)
  between operations  3.95 us (3%)
    all_to_all x1, waiting for transfers between devices, local(): lax.all_to_all(outgoing, 'tile', split_axis=0, concat_axis=0, tiled=True)  35.3 us
    conv_general_dilated x1, matrix products, local(): lax.conv_general_dilated(active[None], conv_weight, window_strides=(1, 1,...  27.4 us
    all_to_all x1, starting transfers between devices, local(): lax.all_to_all(outgoing, 'tile', split_axis=0, concat_axis=0, tiled=True)  6.74 us
    gather x1, local copies, waits for them, and re-layouts, local(): both = jnp.take(both, pick, axis=2)  3.21 us
    reduce_sum x2, other arithmetic, normalize(): jnp.sum(grouped * grouped * live_mask, axis=(0, 1, 3)) / members  3.06 us
    gather x1, local copies, waits for them, and re-layouts, local(): mine = jnp.take(received, take_from, axis=0)  2.8 us
    reduce_sum x2, other arithmetic, local(): second_sum = jnp.sum(grouped * grouped * live_mask, axis=(0, 1, 3))  2.67 us
  transfers between devices with their start and end apart: 1, of which 1 were waited for; matrix products, arithmetic and copies ran while one was open for 0% of the time, Pallas kernels for 0%

profile of v1, /device:TPU:9, one launch (start us, length us, event | category | flops | bytes accessed | tf_op | source)
XLA Modules:
  0.0 113.2 jit_solution(2366486212227796181)
XLA Ops:
  0.6 1.0 select_reduce_fusion.2
  2.4 1.8 %fusion.28 = (s32[]{:T(128)}, s32[16]{0:T(128)}, s32[]{:T(128)}) fusion(s32[16]{0:T(128)} %param.11, s32[]{:T(128)S(6)} %axis_index.12, s32[16]{0:T(128)S(1)} %reduce.8, s32[16]{0:T(128)} %copy-done.4, s32[16]{0:T(128)} %param.10), kind=kLoop, calls=%fused_computation.83 | loop fusion | flops 126 | bytes 332 | tf_op jit(solution)/shard_map/reduce_sum | solution.py:53
  9.1 2.2 %fusion.11 = (f32[256]{0:T(256)}, f32[256]{0:T(256)}) fusion(bf16[12,16,8,256]{3,2,1,0:T(8,128)(2,1)} %param.9, f32[12]{0:T(128)S(1)} %compare_convert_fusion), kind=kLoop, calls=%fused_computation.19 | loop fusion | flops 2358784 | bytes 788528 | tf_op jit(solution)/shard_map/reduce_sum | solution.py:22
  11.3 0.8 reduce_sum.127
  12.1 1.4 %reduce_sum.130 = f32[32,8]{1,0:T(8,128)} reshape(f32[256]{0:T(256)} %get-tuple-element.10) | data formatting | bytes 2048 | tf_op jit(solution)/shard_map/reduce_sum | solution.py:22
  14.1 0.8 reduce_sum.131
  14.9 1.2 %add_rsqrt_fusion.1 = (f32[32]{0:T(128)S(1)}, f32[32]{0:T(128)}) fusion(f32[32]{0:T(128)S(1)} %reduce_sum.131, f32[]{:T(128)S(6)} %mul.166, f32[32]{0:T(128)} %reduce_sum.128), kind=kLoop, calls=%fused_computation.92 | loop fusion | flops 160 | bytes 516 | tf_op jit(solution)/shard_map/rsqrt | solution.py:24
  16.8 0.7 sub.110
  18.2 1.7 %fusion.27 = bf16[1,12,16,8,256]{4,3,2,1,0:T(8,128)(2,1)S(1)} fusion(bf16[12,16,8,256]{3,2,1,0:T(8,128)(2,1)} %param.9, f32[256]{0:T(256)} %param.13, f32[256]{0:T(256)} %param.12, f32[256]{0:T(256)} %mul.171, f32[256]{0:T(256)} %sub.111), kind=kLoop, calls=%fused_computation.38 | loop fusion | flops 3932160 | bytes 1576960 | tf_op jit(solution)/shard_map/broadcast_in_dim | solution.py:60
  19.9 27.4 %fusion.25 = f32[1,12,16,8,256]{4,0,3,2,1:T(1,128)S(1)} fusion(bf16[3,3,3,256,256]{4,3,2,1,0:T(8,128)(2,1)S(1)} %copy-done, bf16[1,12,16,8,256]{4,3,2,1,0:T(8,128)(2,1)S(1)} %fusion.27), kind=kOutput, calls=%fused_computation.36 | convolution fusion | flops 4377280512 | bytes 5898240 | tf_op jit(solution)/shard_map/conv_general_dilated | solution.py:59
  47.4 2.0 %fusion.23 = (f32[256]{0:T(256)}, f32[256]{0:T(256)}, bf16[1,12,16,8,256]{4,3,2,1,0:T(8,128)(2,1)}) fusion(f32[12]{0:T(128)S(1)} %copy-done.6, f32[256]{0:T(256)S(1)} %copy-done.7, f32[1,12,16,8,256]{4,0,3,2,1:T(1,128)S(1)} %fusion.25), kind=kLoop, calls=%fused_computation.31 | loop fusion | flops 3145216 | bytes 2362416 | tf_op jit(solution)/shard_map/reduce_sum | solution.py:73
  49.4 0.8 reduce_sum.133
  50.8 0.8 reduce_sum.136
  52.2 1.2 %add_rsqrt_fusion = (f32[32]{0:T(128)S(1)}, f32[32]{0:T(128)}) fusion(f32[32]{0:T(128)} %reduce_sum.137, f32[]{:T(128)S(6)} %mul.166, f32[32]{0:T(128)} %reduce_sum.134), kind=kLoop, calls=%fused_computation.91 | loop fusion | flops 160 | bytes 516 | tf_op jit(solution)/shard_map/rsqrt | solution.py:76
  55.5 0.7 pad_clamp_fusion.1
  56.3 1.7 %fusion.21 = bf16[1,12,16,8,256]{4,3,2,1,0:T(8,128)(2,1)S(1)} fusion(bf16[1,12,16,8,256]{4,3,2,1,0:T(8,128)(2,1)} %get-tuple-element.18, f32[256]{0:T(256)} %param.17, f32[256]{0:T(256)} %param.16, f32[256]{0:T(256)} %mul.183, f32[256]{0:T(256)} %sub.116), kind=kLoop, calls=%fused_computation.29 | loop fusion | flops 3932160 | bytes 1576960 | tf_op jit(solution)/shard_map/convert_element_type | solution.py:80
  58.0 1.3 %pad_maximum_fusion = bf16[2,6,2,8,2,8,256]{6,5,4,3,2,1,0:T(8,128)(2,1)} fusion(bf16[1,6,2,8,2,8,256]{6,5,4,3,2,1,0:T(8,128)(2,1)S(1)} %bitcast.30, bf16[1,6,2,8,2,8,256]{6,5,4,3,2,1,0:T(8,128)(2,1)S(1)} %bitcast.28), kind=kLoop, calls=%fused_computation.32 | loop fusion | flops 786432 | bytes 3145728 | tf_op jit(solution)/shard_map/stack | solution.py:82
  59.3 3.2 %gather_fusion = bf16[2,2,6,8,2,8,256]{6,5,4,3,2,1,0:T(8,128)(2,1)} fusion(bf16[2,6,2,8,2,8,256]{6,5,4,3,2,1,0:T(8,128)(2,1)} %pad_maximum_fusion, s32[1024]{0:T(1024)S(1)} %pad_clamp_fusion.1), kind=kCustom, calls=%fused_computation | custom fusion | bytes 3145736 | tf_op jit(solution)/shard_map/jit(_take)/gather | solution.py:89
  62.5 1.6 %select_bitcast_fusion = bf16[2,8,6,2,2,8,256]{6,5,4,1,2,3,0:T(8,128)(2,1)S(1)} fusion(bf16[2,2,6,8,2,8,256]{6,5,4,3,2,1,0:T(8,128)(2,1)} %gather_fusion, pred[2]{0:T(512)(128)(4,1)S(1)} %copy-done.8), kind=kLoop, calls=%fused_computation.35 | loop fusion | flops 786432 | bytes 3145730 | tf_op jit(solution)/shard_map/jit(_take)/select_n | solution.py:89
  64.1 1.3 %copy.26 = bf16[2,8,6,2,2,8,256]{6,5,4,3,2,1,0:T(8,128)(2,1)} copy(bf16[2,8,6,2,2,8,256]{6,5,4,1,2,3,0:T(8,128)(2,1)S(1)} %select_bitcast_fusion) | data formatting | bytes 3145728 | tf_op jit(solution)/shard_map/jit(_take)/select_n | solution.py:89
  65.5 6.7 %all-to-all-start = ((bf16[16,6,2,2,8,256]{5,4,3,2,1,0:T(8,128)(2,1)}), bf16[16,6,2,2,8,256]{5,4,3,2,1,0:T(8,128)(2,1)}, u32[]{:S(2)}, u32[]{:S(2)}) async-start(bf16[16,6,2,2,8,256]{5,4,3,2,1,0:T(8,128)(2,1)} %bitcast.29), calls=%async_computation | async-start | bytes 3145728 | tf_op jit(solution)/shard_map/all_to_all | solution.py:93
  72.5 35.3 %all-to-all-done = bf16[16,6,2,2,8,256]{5,4,3,2,1,0:T(8,128)(2,1)} async-done(((bf16[16,6,2,2,8,256]{5,4,3,2,1,0:T(8,128)(2,1)}), bf16[16,6,2,2,8,256]{5,4,3,2,1,0:T(8,128)(2,1)}, u32[]{:S(2)}, u32[]{:S(2)}) %all-to-all-start) | async-done | bytes 1572896 | tf_op jit(solution)/shard_map/all_to_all | solution.py:93
  107.8 2.8 %gather_fusion.1 = bf16[32,2,2,8,256]{4,3,2,1,0:T(8,128)(2,1)} fusion(bf16[96,2,2,8,256]{4,3,2,1,0:T(8,128)(2,1)} %bitcast.7, s32[1024]{0:T(1024)S(1)} %pad_clamp_fusion), kind=kCustom, calls=%fused_computation.1 | custom fusion | bytes 1048704 | tf_op jit(solution)/shard_map/jit(_take)/gather | solution.py:103
  110.6 1.2 %select_bitcast_fusion.1 = bf16[2,2,32,8,256]{4,3,1,0,2:T(8,128)(2,1)S(1)} fusion(bf16[32,2,2,8,256]{4,3,2,1,0:T(8,128)(2,1)} %gather_fusion.1, pred[32]{0:T(512)(128)(4,1)S(1)} %compare_and_fusion.1), kind=kLoop, calls=%fused_computation.39 | loop fusion | flops 262144 | bytes 1048608 | tf_op jit(solution)/shard_map/jit(_take)/select_n | solution.py:103
  (44 shorter events, 9.6 us)
Async XLA Ops:
  0.6 19.3 %copy-start = (bf16[3,3,3,256,256]{4,3,2,1,0:T(8,128)(2,1)S(1)}, bf16[3,3,3,256,256]{4,3,2,1,0:T(8,128)(2,1)}, u32[]{:S(2)}) copy-start(bf16[3,3,3,256,256]{4,3,2,1,0:T(8,128)(2,1)} %param.14) | copy-start | bytes 10616836
  1.7 0.5 copy-start.4
  4.8 6.5 %copy-start.5 = (f32[12]{0:T(128)}, f32[12]{0:T(128)S(1)}, u32[]{:S(2)}) copy-start(f32[12]{0:T(128)S(1)} %compare_convert_fusion) | copy-start | bytes 148
  19.9 27.5 %copy-start.6 = (f32[12]{0:T(128)S(1)}, f32[12]{0:T(128)}, u32[]{:S(2)}) copy-start(f32[12]{0:T(128)} %copy-done.5) | copy-start | bytes 148
  19.9 27.5 %copy-start.7 = (f32[256]{0:T(256)S(1)}, f32[256]{0:T(256)}, u32[]{:S(2)}) copy-start(f32[256]{0:T(256)} %param.15) | copy-start | bytes 3076
  55.5 2.5 %copy-start.1 = (bf16[1,12,16,8,256]{4,3,2,1,0:T(8,128)(2,1)S(1)}, bf16[1,12,16,8,256]{4,3,2,1,0:T(8,128)(2,1)}, u32[]{:S(2)}) copy-start(bf16[1,12,16,8,256]{4,3,2,1,0:T(8,128)(2,1)} %get-tuple-element.18) | copy-start | bytes 2359300
  59.3 3.2 %copy-start.8 = (pred[2]{0:T(512)(128)(4,1)S(1)}, pred[2]{0:T(512)(128)(4,1)}, u32[]{:S(2)}) copy-start(pred[2]{0:T(512)(128)(4,1)} %compare_and_fusion) | copy-start | bytes 10
  65.5 6.8 %copy-start.3 = (s32[16]{0:T(128)S(1)}, s32[16]{0:T(128)}, u32[]{:S(2)}) copy-start(s32[16]{0:T(128)} %get-tuple-element.15) | copy-start | bytes 196
  65.5 6.9 %copy-start.2 = (s32[16]{0:T(128)S(1)}, s32[16]{0:T(128)}, u32[]{:S(2)}) copy-start(s32[16]{0:T(128)} %param.11) | copy-start | bytes 196
  65.5 42.3 %all-to-all-start = ((bf16[16,6,2,2,8,256]{5,4,3,2,1,0:T(8,128)(2,1)}), bf16[16,6,2,2,8,256]{5,4,3,2,1,0:T(8,128)(2,1)}, u32[]{:S(2)}, u32[]{:S(2)}) async-start(bf16[16,6,2,2,8,256]{5,4,3,2,1,0:T(8,128)(2,1)} %bitcast.29), calls=%async_computation | async-start | bytes 3145728 | tf_op jit(solution)/shard_map/all_to_all | solution.py:93

commit v2 on v1

--- a/solution.py
+++ b/solution.py
@@ -56,15 +56,25 @@
     active = normalize(latents.astype(jnp.float32), own_count, norm_scale, norm_offset).astype(
         jnp.bfloat16
     )
-    conv = lax.conv_general_dilated(
-        active[None],
-        conv_weight,
-        window_strides=(1, 1, 1),
-        padding=((2, 0), (1, 1), (1, 1)),
-        dimension_numbers=("NDHWC", "DHWIO", "NDHWC"),
-        preferred_element_type=jnp.float32,
-    )[0]
-    block_out = (conv + conv_bias).astype(jnp.bfloat16)
+    padded = jnp.pad(active, ((2, 0), (1, 1), (1, 1), (0, 0)))
+    unfolded = jnp.concatenate(
+        [
+            padded[:, row_tap : row_tap + frame_rows, col_tap : col_tap + columns]
+            for row_tap in range(3)
+            for col_tap in range(3)
+        ],
+        axis=-1,
+    ).reshape(frames + 2, frame_rows * columns, 9 * channels)
+    kernel = conv_weight.reshape(3, 9 * channels, -1)
+    conv = conv_bias + sum(
+        jnp.dot(
+            unfolded[frame_lag : frame_lag + frames].reshape(-1, 9 * channels),
+            kernel[frame_lag],
+            preferred_element_type=jnp.float32,
+        )
+        for frame_lag in range(3)
+    ).reshape(frames, frame_rows, columns, -1)
+    block_out = conv.astype(jnp.bfloat16)
     per_group = channels // GROUPS
     grouped = block_out.astype(jnp.float32).reshape(frames, frame_rows * columns, GROUPS, per_group)
     live_mask = (jnp.arange(frames) < own_count).astype(jnp.float32)[:, None, None, None]

time: 115 us -> 72.1 us (0.63)
  matrix products: 27.4 us -> 6.58 us
  other arithmetic: 22.5 us -> 7.82 us
  local copies, waits for them, and re-layouts: 17.3 us -> 10.5 us
    conv_general_dilated x1 -> x0, matrix products: 27.4 us -> none  [local(): lax.conv_general_dilated(active[None], conv_weight, window_strides=(1, 1,...]
    dot_general x0 -> x3, matrix products: none -> 6.58 us  [local(): jnp.dot(unfolded[frame_lag:frame_lag + frames].reshape(-1, 9 * channels),...]
    slice x0 -> x2, local copies, waits for them, and re-layouts: none -> 3.95 us  [the longest x1 2.21 us: local(): kernel[frame_lag]]
    gather x1, local copies, waits for them, and re-layouts: 3.21 us -> 0.65 us  [local(): both = jnp.take(both, pick, axis=2)]
    reduce_sum x2 -> x1, other arithmetic: 2.67 us -> 0.13 us  [local(): second_sum = jnp.sum(grouped * grouped * live_mask, axis=(0, 1, 3))]
    gather x1, local copies, waits for them, and re-layouts: 2.8 us -> 0.58 us  [local(): mine = jnp.take(received, take_from, axis=0)]
    select_n x2, other arithmetic: 2.21 us -> 0.23 us  [local(): both = jnp.take(both, pick, axis=2)]
    broadcast_in_dim x1 -> x0, other arithmetic: 1.71 us -> none  [local(): active[None]]
where the time goes in v2:
time: 72.1 us; the launch traced here: 71 us
  waiting for transfers between devices  35.2 us (49%)
  local copies, waits for them, and re-layouts  10.5 us (15%)
  other arithmetic  7.82 us (11%)
  starting transfers between devices  6.74 us (9%)
  matrix products  6.58 us (9%)
  between operations  4.19 us (6%)
    all_to_all x1, waiting for transfers between devices, local(): lax.all_to_all(outgoing, 'tile', split_axis=0, concat_axis=0, tiled=True)  35.2 us
    all_to_all x1, starting transfers between devices, local(): lax.all_to_all(outgoing, 'tile', split_axis=0, concat_axis=0, tiled=True)  6.74 us
    dot_general x3, matrix products, local(): jnp.dot(unfolded[frame_lag:frame_lag + frames].reshape(-1, 9 * channels),...  6.58 us
    unnamed x20, local copies, waits for them, and re-layouts  2.64 us
    slice x1, local copies, waits for them, and re-layouts, local(): kernel[frame_lag]  2.21 us
    reduce_sum x2, other arithmetic, normalize(): jnp.sum(grouped * grouped * live_mask, axis=(0, 1, 3)) / members  1.78 us
    slice x1, local copies, waits for them, and re-layouts, local(): unfolded[frame_lag:frame_lag + frames].reshape(-1, 9 * channels)  1.74 us
  transfers between devices with their start and end apart: 1, of which 1 were waited for; matrix products, arithmetic and copies ran while one was open for 0% of the time, Pallas kernels for 0%

profile of v2, /device:TPU:9, one launch (start us, length us, event | category | flops | bytes accessed | tf_op | source)
XLA Modules:
  0.0 71.0 jit_solution(11246227192255172405)
XLA Ops:
  0.6 0.9 %select_reduce_fusion.2 = s32[16]{0:T(128)S(1)} fusion(s32[16]{0:T(128)} %param.10, s32[16]{0:T(128)} %param.11), kind=kLoop, calls=%fused_computation.54 | loop fusion | flops 752 | bytes 192 | tf_op jit(solution)/shard_map/reduce_sum | solution.py:51
  1.8 1.3 %fusion.24 = (s32[]{:T(128)}, s32[16]{0:T(128)S(1)}, s32[]{:T(128)}) fusion(s32[16]{0:T(128)} %param.11, s32[]{:T(128)S(6)} %axis_index.12, s32[16]{0:T(128)S(1)} %reduce.8, s32[16]{0:T(128)S(1)} %select_reduce_fusion.2, s32[16]{0:T(128)} %param.10), kind=kLoop, calls=%fused_computation.92 | loop fusion | flops 126 | bytes 332 | tf_op jit(solution)/shard_map/reduce_sum | solution.py:53
  3.1 0.6 compare_convert_fusion
  7.1 1.7 %fusion.14 = (f32[256]{0:T(256)S(1)}, f32[256]{0:T(256)S(1)}) fusion(bf16[12,16,8,256]{3,2,1,0:T(8,128)(2,1)} %param.9, f32[12]{0:T(128)S(1)} %compare_convert_fusion), kind=kLoop, calls=%fused_computation.32 | loop fusion | flops 2358784 | bytes 788528 | tf_op jit(solution)/shard_map/reduce_sum | solution.py:22
  9.6 1.2 %fusion.12 = bf16[12,16,8,256]{3,2,1,0:T(8,128)(2,1)S(1)} fusion(bf16[12,16,8,256]{3,2,1,0:T(8,128)(2,1)S(1)} %copy-done, f32[256]{0:T(256)} %param.13, f32[256]{0:T(256)} %param.12, f32[256]{0:T(256)S(1)} %mul.196, f32[256]{0:T(256)S(1)} %sub.118), kind=kLoop, calls=%fused_computation.30 | loop fusion | flops 3932160 | bytes 1576960 | tf_op jit(solution)/shard_map/convert_element_type | solution.py:56
  10.8 0.2 fusion.15
  11.1 0.2 fusion.17
  11.3 0.2 fusion.18
  11.6 0.2 fusion.20
  11.8 0.2 fusion.21
  12.3 1.7 %fusion.30 = (bf16[12,16,8,2304]{3,2,1,0:T(8,128)(2,1)S(1)}, bf16[12,16,8,2304]{3,2,1,0:T(8,128)(2,1)S(1)}, bf16[12,16,8,2304]{3,2,1,0:T(8,128)(2,1)S(1)}) fusion(bf16[14,16,8,2304]{3,2,1,0:T(8,128)(2,1)S(1)} %fusion.23), kind=kLoop, calls=%fused_computation.107 | loop fusion | bytes 42467328 | tf_op jit(solution)/shard_map/slice | solution.py:71
  14.0 2.2 %fusion.31 = (bf16[1,3,3,256,256]{4,3,2,1,0:T(8,128)(2,1)S(1)}, bf16[1,3,3,256,256]{4,3,2,1,0:T(8,128)(2,1)S(1)}, bf16[1,3,3,256,256]{4,3,2,1,0:T(8,128)(2,1)S(1)}) fusion(bf16[3,3,3,256,256]{4,3,2,1,0:T(8,128)(2,1)} %param.14), kind=kLoop, calls=%fused_computation.108 | loop fusion | bytes 7077888 | tf_op jit(solution)/shard_map/slice | solution.py:72
  16.2 2.1 %fusion.32 = f32[1536,256]{1,0:T(8,128)S(1)} fusion(bf16[1536,2304]{1,0:T(8,128)(2,1)S(1)} %bitcast.40, bf16[2304,256]{1,0:T(8,128)(2,1)S(1)} %bitcast.45), kind=kOutput, calls=%fused_computation.109 | convolution fusion | flops 1811939328 | bytes 9830400 | tf_op jit(solution)/shard_map/dot_general | solution.py:70
  18.3 2.2 %convolution_add_fusion.1 = f32[1536,256]{1,0:T(8,128)S(1)} fusion(f32[1536,256]{1,0:T(8,128)S(1)} %fusion.32, bf16[1536,2304]{1,0:T(8,128)(2,1)S(1)} %bitcast.39, bf16[2304,256]{1,0:T(8,128)(2,1)S(1)} %bitcast.44), kind=kOutput, calls=%fused_computation.12 | convolution fusion | flops 1812332544 | bytes 11403264 | tf_op jit(solution)/shard_map/dot_general | solution.py:70
  20.6 2.3 %fusion.2 = (f32[256]{0:T(256)S(1)}, f32[256]{0:T(256)S(1)}, f32[1536,256]{1,0:T(8,128)S(1)}) fusion(f32[1536]{0:T(1024)S(1)} %broadcast_bitcast_fusion, f32[256]{0:T(256)S(1)} %copy-done.4, f32[1536,256]{1,0:T(8,128)S(1)} %convolution_add_fusion.1, bf16[1536,2304]{1,0:T(8,128)(2,1)S(1)} %bitcast.38, bf16[2304,256]{1,0:T(8,128)(2,1)S(1)} %bitcast.43), kind=kOutput, calls=%fused_computation.20 | convolution fusion | flops 1815477760 | bytes 11412480 | tf_op jit(solution)/shard_map/dot_general | solution.py:70
  23.7 0.6 multiply_convert_fusion
  24.4 0.6 gather_fusion
  25.1 0.2 select_bitcast_fusion
  25.3 1.4 %copy.20 = bf16[2,8,6,2,2,8,256]{6,5,4,3,2,1,0:T(8,128)(2,1)} copy(bf16[2,8,6,2,2,8,256]{6,5,4,1,2,3,0:T(8,128)(2,1)S(1)} %select_bitcast_fusion) | data formatting | bytes 3145728 | tf_op jit(solution)/shard_map/jit(_take)/select_n | solution.py:99
  26.7 6.7 %all-to-all-start = ((bf16[16,6,2,2,8,256]{5,4,3,2,1,0:T(8,128)(2,1)}), bf16[16,6,2,2,8,256]{5,4,3,2,1,0:T(8,128)(2,1)S(1)}, u32[]{:S(2)}, u32[]{:S(2)}) async-start(bf16[16,6,2,2,8,256]{5,4,3,2,1,0:T(8,128)(2,1)} %bitcast.11), calls=%async_computation | async-start | bytes 3145728 | tf_op jit(solution)/shard_map/all_to_all | solution.py:103
  33.7 35.2 %all-to-all-done = bf16[16,6,2,2,8,256]{5,4,3,2,1,0:T(8,128)(2,1)S(1)} async-done(((bf16[16,6,2,2,8,256]{5,4,3,2,1,0:T(8,128)(2,1)}), bf16[16,6,2,2,8,256]{5,4,3,2,1,0:T(8,128)(2,1)S(1)}, u32[]{:S(2)}, u32[]{:S(2)}) %all-to-all-start) | async-done | bytes 1572896 | tf_op jit(solution)/shard_map/all_to_all | solution.py:103
  68.8 0.6 gather_fusion.1
  69.6 0.7 %copy.21 = bf16[2,32,8,256]{3,2,1,0:T(8,128)(2,1)} copy(bf16[2,32,8,256]{3,2,0,1:T(8,128)(2,1)S(1)} %get-tuple-element.29) | data formatting | bytes 524288
  70.3 0.7 %copy.22 = bf16[2,32,8,256]{3,2,1,0:T(8,128)(2,1)} copy(bf16[2,32,8,256]{3,2,0,1:T(8,128)(2,1)S(1)} %get-tuple-element.28) | data formatting | bytes 524288
  (49 shorter events, 2.8 us)
Async XLA Ops:
  0.6 9.0 %copy-start = (bf16[12,16,8,256]{3,2,1,0:T(8,128)(2,1)S(1)}, bf16[12,16,8,256]{3,2,1,0:T(8,128)(2,1)}, u32[]{:S(2)}) copy-start(bf16[12,16,8,256]{3,2,1,0:T(8,128)(2,1)} %param.9) | copy-start | bytes 2359300
  18.3 2.2 %copy-start.4 = (f32[256]{0:T(256)S(1)}, f32[256]{0:T(256)}, u32[]{:S(2)}) copy-start(f32[256]{0:T(256)} %param.15) | copy-start | bytes 3076
  20.5 3.1 %copy-start.2 = (f32[256]{0:T(256)S(1)}, f32[256]{0:T(256)}, u32[]{:S(2)}) copy-start(f32[256]{0:T(256)} %param.17) | copy-start | bytes 3076
  20.5 3.1 %copy-start.3 = (f32[256]{0:T(256)S(1)}, f32[256]{0:T(256)}, u32[]{:S(2)}) copy-start(f32[256]{0:T(256)} %param.16) | copy-start | bytes 3076
  26.6 6.8 %copy-start.1 = (s32[16]{0:T(128)S(1)}, s32[16]{0:T(128)}, u32[]{:S(2)}) copy-start(s32[16]{0:T(128)} %param.11) | copy-start | bytes 196
  26.7 42.2 %all-to-all-start = ((bf16[16,6,2,2,8,256]{5,4,3,2,1,0:T(8,128)(2,1)}), bf16[16,6,2,2,8,256]{5,4,3,2,1,0:T(8,128)(2,1)S(1)}, u32[]{:S(2)}, u32[]{:S(2)}) async-start(bf16[16,6,2,2,8,256]{5,4,3,2,1,0:T(8,128)(2,1)} %bitcast.11), calls=%async_computation | async-start | bytes 3145728 | tf_op jit(solution)/shard_map/all_to_all | solution.py:103

commit v3 on v2

--- a/solution.py
+++ b/solution.py
@@ -84,24 +84,30 @@
     clip_mean = first_sum / members
     clip_spread = second_sum / members - clip_mean * clip_mean
     clip_inverse = lax.rsqrt(clip_spread + eps)
-    normed = (grouped - clip_mean[:, None]) * clip_inverse[:, None] * out_scale.reshape(
-        GROUPS, per_group
-    ) + out_offset.reshape(GROUPS, per_group)
-    normed = jax.nn.silu(normed).astype(jnp.bfloat16).reshape(block_out.shape)
 
-    both = jnp.stack([block_out, normed], 0).reshape(
-        2, frames, NRB, tile_rows, columns, channels
-    )
-    both = jnp.pad(both, ((0, 0), (0, per_dest * classes - frames), (0, 0), (0, 0), (0, 0), (0, 0)))
-    both = both.reshape(2, per_dest, classes, NRB, tile_rows, columns, channels)
+    tiles = block_out.reshape(frames, NRB, tile_rows, columns, channels)
+    tiles = jnp.pad(tiles, ((0, per_dest * classes - frames), (0, 0), (0, 0), (0, 0), (0, 0)))
+    tiles = tiles.reshape(per_dest, classes, NRB, tile_rows, columns, channels)
     shift = own_start // NRB
     pick = (jnp.arange(classes, dtype=jnp.int32) - shift) % classes
-    both = jnp.take(both, pick, axis=2)
-    outgoing = jnp.transpose(both, (2, 3, 1, 0, 4, 5, 6)).reshape(
-        devices, per_dest, 2, tile_rows, columns, channels
+    tiles = jnp.take(tiles, pick, axis=1)
+    tiles = jnp.transpose(tiles, (1, 2, 0, 3, 4, 5)).reshape(
+        devices, per_dest * tile_rows * columns, channels
     )
+    stats = jnp.stack([clip_mean, clip_inverse], 0)
+    stats = jnp.repeat(stats, per_group, axis=1)
+    high = lax.reduce_precision(stats, exponent_bits=8, mantissa_bits=7)
+    low = stats - high
+    stat_rows = jnp.concatenate([high, low, jnp.zeros((4, channels), jnp.float32)], 0)
+    stat_rows = jnp.broadcast_to(stat_rows.astype(jnp.bfloat16)[None], (devices, 8, channels))
+    outgoing = jnp.concatenate([tiles, stat_rows], 1)
     received = lax.all_to_all(outgoing, "tile", split_axis=0, concat_axis=0, tiled=True)
-    received = received.reshape(devices * per_dest, 2, tile_rows, columns, channels)
+    block_part = received[:, : per_dest * tile_rows * columns].reshape(
+        devices * per_dest, tile_rows, columns, channels
+    )
+    stat_part = received[:, per_dest * tile_rows * columns :].astype(jnp.float32)
+    src_mean = stat_part[:, 0] + stat_part[:, 2]
+    src_inverse = stat_part[:, 1] + stat_part[:, 3]
 
     local_slot = jnp.arange(worker_tiles, dtype=jnp.int32)
     tile_id = local_slot * devices + device
@@ -110,9 +116,14 @@
     clip_id = jnp.sum(jnp.where(at_place, clip_order[None, :], 0), axis=1)
     within = tile_id - jnp.sum(jnp.where(at_place, starts[None, :], 0), axis=1)
     take_from = clip_id * per_dest + within // NRB // classes
-    mine = jnp.take(received, take_from, axis=0)
-    mine = jnp.transpose(mine, (1, 2, 0, 3, 4))
-    return (mine[0], mine[1])
+    mine = jnp.take(block_part, take_from, axis=0)
+    tile_mean = jnp.take(src_mean, clip_id, axis=0)
+    tile_inverse = jnp.take(src_inverse, clip_id, axis=0)
+    normed = (mine.astype(jnp.float32) - tile_mean[:, None, None, :]) * tile_inverse[
+        :, None, None, :
+    ] * out_scale + out_offset
+    normed = jax.nn.silu(normed).astype(jnp.bfloat16)
+    return (jnp.transpose(mine, (1, 0, 2, 3)), jnp.transpose(normed, (1, 0, 2, 3)))
 
 
 def solution(mesh):

time: 72.1 us -> 57.7 us (0.80)
  waiting for transfers between devices: 35.2 us -> 20.6 us
  other arithmetic: 7.82 us -> 8.96 us
    all_to_all x1, waiting for transfers between devices: 35.2 us -> 20.6 us  [local(): lax.all_to_all(outgoing, 'tile', split_axis=0, concat_axis=0, tiled=True)]
    select_n x1, local copies, waits for them, and re-layouts: 1.35 us -> 0.07 us  [local(): tiles = jnp.take(tiles, pick, axis=1)]
    gather x2 -> x4, local copies, waits for them, and re-layouts: 1.23 us -> 2.37 us  [the longest x1 0.6 us: local(): tile_inverse = jnp.take(src_inverse, clip_id, axis=0)]
    concatenate x0 -> x2, other arithmetic: none -> 1.04 us  [the longest x1 0.96 us: local(): outgoing = jnp.concatenate([tiles, stat_rows], 1)]
    unnamed x20 -> x18, local copies, waits for them, and re-layouts: 2.64 us -> 2.63 us
where the time goes in v3:
time: 57.7 us; the launch traced here: 57.3 us
  waiting for transfers between devices  20.6 us (36%)
  local copies, waits for them, and re-layouts  10.4 us (18%)
  other arithmetic  8.96 us (16%)
  starting transfers between devices  6.61 us (11%)
  matrix products  6.58 us (11%)
  between operations  4.23 us (7%)
    all_to_all x1, waiting for transfers between devices, local(): lax.all_to_all(outgoing, 'tile', split_axis=0, concat_axis=0, tiled=True)  20.6 us
    all_to_all x1, starting transfers between devices, local(): lax.all_to_all(outgoing, 'tile', split_axis=0, concat_axis=0, tiled=True)  6.61 us
    dot_general x3, matrix products, local(): jnp.dot(unfolded[frame_lag:frame_lag + frames].reshape(-1, 9 * channels),...  6.58 us
    unnamed x18, local copies, waits for them, and re-layouts  2.63 us
    slice x1, local copies, waits for them, and re-layouts, local(): kernel[frame_lag]  2.21 us
    reduce_sum x2, other arithmetic, normalize(): jnp.sum(grouped * grouped * live_mask, axis=(0, 1, 3)) / members  1.78 us
    slice x1, local copies, waits for them, and re-layouts, local(): unfolded[frame_lag:frame_lag + frames].reshape(-1, 9 * channels)  1.74 us
    convert_element_type x1, other arithmetic, local(): normalize(latents.astype(jnp.float32), own_count, norm_scale, norm_offset)  1.7 us
  transfers between devices with their start and end apart: 1, of which 1 were waited for; matrix products, arithmetic and copies ran while one was open for 0% of the time, Pallas kernels for 0%

profile of v3, /device:TPU:9, one launch (start us, length us, event | category | flops | bytes accessed | tf_op | source)
XLA Modules:
  0.0 57.3 jit_solution(15463350380763943200)
XLA Ops:
  0.6 0.9 %select_reduce_fusion.2 = s32[16]{0:T(128)S(1)} fusion(s32[16]{0:T(128)} %param.12, s32[16]{0:T(128)} %param.13), kind=kLoop, calls=%fused_computation.61 | loop fusion | flops 752 | bytes 192 | tf_op jit(solution)/shard_map/reduce_sum | solution.py:51
  1.7 1.3 %fusion.27 = (s32[]{:T(128)}, s32[16]{0:T(128)S(1)}, s32[]{:T(128)}) fusion(s32[16]{0:T(128)} %param.13, s32[]{:T(128)S(6)} %axis_index.12, s32[16]{0:T(128)S(1)} %reduce.8, s32[16]{0:T(128)S(1)} %select_reduce_fusion.2, s32[16]{0:T(128)} %param.12), kind=kLoop, calls=%fused_computation.106 | loop fusion | flops 126 | bytes 332 | tf_op jit(solution)/shard_map/reduce_sum | solution.py:53
  3.1 0.6 %compare_convert_fusion = f32[12]{0:T(128)S(1)} fusion(s32[]{:T(128)} %get-tuple-element.36), kind=kLoop, calls=%fused_computation.84 | loop fusion | flops 24 | bytes 52 | tf_op jit(solution)/shard_map/convert_element_type | solution.py:18
  7.1 1.7 %fusion.14 = (f32[256]{0:T(256)S(1)}, f32[256]{0:T(256)S(1)}) fusion(bf16[12,16,8,256]{3,2,1,0:T(8,128)(2,1)} %param.11, f32[12]{0:T(128)S(1)} %compare_convert_fusion), kind=kLoop, calls=%fused_computation.34 | loop fusion | flops 2358784 | bytes 788528 | tf_op jit(solution)/shard_map/reduce_sum | solution.py:22
  9.5 1.7 %fusion.12 = bf16[12,16,8,256]{3,2,1,0:T(8,128)(2,1)S(1)} fusion(bf16[12,16,8,256]{3,2,1,0:T(8,128)(2,1)} %param.11, f32[256]{0:T(256)} %param.15, f32[256]{0:T(256)} %param.14, f32[256]{0:T(256)S(1)} %mul.175, f32[256]{0:T(256)S(1)} %sub.115), kind=kLoop, calls=%fused_computation.32 | loop fusion | flops 3932160 | bytes 1576960 | tf_op jit(solution)/shard_map/convert_element_type | solution.py:56
  11.2 0.2 fusion.15
  11.7 0.2 fusion.18
  12.0 0.2 fusion.20
  12.6 1.7 %fusion.35 = (bf16[12,16,8,2304]{3,2,1,0:T(8,128)(2,1)S(1)}, bf16[12,16,8,2304]{3,2,1,0:T(8,128)(2,1)S(1)}, bf16[12,16,8,2304]{3,2,1,0:T(8,128)(2,1)S(1)}) fusion(bf16[14,16,8,2304]{3,2,1,0:T(8,128)(2,1)S(1)} %fusion.23), kind=kLoop, calls=%fused_computation.123 | loop fusion | bytes 42467328 | tf_op jit(solution)/shard_map/slice | solution.py:71
  14.4 2.2 %fusion.36 = (bf16[1,3,3,256,256]{4,3,2,1,0:T(8,128)(2,1)S(1)}, bf16[1,3,3,256,256]{4,3,2,1,0:T(8,128)(2,1)S(1)}, bf16[1,3,3,256,256]{4,3,2,1,0:T(8,128)(2,1)S(1)}) fusion(bf16[3,3,3,256,256]{4,3,2,1,0:T(8,128)(2,1)} %param.16), kind=kLoop, calls=%fused_computation.124 | loop fusion | bytes 7077888 | tf_op jit(solution)/shard_map/slice | solution.py:72
  16.6 2.1 %fusion.37 = f32[1536,256]{1,0:T(8,128)S(1)} fusion(bf16[1536,2304]{1,0:T(8,128)(2,1)S(1)} %bitcast.51, bf16[2304,256]{1,0:T(8,128)(2,1)S(1)} %bitcast.57), kind=kOutput, calls=%fused_computation.125 | convolution fusion | flops 1811939328 | bytes 9830400 | tf_op jit(solution)/shard_map/dot_general | solution.py:70
  18.7 2.2 %convolution_add_fusion.1 = f32[1536,256]{1,0:T(8,128)S(1)} fusion(f32[1536,256]{1,0:T(8,128)S(1)} %fusion.37, bf16[1536,2304]{1,0:T(8,128)(2,1)S(1)} %bitcast.50, bf16[2304,256]{1,0:T(8,128)(2,1)S(1)} %bitcast.56), kind=kOutput, calls=%fused_computation.14 | convolution fusion | flops 1812332544 | bytes 11403264 | tf_op jit(solution)/shard_map/dot_general | solution.py:70
  20.9 2.3 %fusion = (f32[256]{0:T(256)S(1)}, f32[256]{0:T(256)S(1)}, f32[1536,256]{1,0:T(8,128)S(1)}) fusion(f32[1536]{0:T(1024)S(1)} %broadcast_bitcast_fusion, f32[256]{0:T(256)S(1)} %copy-done.1, f32[1536,256]{1,0:T(8,128)S(1)} %convolution_add_fusion.1, bf16[1536,2304]{1,0:T(8,128)(2,1)S(1)} %bitcast.49, bf16[2304,256]{1,0:T(8,128)(2,1)S(1)} %bitcast.55), kind=kOutput, calls=%fused_computation.20 | convolution fusion | flops 1815477760 | bytes 11412480 | tf_op jit(solution)/shard_map/dot_general | solution.py:70
  23.2 0.2 add_convert_fusion.1
  23.5 0.6 %gather_fusion = bf16[2,6,8,2,8,256]{5,4,3,2,1,0:T(8,128)(2,1)S(1)} fusion(bf16[6,2,8,2,8,256]{5,4,3,2,1,0:T(8,128)(2,1)S(1)} %add_convert_fusion.1, s32[1024]{0:T(1024)S(1)} %pad_clamp_fusion.2), kind=kCustom, calls=%fused_computation.2 | custom fusion | bytes 1572872 | tf_op jit(solution)/shard_map/jit(_take)/gather | solution.py:93
  25.1 1.0 %pad_maximum_fusion = bf16[16,104,256]{2,1,0:T(8,128)(2,1)} fusion(bf16[16,8,256]{2,1,0:T(8,128)(2,1)S(1)} %broadcast_in_dim.100, bf16[16,96,256]{2,1,0:T(8,128)(2,1)S(1)} %bitcast.52), kind=kLoop, calls=%fused_computation.46 | loop fusion | flops 1703936 | bytes 1703936 | tf_op jit(solution)/shard_map/concatenate | solution.py:103
  26.1 6.6 %all-to-all-start = ((bf16[16,104,256]{2,1,0:T(8,128)(2,1)}), bf16[16,104,256]{2,1,0:T(8,128)(2,1)S(1)}, u32[]{:S(2)}, u32[]{:S(2)}) async-start(bf16[16,104,256]{2,1,0:T(8,128)(2,1)} %pad_maximum_fusion), calls=%async_computation | async-start | bytes 1703936 | tf_op jit(solution)/shard_map/all_to_all | solution.py:104
  33.0 20.6 %all-to-all-done = bf16[16,104,256]{2,1,0:T(8,128)(2,1)S(1)} async-done(((bf16[16,104,256]{2,1,0:T(8,128)(2,1)}), bf16[16,104,256]{2,1,0:T(8,128)(2,1)S(1)}, u32[]{:S(2)}, u32[]{:S(2)}) %all-to-all-start) | async-done | bytes 852000 | tf_op jit(solution)/shard_map/all_to_all | solution.py:104
  53.6 0.6 %gather_fusion.3 = f32[32,256]{1,0:T(8,128)S(1)} fusion(f32[16,256]{1,0:T(8,128)S(1)} %get-tuple-element.28, s32[1024]{0:T(1024)S(1)} %pad_clamp_fusion), kind=kCustom, calls=%fused_computation.1.clone | custom fusion | bytes 65664 | tf_op jit(solution)/shard_map/jit(_take)/gather | solution.py:121
  54.2 0.6 %gather_fusion.2 = f32[32,256]{1,0:T(8,128)S(1)} fusion(f32[16,256]{1,0:T(8,128)S(1)} %get-tuple-element.27, s32[1024]{0:T(1024)S(1)} %pad_clamp_fusion), kind=kCustom, calls=%fused_computation.clone | custom fusion | bytes 65664 | tf_op jit(solution)/shard_map/jit(_take)/gather | solution.py:120
  54.9 0.6 gather_fusion.1
  55.6 0.3 multiply_convert_fusion
  55.9 0.7 %copy.26 = bf16[2,32,8,256]{3,2,1,0:T(8,128)(2,1)} copy(bf16[2,32,8,256]{3,2,0,1:T(8,128)(2,1)S(1)} %get-tuple-element.16) | data formatting | bytes 524288
  56.6 0.7 %copy.27 = bf16[2,32,8,256]{3,2,1,0:T(8,128)(2,1)} copy(bf16[2,32,8,256]{3,2,0,1:T(8,128)(2,1)S(1)} %get-tuple-element.15) | data formatting | bytes 524288
  (60 shorter events, 3.3 us)
Async XLA Ops:
  18.7 2.2 %copy-start.1 = (f32[256]{0:T(256)S(1)}, f32[256]{0:T(256)}, u32[]{:S(2)}) copy-start(f32[256]{0:T(256)} %param.17) | copy-start | bytes 3076
  25.1 7.7 %copy-start = (s32[16]{0:T(128)S(1)}, s32[16]{0:T(128)}, u32[]{:S(2)}) copy-start(s32[16]{0:T(128)} %param.13) | copy-start | bytes 196
  26.1 27.5 %all-to-all-start = ((bf16[16,104,256]{2,1,0:T(8,128)(2,1)}), bf16[16,104,256]{2,1,0:T(8,128)(2,1)S(1)}, u32[]{:S(2)}, u32[]{:S(2)}) async-start(bf16[16,104,256]{2,1,0:T(8,128)(2,1)} %pad_maximum_fusion), calls=%async_computation | async-start | bytes 1703936 | tf_op jit(solution)/shard_map/all_to_all | solution.py:104
  32.7 22.9 %copy-start.2 = (f32[256]{0:T(256)S(1)}, f32[256]{0:T(256)}, u32[]{:S(2)}) copy-start(f32[256]{0:T(256)} %param.19) | copy-start | bytes 3076
  32.7 22.9 %copy-start.3 = (f32[256]{0:T(256)S(1)}, f32[256]{0:T(256)}, u32[]{:S(2)}) copy-start(f32[256]{0:T(256)} %param.18) | copy-start | bytes 3076

commit v4 on v3

--- a/solution.py
+++ b/solution.py
@@ -101,7 +101,16 @@
     stat_rows = jnp.concatenate([high, low, jnp.zeros((4, channels), jnp.float32)], 0)
     stat_rows = jnp.broadcast_to(stat_rows.astype(jnp.bfloat16)[None], (devices, 8, channels))
     outgoing = jnp.concatenate([tiles, stat_rows], 1)
-    received = lax.all_to_all(outgoing, "tile", split_axis=0, concat_axis=0, tiled=True)
+    arrived = [None] * devices
+    for step in range(devices):
+        block = jnp.take(outgoing, (device + step) % devices, axis=0)
+        if step:
+            block = lax.ppermute(
+                block, "tile", [(src, (src + step) % devices) for src in range(devices)]
+            )
+        arrived[step] = block
+    by_step = jnp.stack(arrived, 0)
+    received = jnp.take(by_step, (device - jnp.arange(devices)) % devices, axis=0)
     block_part = received[:, : per_dest * tile_rows * columns].reshape(
         devices * per_dest, tile_rows, columns, channels
     )

time: 57.7 us -> 73.2 us (1.27)
  starting transfers between devices: 6.61 us -> 30.1 us
  waiting for transfers between devices: 20.6 us -> 12.1 us
  other arithmetic: 8.96 us -> 8.01 us
    ppermute x0 -> x15, starting transfers between devices: none -> 30.1 us  [local(): lax.ppermute(block, 'tile', [(src, (src + step) % devices) for src in ran...]
    all_to_all x1 -> x0, waiting for transfers between devices: 20.6 us -> none  [local(): lax.all_to_all(outgoing, 'tile', split_axis=0, concat_axis=0, tiled=True)]
    ppermute x0 -> x15, waiting for transfers between devices: none -> 12.1 us  [local(): lax.ppermute(block, 'tile', [(src, (src + step) % devices) for src in ran...]
    all_to_all x1 -> x0, starting transfers between devices: 6.61 us -> none  [local(): lax.all_to_all(outgoing, 'tile', split_axis=0, concat_axis=0, tiled=True)]
    concatenate x1 -> x0, other arithmetic: 0.96 us -> none  [local(): outgoing = jnp.concatenate([tiles, stat_rows], 1)]
    unnamed x18 -> x36, local copies, waits for them, and re-layouts: 2.63 us -> 2.74 us
  transfers between devices with their start and end apart: 1 -> 15, of which waited for: 1 -> 6; matrix products, arithmetic and copies ran while one was open for 0% -> 1% of each run, Pallas kernels for 0% -> 0%
where the time goes in v4:
time: 73.2 us; the launch traced here: 72.4 us
  starting transfers between devices  30.1 us (41%)
  waiting for transfers between devices  12.1 us (17%)
  local copies, waits for them, and re-layouts  11.1 us (15%)
  other arithmetic  8.01 us (11%)
  matrix products  6.58 us (9%)
  between operations  4.54 us (6%)
    ppermute x15, starting transfers between devices, local(): lax.ppermute(block, 'tile', [(src, (src + step) % devices) for src in ran...  30.1 us
    ppermute x15, waiting for transfers between devices, local(): lax.ppermute(block, 'tile', [(src, (src + step) % devices) for src in ran...  12.1 us
    dot_general x3, matrix products, local(): jnp.dot(unfolded[frame_lag:frame_lag + frames].reshape(-1, 9 * channels),...  6.58 us
    unnamed x36, local copies, waits for them, and re-layouts  2.74 us
    slice x1, local copies, waits for them, and re-layouts, local(): kernel[frame_lag]  2.21 us
    reduce_sum x2, other arithmetic, normalize(): jnp.sum(grouped * grouped * live_mask, axis=(0, 1, 3)) / members  1.78 us
    slice x1, local copies, waits for them, and re-layouts, local(): unfolded[frame_lag:frame_lag + frames].reshape(-1, 9 * channels)  1.74 us
  transfers between devices with their start and end apart: 15, of which 6 were waited for; matrix products, arithmetic and copies ran while one was open for 1% of the time, Pallas kernels for 0%

profile of v4, /device:TPU:9, one launch (start us, length us, event | category | flops | bytes accessed | tf_op | source)
XLA Modules:
  0.0 72.4 jit_solution(5820564895286896825)
XLA Ops:
  0.6 0.9 %select_reduce_fusion.2 = s32[16]{0:T(128)S(1)} fusion(s32[16]{0:T(128)} %param.14, s32[16]{0:T(128)} %param.15), kind=kLoop, calls=%fused_computation.125 | loop fusion | flops 752 | bytes 192 | tf_op jit(solution)/shard_map/reduce_sum | solution.py:51
  1.8 1.3 %fusion.41 = (s32[]{:T(128)}, s32[16]{0:T(128)S(1)}, s32[]{:T(128)}) fusion(s32[16]{0:T(128)} %param.15, s32[]{:T(128)S(6)} %axis_index.12, s32[16]{0:T(128)S(1)} %reduce.8, s32[16]{0:T(128)S(1)} %select_reduce_fusion.2, s32[16]{0:T(128)} %param.14), kind=kLoop, calls=%fused_computation.180 | loop fusion | flops 126 | bytes 332 | tf_op jit(solution)/shard_map/reduce_sum | solution.py:53
  7.2 1.7 %fusion.14 = (f32[256]{0:T(256)S(1)}, f32[256]{0:T(256)S(1)}) fusion(bf16[12,16,8,256]{3,2,1,0:T(8,128)(2,1)} %param.13, f32[12]{0:T(128)S(1)} %compare_convert_fusion), kind=kLoop, calls=%fused_computation.51 | loop fusion | flops 2358784 | bytes 788528 | tf_op jit(solution)/shard_map/reduce_sum | solution.py:22
  9.6 1.2 %fusion.12 = bf16[12,16,8,256]{3,2,1,0:T(8,128)(2,1)S(1)} fusion(bf16[12,16,8,256]{3,2,1,0:T(8,128)(2,1)S(1)} %copy-done, f32[256]{0:T(256)} %param.17, f32[256]{0:T(256)} %param.16, f32[256]{0:T(256)S(1)} %mul.175, f32[256]{0:T(256)S(1)} %sub.136), kind=kLoop, calls=%fused_computation.49 | loop fusion | flops 3932160 | bytes 1576960 | tf_op jit(solution)/shard_map/convert_element_type | solution.py:56
  12.3 1.7 %fusion.52 = (bf16[12,16,8,2304]{3,2,1,0:T(8,128)(2,1)S(1)}, bf16[12,16,8,2304]{3,2,1,0:T(8,128)(2,1)S(1)}, bf16[12,16,8,2304]{3,2,1,0:T(8,128)(2,1)S(1)}) fusion(bf16[14,16,8,2304]{3,2,1,0:T(8,128)(2,1)S(1)} %fusion.23), kind=kLoop, calls=%fused_computation.200 | loop fusion | bytes 42467328 | tf_op jit(solution)/shard_map/slice | solution.py:71
  14.0 2.2 %fusion.53 = (bf16[1,3,3,256,256]{4,3,2,1,0:T(8,128)(2,1)S(1)}, bf16[1,3,3,256,256]{4,3,2,1,0:T(8,128)(2,1)S(1)}, bf16[1,3,3,256,256]{4,3,2,1,0:T(8,128)(2,1)S(1)}) fusion(bf16[3,3,3,256,256]{4,3,2,1,0:T(8,128)(2,1)} %param.18), kind=kLoop, calls=%fused_computation.201 | loop fusion | bytes 7077888 | tf_op jit(solution)/shard_map/slice | solution.py:72
  16.3 2.1 %fusion.54 = f32[1536,256]{1,0:T(8,128)S(1)} fusion(bf16[1536,2304]{1,0:T(8,128)(2,1)S(1)} %bitcast.122, bf16[2304,256]{1,0:T(8,128)(2,1)S(1)} %bitcast.129), kind=kOutput, calls=%fused_computation.202 | convolution fusion | flops 1811939328 | bytes 9830400 | tf_op jit(solution)/shard_map/dot_general | solution.py:70
  18.4 2.2 %convolution_add_fusion.1 = f32[1536,256]{1,0:T(8,128)S(1)} fusion(f32[1536,256]{1,0:T(8,128)S(1)} %fusion.54, bf16[1536,2304]{1,0:T(8,128)(2,1)S(1)} %bitcast.121, bf16[2304,256]{1,0:T(8,128)(2,1)S(1)} %bitcast.128), kind=kOutput, calls=%fused_computation.31 | convolution fusion | flops 1812332544 | bytes 11403264 | tf_op jit(solution)/shard_map/dot_general | solution.py:70
  20.6 2.3 %fusion = (f32[256]{0:T(256)S(1)}, f32[256]{0:T(256)S(1)}, f32[1536,256]{1,0:T(8,128)S(1)}) fusion(f32[1536]{0:T(1024)S(1)} %broadcast_bitcast_fusion, f32[256]{0:T(256)S(1)} %copy-done.2, f32[1536,256]{1,0:T(8,128)S(1)} %convolution_add_fusion.1, bf16[1536,2304]{1,0:T(8,128)(2,1)S(1)} %bitcast.120, bf16[2304,256]{1,0:T(8,128)(2,1)S(1)} %bitcast.127), kind=kOutput, calls=%fused_computation.37 | convolution fusion | flops 1815477760 | bytes 11412480 | tf_op jit(solution)/shard_map/dot_general | solution.py:70
  24.8 3.3 %collective-permute-start.9 = (bf16[104,256]{1,0:T(8,128)(2,1)S(1)}, bf16[104,256]{1,0:T(8,128)(2,1)S(1)}, u32[]{:S(2)}, u32[]{:S(2)}) collective-permute-start(bf16[104,256]{1,0:T(8,128)(2,1)S(1)} %select_bitcast_fusion.7), channel_id=1, source_target_pairs={{0,10},{1,11},{2,12},{3,13},{4,14},{5,15},{6,0},{7,1},{8,2},{9,3},... | collective-permute-start | bytes 159752 | tf_op jit(solution)/shard_map/ppermute | solution.py:108
  28.4 2.3 %collective-permute-start.5 = (bf16[104,256]{1,0:T(8,128)(2,1)S(1)}, bf16[104,256]{1,0:T(8,128)(2,1)S(1)}, u32[]{:S(2)}, u32[]{:S(2)}) collective-permute-start(bf16[104,256]{1,0:T(8,128)(2,1)S(1)} %get-tuple-element.49), channel_id=1, source_target_pairs={{0,6},{1,7},{2,8},{3,9},{4,10},{5,11},{6,12},{7,13},{8,14},{9,15},... | collective-permute-start | bytes 159752 | tf_op jit(solution)/shard_map/ppermute | solution.py:108
  30.8 2.7 %collective-permute-start = (bf16[104,256]{1,0:T(8,128)(2,1)S(1)}, bf16[104,256]{1,0:T(8,128)(2,1)S(1)}, u32[]{:S(2)}, u32[]{:S(2)}) collective-permute-start(bf16[104,256]{1,0:T(8,128)(2,1)S(1)} %get-tuple-element.41), channel_id=1, source_target_pairs={{0,1},{1,2},{2,3},{3,4},{4,5},{5,6},{6,7},{7,8},{8,9},{9,10},{10,1... | collective-permute-start | bytes 159752 | tf_op jit(solution)/shard_map/ppermute | solution.py:108
  33.9 0.8 %collective-permute-done = bf16[104,256]{1,0:T(8,128)(2,1)S(1)} collective-permute-done((bf16[104,256]{1,0:T(8,128)(2,1)S(1)}, bf16[104,256]{1,0:T(8,128)(2,1)S(1)}, u32[]{:S(2)}, u32[]{:S(2)}) %collective-permute-start) | collective-permute-done | bytes 53280 | tf_op jit(solution)/shard_map/ppermute | solution.py:108
  34.7 1.6 %collective-permute-start.1 = (bf16[104,256]{1,0:T(8,128)(2,1)S(1)}, bf16[104,256]{1,0:T(8,128)(2,1)S(1)}, u32[]{:S(2)}, u32[]{:S(2)}) collective-permute-start(bf16[104,256]{1,0:T(8,128)(2,1)S(1)} %get-tuple-element.43), channel_id=1, source_target_pairs={{0,2},{1,3},{2,4},{3,5},{4,6},{5,7},{6,8},{7,9},{8,10},{9,11},{10,... | collective-permute-start | bytes 159752 | tf_op jit(solution)/shard_map/ppermute | solution.py:108
  36.3 2.3 %collective-permute-done.1 = bf16[104,256]{1,0:T(8,128)(2,1)S(1)} collective-permute-done((bf16[104,256]{1,0:T(8,128)(2,1)S(1)}, bf16[104,256]{1,0:T(8,128)(2,1)S(1)}, u32[]{:S(2)}, u32[]{:S(2)}) %collective-permute-start.1) | collective-permute-done | bytes 53280 | tf_op jit(solution)/shard_map/ppermute | solution.py:108
  38.6 4.9 %collective-permute-start.2 = (bf16[104,256]{1,0:T(8,128)(2,1)S(1)}, bf16[104,256]{1,0:T(8,128)(2,1)S(1)}, u32[]{:S(2)}, u32[]{:S(2)}) collective-permute-start(bf16[104,256]{1,0:T(8,128)(2,1)S(1)} %get-tuple-element.44), channel_id=1, source_target_pairs={{0,3},{1,4},{2,5},{3,6},{4,7},{5,8},{6,9},{7,10},{8,11},{9,12},{10... | collective-permute-start | bytes 159752 | tf_op jit(solution)/shard_map/ppermute | solution.py:108
  43.5 2.1 %collective-permute-done.2 = bf16[104,256]{1,0:T(8,128)(2,1)S(1)} collective-permute-done((bf16[104,256]{1,0:T(8,128)(2,1)S(1)}, bf16[104,256]{1,0:T(8,128)(2,1)S(1)}, u32[]{:S(2)}, u32[]{:S(2)}) %collective-permute-start.2) | collective-permute-done | bytes 53280 | tf_op jit(solution)/shard_map/ppermute | solution.py:108
  45.9 5.2 %collective-permute-start.6 = (bf16[104,256]{1,0:T(8,128)(2,1)S(1)}, bf16[104,256]{1,0:T(8,128)(2,1)S(1)}, u32[]{:S(2)}, u32[]{:S(2)}) collective-permute-start(bf16[104,256]{1,0:T(8,128)(2,1)S(1)} %get-tuple-element.50), channel_id=1, source_target_pairs={{0,7},{1,8},{2,9},{3,10},{4,11},{5,12},{6,13},{7,14},{8,15},{9,0},... | collective-permute-start | bytes 159752 | tf_op jit(solution)/shard_map/ppermute | solution.py:108
  51.1 3.4 %collective-permute-done.4 = bf16[104,256]{1,0:T(8,128)(2,1)S(1)} collective-permute-done((bf16[104,256]{1,0:T(8,128)(2,1)S(1)}, bf16[104,256]{1,0:T(8,128)(2,1)S(1)}, u32[]{:S(2)}, u32[]{:S(2)}) %collective-permute-start.4) | collective-permute-done | bytes 53280 | tf_op jit(solution)/shard_map/ppermute | solution.py:108
  54.5 3.3 %collective-permute-start.10 = (bf16[104,256]{1,0:T(8,128)(2,1)S(1)}, bf16[104,256]{1,0:T(8,128)(2,1)S(1)}, u32[]{:S(2)}, u32[]{:S(2)}) collective-permute-start(bf16[104,256]{1,0:T(8,128)(2,1)S(1)} %get-tuple-element.51), channel_id=1, source_target_pairs={{0,11},{1,12},{2,13},{3,14},{4,15},{5,0},{6,1},{7,2},{8,3},{9,4},{... | collective-permute-start | bytes 159752 | tf_op jit(solution)/shard_map/ppermute | solution.py:108
  58.5 2.8 %collective-permute-start.12 = (bf16[104,256]{1,0:T(8,128)(2,1)S(1)}, bf16[104,256]{1,0:T(8,128)(2,1)S(1)}, u32[]{:S(2)}, u32[]{:S(2)}) collective-permute-start(bf16[104,256]{1,0:T(8,128)(2,1)S(1)} %get-tuple-element.45), channel_id=1, source_target_pairs={{0,13},{1,14},{2,15},{3,0},{4,1},{5,2},{6,3},{7,4},{8,5},{9,6},{10... | collective-permute-start | bytes 159752 | tf_op jit(solution)/shard_map/ppermute | solution.py:108
  61.3 2.9 %collective-permute-start.13 = (bf16[104,256]{1,0:T(8,128)(2,1)S(1)}, bf16[104,256]{1,0:T(8,128)(2,1)S(1)}, u32[]{:S(2)}, u32[]{:S(2)}) collective-permute-start(bf16[104,256]{1,0:T(8,128)(2,1)S(1)} %get-tuple-element.42), channel_id=1, source_target_pairs={{0,14},{1,15},{2,0},{3,1},{4,2},{5,3},{6,4},{7,5},{8,6},{9,7},{10,... | collective-permute-start | bytes 159752 | tf_op jit(solution)/shard_map/ppermute | solution.py:108
  64.4 1.1 %collective-permute-done.13 = bf16[104,256]{1,0:T(8,128)(2,1)S(1)} collective-permute-done((bf16[104,256]{1,0:T(8,128)(2,1)S(1)}, bf16[104,256]{1,0:T(8,128)(2,1)S(1)}, u32[]{:S(2)}, u32[]{:S(2)}) %collective-permute-start.13) | collective-permute-done | bytes 53280 | tf_op jit(solution)/shard_map/ppermute | solution.py:108
  65.4 2.4 %collective-permute-done.14 = bf16[104,256]{1,0:T(8,128)(2,1)S(1)} collective-permute-done((bf16[104,256]{1,0:T(8,128)(2,1)S(1)}, bf16[104,256]{1,0:T(8,128)(2,1)S(1)}, u32[]{:S(2)}, u32[]{:S(2)}) %collective-permute-start.14) | collective-permute-done | bytes 53280 | tf_op jit(solution)/shard_map/ppermute | solution.py:108
  (116 shorter events, 11.2 us)
Async XLA Ops:
  0.6 9.0 %copy-start = (bf16[12,16,8,256]{3,2,1,0:T(8,128)(2,1)S(1)}, bf16[12,16,8,256]{3,2,1,0:T(8,128)(2,1)}, u32[]{:S(2)}) copy-start(bf16[12,16,8,256]{3,2,1,0:T(8,128)(2,1)} %param.13) | copy-start | bytes 2359300
  18.4 2.2 %copy-start.2 = (f32[256]{0:T(256)S(1)}, f32[256]{0:T(256)}, u32[]{:S(2)}) copy-start(f32[256]{0:T(256)} %param.19) | copy-start | bytes 3076
  24.8 39.4 %collective-permute-start.9 = (bf16[104,256]{1,0:T(8,128)(2,1)S(1)}, bf16[104,256]{1,0:T(8,128)(2,1)S(1)}, u32[]{:S(2)}, u32[]{:S(2)}) collective-permute-start(bf16[104,256]{1,0:T(8,128)(2,1)S(1)} %select_bitcast_fusion.7), channel_id=1, source_target_pairs={{0,10},{1,11},{2,12},{3,13},{4,14},{5,15},{6,0},{7,1},{8,2},{9,3},... | collective-permute-start | bytes 159752 | tf_op jit(solution)/shard_map/ppermute | solution.py:108
  28.2 30.3 %collective-permute-start.7 = (bf16[104,256]{1,0:T(8,128)(2,1)S(1)}, bf16[104,256]{1,0:T(8,128)(2,1)S(1)}, u32[]{:S(2)}, u32[]{:S(2)}) collective-permute-start(bf16[104,256]{1,0:T(8,128)(2,1)S(1)} %get-tuple-element.52), channel_id=1, source_target_pairs={{0,8},{1,9},{2,10},{3,11},{4,12},{5,13},{6,14},{7,15},{8,0},{9,1},... | collective-permute-start | bytes 159752 | tf_op jit(solution)/shard_map/ppermute | solution.py:108
  28.3 5.3 %copy-start.1 = (s32[16]{0:T(128)S(1)}, s32[16]{0:T(128)}, u32[]{:S(2)}) copy-start(s32[16]{0:T(128)} %param.15) | copy-start | bytes 196
  28.4 26.2 %collective-permute-start.5 = (bf16[104,256]{1,0:T(8,128)(2,1)S(1)}, bf16[104,256]{1,0:T(8,128)(2,1)S(1)}, u32[]{:S(2)}, u32[]{:S(2)}) collective-permute-start(bf16[104,256]{1,0:T(8,128)(2,1)S(1)} %get-tuple-element.49), channel_id=1, source_target_pairs={{0,6},{1,7},{2,8},{3,9},{4,10},{5,11},{6,12},{7,13},{8,14},{9,15},... | collective-permute-start | bytes 159752 | tf_op jit(solution)/shard_map/ppermute | solution.py:108
  30.7 15.3 %collective-permute-start.3 = (bf16[104,256]{1,0:T(8,128)(2,1)S(1)}, bf16[104,256]{1,0:T(8,128)(2,1)S(1)}, u32[]{:S(2)}, u32[]{:S(2)}) collective-permute-start(bf16[104,256]{1,0:T(8,128)(2,1)S(1)} %get-tuple-element.46), channel_id=1, source_target_pairs={{0,4},{1,5},{2,6},{3,7},{4,8},{5,9},{6,10},{7,11},{8,12},{9,13},{1... | collective-permute-start | bytes 159752 | tf_op jit(solution)/shard_map/ppermute | solution.py:108
  30.8 3.9 %collective-permute-start = (bf16[104,256]{1,0:T(8,128)(2,1)S(1)}, bf16[104,256]{1,0:T(8,128)(2,1)S(1)}, u32[]{:S(2)}, u32[]{:S(2)}) collective-permute-start(bf16[104,256]{1,0:T(8,128)(2,1)S(1)} %get-tuple-element.41), channel_id=1, source_target_pairs={{0,1},{1,2},{2,3},{3,4},{4,5},{5,6},{6,7},{7,8},{8,9},{9,10},{10,1... | collective-permute-start | bytes 159752 | tf_op jit(solution)/shard_map/ppermute | solution.py:108
  34.7 3.9 %collective-permute-start.1 = (bf16[104,256]{1,0:T(8,128)(2,1)S(1)}, bf16[104,256]{1,0:T(8,128)(2,1)S(1)}, u32[]{:S(2)}, u32[]{:S(2)}) collective-permute-start(bf16[104,256]{1,0:T(8,128)(2,1)S(1)} %get-tuple-element.43), channel_id=1, source_target_pairs={{0,2},{1,3},{2,4},{3,5},{4,6},{5,7},{6,8},{7,9},{8,10},{9,11},{10,... | collective-permute-start | bytes 159752 | tf_op jit(solution)/shard_map/ppermute | solution.py:108
  38.6 7.0 %collective-permute-start.2 = (bf16[104,256]{1,0:T(8,128)(2,1)S(1)}, bf16[104,256]{1,0:T(8,128)(2,1)S(1)}, u32[]{:S(2)}, u32[]{:S(2)}) collective-permute-start(bf16[104,256]{1,0:T(8,128)(2,1)S(1)} %get-tuple-element.44), channel_id=1, source_target_pairs={{0,3},{1,4},{2,5},{3,6},{4,7},{5,8},{6,9},{7,10},{8,11},{9,12},{10... | collective-permute-start | bytes 159752 | tf_op jit(solution)/shard_map/ppermute | solution.py:108
  45.6 8.9 %collective-permute-start.4 = (bf16[104,256]{1,0:T(8,128)(2,1)S(1)}, bf16[104,256]{1,0:T(8,128)(2,1)S(1)}, u32[]{:S(2)}, u32[]{:S(2)}) collective-permute-start(bf16[104,256]{1,0:T(8,128)(2,1)S(1)} %get-tuple-element.47), channel_id=1, source_target_pairs={{0,5},{1,6},{2,7},{3,8},{4,9},{5,10},{6,11},{7,12},{8,13},{9,14},{... | collective-permute-start | bytes 159752 | tf_op jit(solution)/shard_map/ppermute | solution.py:108
  45.9 11.9 %collective-permute-start.6 = (bf16[104,256]{1,0:T(8,128)(2,1)S(1)}, bf16[104,256]{1,0:T(8,128)(2,1)S(1)}, u32[]{:S(2)}, u32[]{:S(2)}) collective-permute-start(bf16[104,256]{1,0:T(8,128)(2,1)S(1)} %get-tuple-element.50), channel_id=1, source_target_pairs={{0,7},{1,8},{2,9},{3,10},{4,11},{5,12},{6,13},{7,14},{8,15},{9,0},... | collective-permute-start | bytes 159752 | tf_op jit(solution)/shard_map/ppermute | solution.py:108
  54.5 6.8 %collective-permute-start.8 = (bf16[104,256]{1,0:T(8,128)(2,1)S(1)}, bf16[104,256]{1,0:T(8,128)(2,1)S(1)}, u32[]{:S(2)}, u32[]{:S(2)}) collective-permute-start(bf16[104,256]{1,0:T(8,128)(2,1)S(1)} %get-tuple-element.53), channel_id=1, source_target_pairs={{0,9},{1,10},{2,11},{3,12},{4,13},{5,14},{6,15},{7,0},{8,1},{9,2},... | collective-permute-start | bytes 159752 | tf_op jit(solution)/shard_map/ppermute | solution.py:108
  54.5 9.7 %collective-permute-start.10 = (bf16[104,256]{1,0:T(8,128)(2,1)S(1)}, bf16[104,256]{1,0:T(8,128)(2,1)S(1)}, u32[]{:S(2)}, u32[]{:S(2)}) collective-permute-start(bf16[104,256]{1,0:T(8,128)(2,1)S(1)} %get-tuple-element.51), channel_id=1, source_target_pairs={{0,11},{1,12},{2,13},{3,14},{4,15},{5,0},{6,1},{7,2},{8,3},{9,4},{... | collective-permute-start | bytes 159752 | tf_op jit(solution)/shard_map/ppermute | solution.py:108
  57.8 6.5 %collective-permute-start.11 = (bf16[104,256]{1,0:T(8,128)(2,1)S(1)}, bf16[104,256]{1,0:T(8,128)(2,1)S(1)}, u32[]{:S(2)}, u32[]{:S(2)}) collective-permute-start(bf16[104,256]{1,0:T(8,128)(2,1)S(1)} %get-tuple-element.48), channel_id=1, source_target_pairs={{0,12},{1,13},{2,14},{3,15},{4,0},{5,1},{6,2},{7,3},{8,4},{9,5},{1... | collective-permute-start | bytes 159752 | tf_op jit(solution)/shard_map/ppermute | solution.py:108
  58.5 5.8 %collective-permute-start.12 = (bf16[104,256]{1,0:T(8,128)(2,1)S(1)}, bf16[104,256]{1,0:T(8,128)(2,1)S(1)}, u32[]{:S(2)}, u32[]{:S(2)}) collective-permute-start(bf16[104,256]{1,0:T(8,128)(2,1)S(1)} %get-tuple-element.45), channel_id=1, source_target_pairs={{0,13},{1,14},{2,15},{3,0},{4,1},{5,2},{6,3},{7,4},{8,5},{9,6},{10... | collective-permute-start | bytes 159752 | tf_op jit(solution)/shard_map/ppermute | solution.py:108
  61.3 4.1 %collective-permute-start.13 = (bf16[104,256]{1,0:T(8,128)(2,1)S(1)}, bf16[104,256]{1,0:T(8,128)(2,1)S(1)}, u32[]{:S(2)}, u32[]{:S(2)}) collective-permute-start(bf16[104,256]{1,0:T(8,128)(2,1)S(1)} %get-tuple-element.42), channel_id=1, source_target_pairs={{0,14},{1,15},{2,0},{3,1},{4,2},{5,3},{6,4},{7,5},{8,6},{9,7},{10,... | collective-permute-start | bytes 159752 | tf_op jit(solution)/shard_map/ppermute | solution.py:108
  64.2 3.6 %collective-permute-start.14 = (bf16[104,256]{1,0:T(8,128)(2,1)S(1)}, bf16[104,256]{1,0:T(8,128)(2,1)S(1)}, u32[]{:S(2)}, u32[]{:S(2)}) collective-permute-start(bf16[104,256]{1,0:T(8,128)(2,1)S(1)} %get-tuple-element.39), channel_id=1, source_target_pairs={{0,15},{1,0},{2,1},{3,2},{4,3},{5,4},{6,5},{7,6},{8,7},{9,8},{10,9... | collective-permute-start | bytes 159752 | tf_op jit(solution)/shard_map/ppermute | solution.py:108
  68.6 2.1 %copy-start.3 = (f32[256]{0:T(256)S(1)}, f32[256]{0:T(256)}, u32[]{:S(2)}) copy-start(f32[256]{0:T(256)} %param.21) | copy-start | bytes 3076
  68.6 2.0 %copy-start.4 = (f32[256]{0:T(256)S(1)}, f32[256]{0:T(256)}, u32[]{:S(2)}) copy-start(f32[256]{0:T(256)} %param.20) | copy-start | bytes 3076

commit v5 on v3

--- a/solution.py
+++ b/solution.py
@@ -1,6 +1,8 @@
 import jax
 import jax.numpy as jnp
 from jax import lax
+from jax.experimental import pallas as pl
+from jax.experimental.pallas import tpu as pltpu
 from jax.sharding import PartitionSpec as P
 
 GROUPS = 32
@@ -14,18 +16,61 @@
 def normalize(values, frame_count, scaling, offsets):
     frames = values.shape[0]
     channels = values.shape[-1]
+    flat = values.reshape(frames, -1, channels)
+    live_mask = (jnp.arange(frames) < frame_count).astype(jnp.float32)[:, None]
+    members = frame_count.astype(jnp.float32) * flat.shape[1] * (channels // GROUPS)
+    first = jnp.sum(jnp.sum(flat, axis=1) * live_mask, axis=0)
+    second = jnp.sum(jnp.sum(flat * flat, axis=1) * live_mask, axis=0)
+    group_mean = jnp.sum(first.reshape(GROUPS, -1), axis=1) / members
+    spread = jnp.sum(second.reshape(GROUPS, -1), axis=1) / members - group_mean * group_mean
+    inverse = lax.rsqrt(spread + eps)
     grouped = values.reshape(frames, -1, GROUPS, channels // GROUPS)
-    live_mask = (jnp.arange(frames) < frame_count).astype(jnp.float32)[:, None, None, None]
-    members = frame_count.astype(jnp.float32) * grouped.shape[1] * grouped.shape[3]
-    group_mean = jnp.sum(grouped * live_mask, axis=(0, 1, 3)) / members
-    spread = (
-        jnp.sum(grouped * grouped * live_mask, axis=(0, 1, 3)) / members - group_mean * group_mean
-    )
-    inverse = lax.rsqrt(spread + eps)
     normed = (grouped - group_mean[:, None]) * inverse[:, None] * scaling.reshape(
         GROUPS, -1
     ) + offsets.reshape(GROUPS, -1)
     return jax.nn.silu(normed).reshape(values.shape)
+
+
+def conv_body(x_ref, w_ref, b_ref, o_ref, s1_ref, s2_ref):
+    step = 2
+    positions = x_ref.shape[1]
+
+    def one(j, carry):
+        frame = pl.multiple_of(j * step, step)
+        acc = jnp.broadcast_to(b_ref[...], (step * positions, o_ref.shape[-1]))
+        for frame_lag in range(3):
+            lhs = x_ref[pl.ds(frame + frame_lag, step)].reshape(step * positions, -1)
+            acc = acc + jnp.dot(lhs, w_ref[frame_lag], preferred_element_type=jnp.float32)
+        out = acc.astype(jnp.bfloat16)
+        o_ref[pl.ds(frame, step)] = out.reshape(step, positions, -1)
+        value = out.astype(jnp.float32).reshape(step, positions, -1)
+        s1_ref[pl.ds(frame, step)] = jnp.sum(value, axis=1, keepdims=True)
+        s2_ref[pl.ds(frame, step)] = jnp.sum(value * value, axis=1, keepdims=True)
+        return carry
+
+    lax.fori_loop(0, o_ref.shape[0] // step, one, 0)
+
+
+def conv_call(unfolded, kernel, bias):
+    frames = unfolded.shape[0] - 2
+    positions, width = unfolded.shape[1], unfolded.shape[2]
+    channels = kernel.shape[-1]
+    vmem = pl.BlockSpec(memory_space=pltpu.VMEM)
+    return pl.pallas_call(
+        conv_body,
+        out_shape=(
+            jax.ShapeDtypeStruct((frames, positions, channels), jnp.bfloat16),
+            jax.ShapeDtypeStruct((frames, 1, channels), jnp.float32),
+            jax.ShapeDtypeStruct((frames, 1, channels), jnp.float32),
+        ),
+        in_specs=[vmem, vmem, vmem],
+        out_specs=(vmem, vmem, vmem),
+        cost_estimate=pl.CostEstimate(
+            flops=2 * frames * positions * 3 * width * channels,
+            transcendentals=0,
+            bytes_accessed=unfolded.size * 2 + kernel.size * 2 + frames * positions * channels * 2,
+        ),
+    )(unfolded, kernel, bias.reshape(1, channels))
 
 
 def local(
@@ -66,21 +111,15 @@
         axis=-1,
     ).reshape(frames + 2, frame_rows * columns, 9 * channels)
     kernel = conv_weight.reshape(3, 9 * channels, -1)
-    conv = conv_bias + sum(
-        jnp.dot(
-            unfolded[frame_lag : frame_lag + frames].reshape(-1, 9 * channels),
-            kernel[frame_lag],
-            preferred_element_type=jnp.float32,
-        )
-        for frame_lag in range(3)
-    ).reshape(frames, frame_rows, columns, -1)
-    block_out = conv.astype(jnp.bfloat16)
+    block_out, frame_first, frame_second = conv_call(unfolded, kernel, conv_bias)
+    frame_first = frame_first[:, 0]
+    frame_second = frame_second[:, 0]
+    block_out = block_out.reshape(frames, frame_rows, columns, channels)
     per_group = channels // GROUPS
-    grouped = block_out.astype(jnp.float32).reshape(frames, frame_rows * columns, GROUPS, per_group)
-    live_mask = (jnp.arange(frames) < own_count).astype(jnp.float32)[:, None, None, None]
+    live_mask = (jnp.arange(frames) < own_count).astype(jnp.float32)[:, None]
     members = own_count.astype(jnp.float32) * (frame_rows * columns * per_group)
-    first_sum = jnp.sum(grouped * live_mask, axis=(0, 1, 3))
-    second_sum = jnp.sum(grouped * grouped * live_mask, axis=(0, 1, 3))
+    first_sum = jnp.sum(jnp.sum(frame_first * live_mask, axis=0).reshape(GROUPS, per_group), axis=1)
+    second_sum = jnp.sum(jnp.sum(frame_second * live_mask, axis=0).reshape(GROUPS, per_group), axis=1)
     clip_mean = first_sum / members
     clip_spread = second_sum / members - clip_mean * clip_mean
     clip_inverse = lax.rsqrt(clip_spread + eps)
@@ -88,8 +127,8 @@
     tiles = block_out.reshape(frames, NRB, tile_rows, columns, channels)
     tiles = jnp.pad(tiles, ((0, per_dest * classes - frames), (0, 0), (0, 0), (0, 0), (0, 0)))
     tiles = tiles.reshape(per_dest, classes, NRB, tile_rows, columns, channels)
-    shift = own_start // NRB
-    pick = (jnp.arange(classes, dtype=jnp.int32) - shift) % classes
+    lag_of = (jnp.arange(classes, dtype=jnp.int32)[:, None] - (starts // NRB)[None, :] % classes) % classes
+    pick = jnp.sum(jnp.where(clip_order[None, :] == device, lag_of, 0), axis=1)
     tiles = jnp.take(tiles, pick, axis=1)
     tiles = jnp.transpose(tiles, (1, 2, 0, 3, 4, 5)).reshape(
         devices, per_dest * tile_rows * columns, channels

time: 57.7 us -> 61.5 us (1.066)
  Pallas kernels: 0 us -> 12 us
  matrix products: 6.58 us -> 0 us
  between operations: 4.23 us -> 1.58 us
    pallas_call x0 -> x1, Pallas kernels: none -> 12 us  [conv_call(): pl.pallas_call(conv_body, out_shape=(jax.ShapeDtypeStruct((frames, positi...]
    dot_general x3 -> x0, matrix products: 6.58 us -> none  [local(): jnp.dot(unfolded[frame_lag:frame_lag + frames].reshape(-1, 9 * channels),...]
    slice x2 -> x0, local copies, waits for them, and re-layouts: 3.95 us -> none  [the longest x1 2.21 us: local(): kernel[frame_lag]]
    unnamed x18 -> x22, local copies, waits for them, and re-layouts: 2.63 us -> 5.79 us
    gather x1, local copies, waits for them, and re-layouts: 0.6 us -> 1.75 us  [local(): tiles = jnp.take(tiles, pick, axis=1)]
    eq x0 -> x1, other arithmetic: none -> 0.66 us  [local(): pick = jnp.sum(jnp.where(clip_order[None, :] == device, lag_of, 0), axis=1)]
    reduce_sum x6 -> x9, other arithmetic: 3.48 us -> 3.46 us  [the longest x2 1.47 us: normalize(): second = jnp.sum(jnp.sum(flat * flat, axis=1) * live_mask, axis=0)]
where the time goes in v5:
time: 61.5 us; the launch traced here: 61.1 us
  waiting for transfers between devices  20.8 us (34%)
  Pallas kernels  12 us (20%)
  local copies, waits for them, and re-layouts  10.6 us (17%)
  other arithmetic  9.38 us (15%)
  starting transfers between devices  6.74 us (11%)
  between operations  1.58 us (3%)
    all_to_all x1, waiting for transfers between devices, local(): lax.all_to_all(outgoing, 'tile', split_axis=0, concat_axis=0, tiled=True)  20.8 us
    pallas_call x1, Pallas kernels, conv_call(): pl.pallas_call(conv_body, out_shape=(jax.ShapeDtypeStruct((frames, positi...  12 us
    all_to_all x1, starting transfers between devices, local(): lax.all_to_all(outgoing, 'tile', split_axis=0, concat_axis=0, tiled=True)  6.74 us
    unnamed x22, local copies, waits for them, and re-layouts  5.79 us
    gather x1, local copies, waits for them, and re-layouts, local(): tiles = jnp.take(tiles, pick, axis=1)  1.75 us
    convert_element_type x1, other arithmetic, local(): normalize(latents.astype(jnp.float32), own_count, norm_scale, norm_offset)  1.7 us
    reduce_sum x2, other arithmetic, normalize(): second = jnp.sum(jnp.sum(flat * flat, axis=1) * live_mask, axis=0)  1.47 us
    reduce_sum x1, other arithmetic, local(): own_count = jnp.sum(jnp.where(positions == device, frame_counts, 0))  1.29 us
  transfers between devices with their start and end apart: 1, of which 1 were waited for; matrix products, arithmetic and copies ran while one was open for 0% of the time, Pallas kernels for 0%

profile of v5, /device:TPU:9, one launch (start us, length us, event | category | flops | bytes accessed | tf_op | source)
XLA Modules:
  0.0 61.1 jit_solution(6465024033542500995)
XLA Ops:
  0.6 1.3 %fusion.27 = s32[]{:T(128)} fusion(s32[16]{0:T(128)} %param.12, s32[]{:T(128)S(6)} %axis_index.12), kind=kLoop, calls=%fused_computation.106 | loop fusion | flops 47 | bytes 72 | tf_op jit(solution)/shard_map/reduce_sum | solution.py:99
  1.9 0.6 %compare_convert_fusion = f32[12]{0:T(128)S(1)} fusion(s32[]{:T(128)} %fusion.27), kind=kLoop, calls=%fused_computation.77 | loop fusion | flops 24 | bytes 52 | tf_op jit(solution)/shard_map/convert_element_type | solution.py:20
  3.2 0.9 %select_reduce_fusion.2 = s32[16]{0:T(128)S(1)} fusion(s32[16]{0:T(128)} %param.12, s32[16]{0:T(128)} %param.13), kind=kLoop, calls=%fused_computation.56 | loop fusion | flops 752 | bytes 192 | tf_op jit(solution)/shard_map/reduce_sum | solution.py:96
  4.1 0.7 %broadcast_compare_fusion = pred[16]{0:T(512)(128)(4,1)S(1)} fusion(s32[16]{0:T(128)} %param.13, s32[]{:T(128)S(6)} %axis_index.12), kind=kLoop, calls=%fused_computation.120 | loop fusion | flops 16 | bytes 84 | tf_op jit(solution)/shard_map/eq | solution.py:131
  5.2 1.4 %fusion.9 = (f32[12,256]{1,0:T(8,128)S(1)}, f32[12,256]{1,0:T(8,128)S(1)}) fusion(bf16[12,16,8,256]{3,2,1,0:T(8,128)(2,1)} %param.11), kind=kLoop, calls=%fused_computation.25 | loop fusion | flops 1566720 | bytes 811008 | tf_op jit(solution)/shard_map/reduce_sum | solution.py:23
  7.4 1.7 %fusion.8 = bf16[12,16,8,256]{3,2,1,0:T(8,128)(2,1)S(1)} fusion(bf16[12,16,8,256]{3,2,1,0:T(8,128)(2,1)} %param.11, f32[256]{0:T(256)} %param.15, f32[256]{0:T(256)} %param.14, f32[256]{0:T(256)S(1)} %mul.164, f32[256]{0:T(256)S(1)} %sub.113), kind=kLoop, calls=%fused_computation.24 | loop fusion | flops 3932160 | bytes 1576960 | tf_op jit(solution)/shard_map/convert_element_type | solution.py:101
  9.1 0.2 fusion.10
  9.4 0.2 fusion.12
  9.6 0.2 fusion.13
  9.9 0.2 fusion.15
  10.1 0.2 fusion.16
  10.4 0.2 fusion.18
  10.6 3.2 %copy-done = bf16[14,16,8,2304]{3,2,1,0:T(8,128)(2,1)} copy-done((bf16[14,16,8,2304]{3,2,1,0:T(8,128)(2,1)}, bf16[14,16,8,2304]{3,2,1,0:T(8,128)(2,1)S(1)}, u32[]{:S(2)}) %copy-start) | copy-done | bytes 8257560
  13.9 12.0 %shard_map.104 = (bf16[12,128,256]{2,1,0:T(8,128)(2,1)}, f32[12,1,256]{2,1,0:T(1,128)}, f32[12,1,256]{2,1,0:T(1,128)}) custom-call(bf16[14,128,2304]{2,1,0:T(8,128)(2,1)} %bitcast.51, bf16[3,2304,256]{2,1,0:T(8,128)(2,1)} %bitcast.53, f32[1,256]{1,0:T(1,128)} %bitcast.54), custom_call_target="tpu_custom_call" | custom-call | flops 5435817984 | bytes 12582912 | tf_op jit(solution)/shard_map/pallas_call | solution.py:59
  25.9 1.8 %gather_fusion = bf16[2,6,8,2,8,256]{5,4,3,2,1,0:T(8,128)(2,1)S(1)} fusion(bf16[6,2,8,2,8,256]{5,4,3,2,1,0:T(8,128)(2,1)} %bitcast.50, s32[1024]{0:T(1024)S(1)} %get-tuple-element.38), kind=kCustom, calls=%fused_computation.2 | custom fusion | bytes 1572872 | tf_op jit(solution)/shard_map/jit(_take)/gather | solution.py:132
  28.8 1.0 %pad_maximum_fusion = bf16[16,104,256]{2,1,0:T(8,128)(2,1)} fusion(bf16[16,8,256]{2,1,0:T(8,128)(2,1)S(1)} %broadcast_in_dim.109, bf16[16,96,256]{2,1,0:T(8,128)(2,1)S(1)} %bitcast.48), kind=kLoop, calls=%fused_computation.35 | loop fusion | flops 1703936 | bytes 1703936 | tf_op jit(solution)/shard_map/concatenate | solution.py:142
  29.8 6.7 %all-to-all-start = ((bf16[16,104,256]{2,1,0:T(8,128)(2,1)}), bf16[16,104,256]{2,1,0:T(8,128)(2,1)S(1)}, u32[]{:S(2)}, u32[]{:S(2)}) async-start(bf16[16,104,256]{2,1,0:T(8,128)(2,1)} %pad_maximum_fusion), calls=%async_computation | async-start | bytes 1703936 | tf_op jit(solution)/shard_map/all_to_all | solution.py:143
  36.6 20.8 %all-to-all-done = bf16[16,104,256]{2,1,0:T(8,128)(2,1)S(1)} async-done(((bf16[16,104,256]{2,1,0:T(8,128)(2,1)}), bf16[16,104,256]{2,1,0:T(8,128)(2,1)S(1)}, u32[]{:S(2)}, u32[]{:S(2)}) %all-to-all-start) | async-done | bytes 852000 | tf_op jit(solution)/shard_map/all_to_all | solution.py:143
  57.5 0.6 gather_fusion.3
  58.1 0.6 gather_fusion.2
  58.8 0.6 gather_fusion.1
  59.4 0.3 multiply_convert_fusion
  59.7 0.7 %copy.26 = bf16[2,32,8,256]{3,2,1,0:T(8,128)(2,1)} copy(bf16[2,32,8,256]{3,2,0,1:T(8,128)(2,1)S(1)} %get-tuple-element.24) | data formatting | bytes 524288
  60.4 0.7 %copy.27 = bf16[2,32,8,256]{3,2,1,0:T(8,128)(2,1)} copy(bf16[2,32,8,256]{3,2,0,1:T(8,128)(2,1)S(1)} %get-tuple-element.23) | data formatting | bytes 524288
  (62 shorter events, 3.0 us)
Async XLA Ops:
  10.3 3.5 %copy-start.5 = (s32[16]{0:T(128)S(1)}, s32[16]{0:T(128)}, u32[]{:S(2)}) copy-start(s32[16]{0:T(128)} %param.13) | copy-start | bytes 196
  10.6 3.2 %copy-start = (bf16[14,16,8,2304]{3,2,1,0:T(8,128)(2,1)}, bf16[14,16,8,2304]{3,2,1,0:T(8,128)(2,1)S(1)}, u32[]{:S(2)}) copy-start(bf16[14,16,8,2304]{3,2,1,0:T(8,128)(2,1)S(1)} %fusion.18) | copy-start | bytes 24772612
  25.9 2.0 %copy-start.1 = (f32[12,1,256]{2,1,0:T(1,128)S(1)}, f32[12,1,256]{2,1,0:T(1,128)}, u32[]{:S(2)}) copy-start(f32[12,1,256]{2,1,0:T(1,128)} %get-tuple-element.7) | copy-start | bytes 36868
  25.9 2.0 %copy-start.2 = (f32[12,1,256]{2,1,0:T(1,128)S(1)}, f32[12,1,256]{2,1,0:T(1,128)}, u32[]{:S(2)}) copy-start(f32[12,1,256]{2,1,0:T(1,128)} %get-tuple-element.8) | copy-start | bytes 36868
  29.8 29.6 %copy-start.3 = (f32[256]{0:T(256)S(1)}, f32[256]{0:T(256)}, u32[]{:S(2)}) copy-start(f32[256]{0:T(256)} %param.19) | copy-start | bytes 3076
  29.8 29.6 %copy-start.4 = (f32[256]{0:T(256)S(1)}, f32[256]{0:T(256)}, u32[]{:S(2)}) copy-start(f32[256]{0:T(256)} %param.18) | copy-start | bytes 3076
  29.8 27.6 %all-to-all-start = ((bf16[16,104,256]{2,1,0:T(8,128)(2,1)}), bf16[16,104,256]{2,1,0:T(8,128)(2,1)S(1)}, u32[]{:S(2)}, u32[]{:S(2)}) async-start(bf16[16,104,256]{2,1,0:T(8,128)(2,1)} %pad_maximum_fusion), calls=%async_computation | async-start | bytes 1703936 | tf_op jit(solution)/shard_map/all_to_all | solution.py:143

commit v6 on v3

--- a/solution.py
+++ b/solution.py
@@ -14,14 +14,15 @@
 def normalize(values, frame_count, scaling, offsets):
     frames = values.shape[0]
     channels = values.shape[-1]
+    flat = values.reshape(frames, -1, channels)
+    live_mask = (jnp.arange(frames) < frame_count).astype(jnp.float32)[:, None]
+    members = frame_count.astype(jnp.float32) * flat.shape[1] * (channels // GROUPS)
+    first = jnp.sum(jnp.sum(flat, axis=1) * live_mask, axis=0)
+    second = jnp.sum(jnp.sum(flat * flat, axis=1) * live_mask, axis=0)
+    group_mean = jnp.sum(first.reshape(GROUPS, -1), axis=1) / members
+    spread = jnp.sum(second.reshape(GROUPS, -1), axis=1) / members - group_mean * group_mean
+    inverse = lax.rsqrt(spread + eps)
     grouped = values.reshape(frames, -1, GROUPS, channels // GROUPS)
-    live_mask = (jnp.arange(frames) < frame_count).astype(jnp.float32)[:, None, None, None]
-    members = frame_count.astype(jnp.float32) * grouped.shape[1] * grouped.shape[3]
-    group_mean = jnp.sum(grouped * live_mask, axis=(0, 1, 3)) / members
-    spread = (
-        jnp.sum(grouped * grouped * live_mask, axis=(0, 1, 3)) / members - group_mean * group_mean
-    )
-    inverse = lax.rsqrt(spread + eps)
     normed = (grouped - group_mean[:, None]) * inverse[:, None] * scaling.reshape(
         GROUPS, -1
     ) + offsets.reshape(GROUPS, -1)
@@ -59,28 +60,25 @@
     padded = jnp.pad(active, ((2, 0), (1, 1), (1, 1), (0, 0)))
     unfolded = jnp.concatenate(
         [
-            padded[:, row_tap : row_tap + frame_rows, col_tap : col_tap + columns]
+            padded[frame_lag : frame_lag + frames, row_tap : row_tap + frame_rows, col_tap : col_tap + columns]
+            for frame_lag in range(3)
             for row_tap in range(3)
             for col_tap in range(3)
         ],
         axis=-1,
-    ).reshape(frames + 2, frame_rows * columns, 9 * channels)
-    kernel = conv_weight.reshape(3, 9 * channels, -1)
-    conv = conv_bias + sum(
-        jnp.dot(
-            unfolded[frame_lag : frame_lag + frames].reshape(-1, 9 * channels),
-            kernel[frame_lag],
-            preferred_element_type=jnp.float32,
-        )
-        for frame_lag in range(3)
-    ).reshape(frames, frame_rows, columns, -1)
-    block_out = conv.astype(jnp.bfloat16)
+    ).reshape(frames * frame_rows * columns, 27 * channels)
+    conv = conv_bias + jnp.dot(
+        unfolded, conv_weight.reshape(27 * channels, -1), preferred_element_type=jnp.float32
+    )
+    block_out = conv.astype(jnp.bfloat16).reshape(frames, frame_rows, columns, channels)
     per_group = channels // GROUPS
-    grouped = block_out.astype(jnp.float32).reshape(frames, frame_rows * columns, GROUPS, per_group)
-    live_mask = (jnp.arange(frames) < own_count).astype(jnp.float32)[:, None, None, None]
+    value = block_out.astype(jnp.float32).reshape(frames, -1, channels)
+    live_mask = (jnp.arange(frames) < own_count).astype(jnp.float32)[:, None]
     members = own_count.astype(jnp.float32) * (frame_rows * columns * per_group)
-    first_sum = jnp.sum(grouped * live_mask, axis=(0, 1, 3))
-    second_sum = jnp.sum(grouped * grouped * live_mask, axis=(0, 1, 3))
+    frame_first = jnp.sum(value, axis=1)
+    frame_second = jnp.sum(value * value, axis=1)
+    first_sum = jnp.sum(jnp.sum(frame_first * live_mask, axis=0).reshape(GROUPS, per_group), axis=1)
+    second_sum = jnp.sum(jnp.sum(frame_second * live_mask, axis=0).reshape(GROUPS, per_group), axis=1)
     clip_mean = first_sum / members
     clip_spread = second_sum / members - clip_mean * clip_mean
     clip_inverse = lax.rsqrt(clip_spread + eps)
@@ -88,8 +86,8 @@
     tiles = block_out.reshape(frames, NRB, tile_rows, columns, channels)
     tiles = jnp.pad(tiles, ((0, per_dest * classes - frames), (0, 0), (0, 0), (0, 0), (0, 0)))
     tiles = tiles.reshape(per_dest, classes, NRB, tile_rows, columns, channels)
-    shift = own_start // NRB
-    pick = (jnp.arange(classes, dtype=jnp.int32) - shift) % classes
+    lag_of = (jnp.arange(classes, dtype=jnp.int32)[:, None] - (starts // NRB)[None, :] % classes) % classes
+    pick = jnp.sum(jnp.where(clip_order[None, :] == device, lag_of, 0), axis=1)
     tiles = jnp.take(tiles, pick, axis=1)
     tiles = jnp.transpose(tiles, (1, 2, 0, 3, 4, 5)).reshape(
         devices, per_dest * tile_rows * columns, channels

time: 57.7 us -> 90.9 us (1.58)
  other arithmetic: 8.96 us -> 31 us
  local copies, waits for them, and re-layouts: 10.4 us -> 25.3 us
  between operations: 4.23 us -> 1.71 us
  waiting for transfers between devices: 20.6 us -> 18.5 us
    reduce_sum x6 -> x10, other arithmetic: 3.48 us -> 9.75 us  [the longest x2 2.7 us: normalize(): second = jnp.sum(jnp.sum(flat * flat, axis=1) * live_mask, axis=0)]
    slice x2 -> x0, local copies, waits for them, and re-layouts: 3.95 us -> none  [the longest x1 2.21 us: local(): kernel[frame_lag]]
    reshape x0 -> x4, local copies, waits for them, and re-layouts: none -> 3.65 us  [the longest x1 1.38 us: normalize(): second.reshape(GROUPS, -1)]
    unnamed x18 -> x57, local copies, waits for them, and re-layouts: 2.63 us -> 5.31 us
    all_to_all x1, waiting for transfers between devices: 20.6 us -> 18.5 us  [local(): lax.all_to_all(outgoing, 'tile', split_axis=0, concat_axis=0, tiled=True)]
    gather x1, local copies, waits for them, and re-layouts: 0.6 us -> 2.6 us  [local(): tiles = jnp.take(tiles, pick, axis=1)]
    slice x1, local copies, waits for them, and re-layouts: 0.07 us -> 2.07 us  [local(): received[:, :per_dest * tile_rows * columns]]
    gather x1, local copies, waits for them, and re-layouts: 0.57 us -> 2.52 us  [local(): mine = jnp.take(block_part, take_from, axis=0)]
  transfers between devices with their start and end apart: 1 -> 1, of which waited for: 1 -> 1; matrix products, arithmetic and copies ran while one was open for 0% -> 3% of each run, Pallas kernels for 0% -> 0%
where the time goes in v6:
time: 90.9 us; the launch traced here: 89.8 us
  other arithmetic  31 us (34%)
  local copies, waits for them, and re-layouts  25.3 us (28%)
  waiting for transfers between devices  18.5 us (20%)
  matrix products  6.68 us (7%)
  starting transfers between devices  6.61 us (7%)
  between operations  1.71 us (2%)
    all_to_all x1, waiting for transfers between devices, local(): lax.all_to_all(outgoing, 'tile', split_axis=0, concat_axis=0, tiled=True)  18.5 us
    dot_general x1, matrix products, local(): jnp.dot(unfolded, conv_weight.reshape(27 * channels, -1), preferred_eleme...  6.68 us
    all_to_all x1, starting transfers between devices, local(): lax.all_to_all(outgoing, 'tile', split_axis=0, concat_axis=0, tiled=True)  6.61 us
    unnamed x57, local copies, waits for them, and re-layouts  5.31 us
    reduce_sum x2, other arithmetic, normalize(): second = jnp.sum(jnp.sum(flat * flat, axis=1) * live_mask, axis=0)  2.7 us
    gather x1, local copies, waits for them, and re-layouts, local(): tiles = jnp.take(tiles, pick, axis=1)  2.6 us
    gather x1, local copies, waits for them, and re-layouts, local(): mine = jnp.take(block_part, take_from, axis=0)  2.52 us
    concatenate x1, other arithmetic, local(): outgoing = jnp.concatenate([tiles, stat_rows], 1)  2.11 us
  transfers between devices with their start and end apart: 1, of which 1 were waited for; matrix products, arithmetic and copies ran while one was open for 3% of the time, Pallas kernels for 0%

profile of v6, /device:TPU:9, one launch (start us, length us, event | category | flops | bytes accessed | tf_op | source)
XLA Modules:
  0.0 89.8 jit_solution(12499279635574245924)
XLA Ops:
  0.6 1.4 %fusion.44 = s32[]{:T(128)} fusion(s32[16]{0:T(128)} %param.12, s32[]{:T(128)S(6)} %axis_index.12), kind=kLoop, calls=%fused_computation.144 | loop fusion | flops 47 | bytes 72 | tf_op jit(solution)/shard_map/reduce_sum | solution.py:55
  2.1 1.2 %compare_convert_fusion = f32[12]{0:T(128)} fusion(s32[]{:T(128)} %fusion.44), kind=kLoop, calls=%fused_computation.115 | loop fusion | flops 24 | bytes 52 | tf_op jit(solution)/shard_map/convert_element_type | solution.py:18
  4.5 0.9 select_reduce_fusion.2
  5.4 1.2 %broadcast_compare_fusion = pred[16]{0:T(512)(128)(4,1)} fusion(s32[16]{0:T(128)} %param.13, s32[]{:T(128)S(6)} %axis_index.12), kind=kLoop, calls=%fused_computation.158 | loop fusion | flops 16 | bytes 84 | tf_op jit(solution)/shard_map/eq | solution.py:90
  6.8 1.2 %and_select_fusion.3 = (s32[16]{0:T(128)S(1)}, s32[16]{0:T(128)}) fusion(s32[16]{0:T(128)S(1)} %reduce.2, s32[16]{0:T(128)} %copy-done.9), kind=kLoop, calls=%fused_computation.119 | loop fusion | flops 448 | bytes 256 | tf_op jit(solution)/shard_map/jit(remainder)/select_n | solution.py:89
  9.9 1.4 %fusion.11 = (f32[12,256]{1,0:T(8,128)S(1)}, f32[12,256]{1,0:T(8,128)S(1)}) fusion(bf16[12,16,8,256]{3,2,1,0:T(8,128)(2,1)} %param.11), kind=kLoop, calls=%fused_computation.47 | loop fusion | flops 1566720 | bytes 811008 | tf_op jit(solution)/shard_map/reduce_sum | solution.py:21
  11.3 1.3 %multiply_reduce_fusion.2 = (f32[256]{0:T(256)}, f32[256]{0:T(256)}) fusion(f32[12,256]{1,0:T(8,128)S(1)} %get-tuple-element.11, f32[12]{0:T(128)} %compare_convert_fusion, f32[12,256]{1,0:T(8,128)S(1)} %get-tuple-element.12), kind=kLoop, calls=%fused_computation.88 | loop fusion | flops 11776 | bytes 26672 | tf_op jit(solution)/shard_map/reduce_sum | solution.py:21
  13.4 1.4 %reshape.360 = f32[32,8]{1,0:T(8,128)} reshape(f32[256]{0:T(256)} %get-tuple-element.17) | data formatting | bytes 2048 | tf_op jit(solution)/shard_map/reshape | solution.py:23
  16.2 1.2 %add_rsqrt_fusion = (f32[32]{0:T(128)S(1)}, f32[32]{0:T(128)}) fusion(f32[32]{0:T(128)S(1)} %reduce_sum.177, f32[]{:T(128)S(6)} %mul.162, f32[32]{0:T(128)} %reduce_sum.174), kind=kLoop, calls=%fused_computation.154 | loop fusion | flops 160 | bytes 516 | tf_op jit(solution)/shard_map/rsqrt | solution.py:24
  19.5 1.8 %fusion.10 = bf16[12,16,8,256]{3,2,1,0:T(8,128)(2,1)S(1)} fusion(bf16[12,16,8,256]{3,2,1,0:T(8,128)(2,1)} %param.11, f32[256]{0:T(256)} %param.15, f32[256]{0:T(256)} %param.14, f32[256]{0:T(256)} %mul.167, f32[256]{0:T(256)} %sub.113), kind=kLoop, calls=%fused_computation.46 | loop fusion | flops 3932160 | bytes 1576960 | tf_op jit(solution)/shard_map/convert_element_type | solution.py:57
  27.6 6.7 %fusion = bf16[1536,256]{1,0:T(8,128)(2,1)} fusion(bf16[1536,6912]{1,0:T(8,128)(2,1)S(1)} %bitcast.48, bf16[6912,256]{1,0:T(8,128)(2,1)S(1)} %bitcast.43, f32[256]{0:T(256)S(1)} %copy-done.13), kind=kOutput, calls=%fused_computation.31 | convolution fusion | flops 5436604416 | bytes 25560064 | tf_op jit(solution)/shard_map/dot_general | solution.py:70
  34.2 2.6 %gather_fusion = bf16[2,6,8,2,8,256]{5,4,3,2,1,0:T(8,128)(2,1)} fusion(bf16[6,2,8,2,8,256]{5,4,3,2,1,0:T(8,128)(2,1)} %bitcast.44, s32[1024]{0:T(1024)S(1)} %get-tuple-element.34), kind=kCustom, calls=%fused_computation.2 | custom fusion | bytes 1572872 | tf_op jit(solution)/shard_map/jit(_take)/gather | solution.py:91
  36.9 1.3 %select_bitcast_fusion = bf16[2,8,6,2,8,256]{5,4,3,1,2,0:T(8,128)(2,1)S(1)} fusion(bf16[2,6,8,2,8,256]{5,4,3,2,1,0:T(8,128)(2,1)} %gather_fusion, pred[2]{0:T(512)(128)(4,1)S(1)} %copy-done.10), kind=kLoop, calls=%fused_computation.75 | loop fusion | flops 393216 | bytes 1572866 | tf_op jit(solution)/shard_map/jit(_take)/select_n | solution.py:91
  38.1 1.0 %copy.24 = bf16[2,8,6,2,8,256]{5,4,3,2,1,0:T(8,128)(2,1)} copy(bf16[2,8,6,2,8,256]{5,4,3,1,2,0:T(8,128)(2,1)S(1)} %select_bitcast_fusion) | data formatting | bytes 1572864 | tf_op jit(solution)/shard_map/jit(_take)/select_n | solution.py:91
  39.1 1.4 %convert_reduce_fusion.1 = (f32[12,256]{1,0:T(8,128)S(1)}, f32[12,256]{1,0:T(8,128)S(1)}) fusion(bf16[12,128,256]{2,1,0:T(8,128)(2,1)} %bitcast.45), kind=kLoop, calls=%fused_computation.36 | loop fusion | flops 1566720 | bytes 811008 | tf_op jit(solution)/shard_map/reduce_sum | solution.py:78
  47.1 2.1 %pad_maximum_fusion = bf16[16,104,256]{2,1,0:T(8,128)(2,1)} fusion(bf16[16,8,256]{2,1,0:T(8,128)(2,1)S(1)} %broadcast_in_dim.110, bf16[16,96,256]{2,1,0:T(8,128)(2,1)} %bitcast.46), kind=kLoop, calls=%fused_computation.48 | loop fusion | flops 1703936 | bytes 1703936 | tf_op jit(solution)/shard_map/concatenate | solution.py:101
  49.2 6.6 %all-to-all-start = ((bf16[16,104,256]{2,1,0:T(8,128)(2,1)}), bf16[16,104,256]{2,1,0:T(8,128)(2,1)}, u32[]{:S(2)}, u32[]{:S(2)}) async-start(bf16[16,104,256]{2,1,0:T(8,128)(2,1)} %pad_maximum_fusion), calls=%async_computation | async-start | bytes 1703936 | tf_op jit(solution)/shard_map/all_to_all | solution.py:102
  57.1 1.2 %compare_and_fusion.2 = (pred[32]{0:T(512)(128)(4,1)}, pred[32]{0:T(512)(128)(4,1)}) fusion(s32[32]{0:T(128)} %get-tuple-element.14, s32[32]{0:T(128)} %copy-done.4, s32[]{:T(128)S(6)} %axis_index.12), kind=kLoop, calls=%fused_computation.121 | loop fusion | flops 1504 | bytes 324 | tf_op jit(solution)/shard_map/jit(_take)/and | solution.py:117
  58.3 18.5 %all-to-all-done = bf16[16,104,256]{2,1,0:T(8,128)(2,1)} async-done(((bf16[16,104,256]{2,1,0:T(8,128)(2,1)}), bf16[16,104,256]{2,1,0:T(8,128)(2,1)}, u32[]{:S(2)}, u32[]{:S(2)}) %all-to-all-start) | async-done | bytes 852000 | tf_op jit(solution)/shard_map/all_to_all | solution.py:102
  78.3 2.0 %gather_fusion.3 = f32[32,256]{1,0:T(8,128)} fusion(f32[16,256]{1,0:T(8,128)} %get-tuple-element.26, s32[1024]{0:T(1024)} %get-tuple-element.33), kind=kCustom, calls=%fused_computation.1.clone | custom fusion | bytes 65664 | tf_op jit(solution)/shard_map/jit(_take)/gather | solution.py:119
  80.3 1.3 %gather_fusion.2 = f32[32,256]{1,0:T(8,128)} fusion(f32[16,256]{1,0:T(8,128)S(1)} %get-tuple-element.25, s32[1024]{0:T(1024)} %get-tuple-element.33), kind=kCustom, calls=%fused_computation.clone | custom fusion | bytes 65664 | tf_op jit(solution)/shard_map/jit(_take)/gather | solution.py:118
  81.6 2.1 %slice.137 = bf16[16,96,256]{2,1,0:T(8,128)(2,1)} slice(bf16[16,104,256]{2,1,0:T(8,128)(2,1)} %all-to-all-done), slice={[0:16], [0:96], [0:256]} | slice | bytes 1572864 | tf_op jit(solution)/shard_map/slice | solution.py:103
  83.7 2.5 %gather_fusion.1 = bf16[32,2,8,256]{3,2,1,0:T(8,128)(2,1)} fusion(bf16[96,2,8,256]{3,2,1,0:T(8,128)(2,1)} %bitcast.47, s32[1024]{0:T(1024)} %pad_clamp_fusion.1), kind=kCustom, calls=%fused_computation.3 | custom fusion | bytes 524416 | tf_op jit(solution)/shard_map/jit(_take)/gather | solution.py:117
  87.1 1.3 %multiply_convert_fusion = (bf16[2,32,8,256]{3,2,0,1:T(8,128)(2,1)S(1)}, bf16[2,32,8,256]{3,2,0,1:T(8,128)(2,1)S(1)}) fusion(f32[256]{0:T(256)} %param.19, f32[256]{0:T(256)} %param.18, f32[32,256]{1,0:T(8,128)S(1)} %get-tuple-element.32, f32[32,256]{1,0:T(8,128)S(1)} %get-tuple-element.31, bf16[32,2,8,256]{3,2,1,0:T(8,128)(2,1)} %gather_fusion.1, ...), kind=kLoop, calls=%fused_computation.76 | loop fusion | flops 1441792 | bytes 854048 | tf_op jit(solution)/shard_map/convert_element_type | solution.py:123
  (99 shorter events, 24.6 us)
Async XLA Ops:
  0.6 26.9 %copy-start = (bf16[3,3,3,256,256]{4,3,2,1,0:T(8,128)(2,1)S(1)}, bf16[3,3,3,256,256]{4,3,2,1,0:T(8,128)(2,1)}, u32[]{:S(2)}) copy-start(bf16[3,3,3,256,256]{4,3,2,1,0:T(8,128)(2,1)} %param.16) | copy-start | bytes 10616836
  5.4 1.2 %copy-start.9 = (s32[16]{0:T(128)}, s32[16]{0:T(128)S(1)}, u32[]{:S(2)}) copy-start(s32[16]{0:T(128)S(1)} %select_reduce_fusion.2) | copy-start | bytes 196
  19.5 4.9 %copy-start.1 = (bf16[12,16,8,256]{3,2,1,0:T(8,128)(2,1)S(1)}, bf16[12,16,8,256]{3,2,1,0:T(8,128)(2,1)}, u32[]{:S(2)}) copy-start(bf16[12,16,8,256]{3,2,1,0:T(8,128)(2,1)} %param.11) | copy-start | bytes 2359300
  19.5 4.9 %copy-start.2 = (f32[256]{0:T(256)S(1)}, f32[256]{0:T(256)}, u32[]{:S(2)}) copy-start(f32[256]{0:T(256)} %mul.167) | copy-start | bytes 3076
  19.5 4.9 %copy-start.3 = (f32[256]{0:T(256)S(1)}, f32[256]{0:T(256)}, u32[]{:S(2)}) copy-start(f32[256]{0:T(256)} %sub.113) | copy-start | bytes 3076
  19.5 5.0 %copy-start.5 = (f32[256]{0:T(256)S(1)}, f32[256]{0:T(256)}, u32[]{:S(2)}) copy-start(f32[256]{0:T(256)} %param.15) | copy-start | bytes 3076
  19.5 5.0 %copy-start.6 = (f32[256]{0:T(256)S(1)}, f32[256]{0:T(256)}, u32[]{:S(2)}) copy-start(f32[256]{0:T(256)} %param.14) | copy-start | bytes 3076
  21.3 4.4 %copy-start.8 = (s32[16]{0:T(128)S(1)}, s32[16]{0:T(128)}, u32[]{:S(2)}) copy-start(s32[16]{0:T(128)} %get-tuple-element.22) | copy-start | bytes 196
  21.3 4.4 %copy-start.14 = (s32[32]{0:T(128)S(1)}, s32[32]{0:T(128)}, u32[]{:S(2)}) copy-start(s32[32]{0:T(128)} %multiply_add_fusion) | copy-start | bytes 388
  21.3 4.5 %copy-start.11 = (s32[16]{0:T(128)S(1)}, s32[16]{0:T(128)}, u32[]{:S(2)}) copy-start(s32[16]{0:T(128)} %param.13) | copy-start | bytes 196
  21.3 5.6 %copy-start.12 = (s32[2]{0:T(128)S(1)}, s32[2]{0:T(128)}, u32[]{:S(2)}) copy-start(s32[2]{0:T(128)} %fusion.46) | copy-start | bytes 28
  21.4 6.2 %copy-start.13 = (f32[256]{0:T(256)S(1)}, f32[256]{0:T(256)}, u32[]{:S(2)}) copy-start(f32[256]{0:T(256)} %param.17) | copy-start | bytes 3076
  25.7 11.2 %copy-start.10 = (pred[2]{0:T(512)(128)(4,1)S(1)}, pred[2]{0:T(512)(128)(4,1)}, u32[]{:S(2)}) copy-start(pred[2]{0:T(512)(128)(4,1)} %compare_and_fusion.1) | copy-start | bytes 10
  26.5 0.5 copy-start.4
  27.6 12.9 %copy-start.7 = (f32[12]{0:T(128)S(1)}, f32[12]{0:T(128)}, u32[]{:S(2)}) copy-start(f32[12]{0:T(128)} %compare_convert_fusion) | copy-start | bytes 148
  49.2 27.6 %all-to-all-start = ((bf16[16,104,256]{2,1,0:T(8,128)(2,1)}), bf16[16,104,256]{2,1,0:T(8,128)(2,1)}, u32[]{:S(2)}, u32[]{:S(2)}) async-start(bf16[16,104,256]{2,1,0:T(8,128)(2,1)} %pad_maximum_fusion), calls=%async_computation | async-start | bytes 1703936 | tf_op jit(solution)/shard_map/all_to_all | solution.py:102

commit v7 on v3

--- a/solution.py
+++ b/solution.py
@@ -14,14 +14,15 @@
 def normalize(values, frame_count, scaling, offsets):
     frames = values.shape[0]
     channels = values.shape[-1]
+    flat = values.reshape(frames, -1, channels)
+    live_mask = (jnp.arange(frames) < frame_count).astype(jnp.float32)[:, None]
+    members = frame_count.astype(jnp.float32) * flat.shape[1] * (channels // GROUPS)
+    first = jnp.sum(jnp.sum(flat, axis=1) * live_mask, axis=0)
+    second = jnp.sum(jnp.sum(flat * flat, axis=1) * live_mask, axis=0)
+    group_mean = jnp.sum(first.reshape(GROUPS, -1), axis=1) / members
+    spread = jnp.sum(second.reshape(GROUPS, -1), axis=1) / members - group_mean * group_mean
+    inverse = lax.rsqrt(spread + eps)
     grouped = values.reshape(frames, -1, GROUPS, channels // GROUPS)
-    live_mask = (jnp.arange(frames) < frame_count).astype(jnp.float32)[:, None, None, None]
-    members = frame_count.astype(jnp.float32) * grouped.shape[1] * grouped.shape[3]
-    group_mean = jnp.sum(grouped * live_mask, axis=(0, 1, 3)) / members
-    spread = (
-        jnp.sum(grouped * grouped * live_mask, axis=(0, 1, 3)) / members - group_mean * group_mean
-    )
-    inverse = lax.rsqrt(spread + eps)
     normed = (grouped - group_mean[:, None]) * inverse[:, None] * scaling.reshape(
         GROUPS, -1
     ) + offsets.reshape(GROUPS, -1)
@@ -50,7 +51,6 @@
     chosen = clip_order[:, None] == positions[None, :]
     ordered = jnp.sum(jnp.where(chosen, frame_counts[None, :], 0), axis=1)
     starts = (jnp.cumsum(ordered) - ordered) * NRB
-    own_start = jnp.sum(jnp.where(clip_order == device, starts, 0))
     own_count = jnp.sum(jnp.where(positions == device, frame_counts, 0))
 
     active = normalize(latents.astype(jnp.float32), own_count, norm_scale, norm_offset).astype(
@@ -88,8 +88,8 @@
     tiles = block_out.reshape(frames, NRB, tile_rows, columns, channels)
     tiles = jnp.pad(tiles, ((0, per_dest * classes - frames), (0, 0), (0, 0), (0, 0), (0, 0)))
     tiles = tiles.reshape(per_dest, classes, NRB, tile_rows, columns, channels)
-    shift = own_start // NRB
-    pick = (jnp.arange(classes, dtype=jnp.int32) - shift) % classes
+    lag_of = (jnp.arange(classes, dtype=jnp.int32)[:, None] - (starts // NRB)[None, :] % classes) % classes
+    pick = jnp.sum(jnp.where(clip_order[None, :] == device, lag_of, 0), axis=1)
     tiles = jnp.take(tiles, pick, axis=1)
     tiles = jnp.transpose(tiles, (1, 2, 0, 3, 4, 5)).reshape(
         devices, per_dest * tile_rows * columns, channels

time: 57.7 us -> 56.1 us (0.972)
  between operations: 4.23 us -> 1.62 us
    eq x0 -> x1, other arithmetic: none -> 0.66 us  [local(): pick = jnp.sum(jnp.where(clip_order[None, :] == device, lag_of, 0), axis=1)]
    reduce_sum x4 -> x6, other arithmetic: 3.23 us -> 3.13 us  [the longest x2 1.47 us: normalize(): second = jnp.sum(jnp.sum(flat * flat, axis=1) * live_mask, axis=0)]
where the time goes in v7:
time: 56.1 us; the launch traced here: 55.8 us
  waiting for transfers between devices  20.8 us (37%)
  local copies, waits for them, and re-layouts  10.7 us (19%)
  other arithmetic  9.52 us (17%)
  starting transfers between devices  6.61 us (12%)
  matrix products  6.58 us (12%)
  between operations  1.62 us (3%)
    all_to_all x1, waiting for transfers between devices, local(): lax.all_to_all(outgoing, 'tile', split_axis=0, concat_axis=0, tiled=True)  20.8 us
    all_to_all x1, starting transfers between devices, local(): lax.all_to_all(outgoing, 'tile', split_axis=0, concat_axis=0, tiled=True)  6.61 us
    dot_general x3, matrix products, local(): jnp.dot(unfolded[frame_lag:frame_lag + frames].reshape(-1, 9 * channels),...  6.58 us
    unnamed x18, local copies, waits for them, and re-layouts  2.94 us
    slice x1, local copies, waits for them, and re-layouts, local(): kernel[frame_lag]  2.21 us
    slice x1, local copies, waits for them, and re-layouts, local(): unfolded[frame_lag:frame_lag + frames].reshape(-1, 9 * channels)  1.74 us
    convert_element_type x1, other arithmetic, local(): normalize(latents.astype(jnp.float32), own_count, norm_scale, norm_offset)  1.7 us
    reduce_sum x2, other arithmetic, normalize(): second = jnp.sum(jnp.sum(flat * flat, axis=1) * live_mask, axis=0)  1.47 us
  transfers between devices with their start and end apart: 1, of which 1 were waited for; matrix products, arithmetic and copies ran while one was open for 0% of the time, Pallas kernels for 0%

profile of v7, /device:TPU:9, one launch (start us, length us, event | category | flops | bytes accessed | tf_op | source)
XLA Modules:
  0.0 55.8 jit_solution(9878207534947356673)
XLA Ops:
  0.6 1.3 %fusion.28 = s32[]{:T(128)} fusion(s32[16]{0:T(128)} %param.12, s32[]{:T(128)S(6)} %axis_index.12), kind=kLoop, calls=%fused_computation.112 | loop fusion | flops 47 | bytes 72 | tf_op jit(solution)/shard_map/reduce_sum | solution.py:54
  1.9 0.6 %compare_convert_fusion = f32[12]{0:T(128)S(1)} fusion(s32[]{:T(128)} %fusion.28), kind=kLoop, calls=%fused_computation.83 | loop fusion | flops 24 | bytes 52 | tf_op jit(solution)/shard_map/convert_element_type | solution.py:18
  3.2 0.9 %select_reduce_fusion.2 = s32[16]{0:T(128)S(1)} fusion(s32[16]{0:T(128)} %param.12, s32[16]{0:T(128)} %param.13), kind=kLoop, calls=%fused_computation.61 | loop fusion | flops 752 | bytes 192 | tf_op jit(solution)/shard_map/reduce_sum | solution.py:52
  4.1 0.7 %broadcast_compare_fusion = pred[16]{0:T(512)(128)(4,1)S(1)} fusion(s32[16]{0:T(128)} %param.13, s32[]{:T(128)S(6)} %axis_index.12), kind=kLoop, calls=%fused_computation.126 | loop fusion | flops 16 | bytes 84 | tf_op jit(solution)/shard_map/eq | solution.py:92
  5.2 1.4 %fusion.12 = (f32[12,256]{1,0:T(8,128)S(1)}, f32[12,256]{1,0:T(8,128)S(1)}) fusion(bf16[12,16,8,256]{3,2,1,0:T(8,128)(2,1)} %param.11), kind=kLoop, calls=%fused_computation.32 | loop fusion | flops 1566720 | bytes 811008 | tf_op jit(solution)/shard_map/reduce_sum | solution.py:21
  7.5 1.7 %fusion.11 = bf16[12,16,8,256]{3,2,1,0:T(8,128)(2,1)S(1)} fusion(bf16[12,16,8,256]{3,2,1,0:T(8,128)(2,1)} %param.11, f32[256]{0:T(256)} %param.15, f32[256]{0:T(256)} %param.14, f32[256]{0:T(256)S(1)} %mul.176, f32[256]{0:T(256)S(1)} %sub.113), kind=kLoop, calls=%fused_computation.31 | loop fusion | flops 3932160 | bytes 1576960 | tf_op jit(solution)/shard_map/convert_element_type | solution.py:56
  9.7 0.2 fusion.16
  10.6 1.7 %fusion.34 = (bf16[12,16,8,2304]{3,2,1,0:T(8,128)(2,1)S(1)}, bf16[12,16,8,2304]{3,2,1,0:T(8,128)(2,1)S(1)}, bf16[12,16,8,2304]{3,2,1,0:T(8,128)(2,1)S(1)}) fusion(bf16[14,16,8,2304]{3,2,1,0:T(8,128)(2,1)S(1)} %fusion.21), kind=kLoop, calls=%fused_computation.128 | loop fusion | bytes 42467328 | tf_op jit(solution)/shard_map/slice | solution.py:71
  12.4 2.2 %fusion.35 = (bf16[1,3,3,256,256]{4,3,2,1,0:T(8,128)(2,1)S(1)}, bf16[1,3,3,256,256]{4,3,2,1,0:T(8,128)(2,1)S(1)}, bf16[1,3,3,256,256]{4,3,2,1,0:T(8,128)(2,1)S(1)}) fusion(bf16[3,3,3,256,256]{4,3,2,1,0:T(8,128)(2,1)} %param.16), kind=kLoop, calls=%fused_computation.129 | loop fusion | bytes 7077888 | tf_op jit(solution)/shard_map/slice | solution.py:72
  14.6 2.1 %fusion.36 = f32[1536,256]{1,0:T(8,128)S(1)} fusion(bf16[1536,2304]{1,0:T(8,128)(2,1)S(1)} %bitcast.53, bf16[2304,256]{1,0:T(8,128)(2,1)S(1)} %bitcast.59), kind=kOutput, calls=%fused_computation.130 | convolution fusion | flops 1811939328 | bytes 9830400 | tf_op jit(solution)/shard_map/dot_general | solution.py:70
  16.7 2.2 %convolution_add_fusion.1 = f32[1536,256]{1,0:T(8,128)S(1)} fusion(f32[1536,256]{1,0:T(8,128)S(1)} %fusion.36, bf16[1536,2304]{1,0:T(8,128)(2,1)S(1)} %bitcast.52, bf16[2304,256]{1,0:T(8,128)(2,1)S(1)} %bitcast.58), kind=kOutput, calls=%fused_computation.14 | convolution fusion | flops 1812332544 | bytes 11403264 | tf_op jit(solution)/shard_map/dot_general | solution.py:70
  18.9 2.3 %fusion = (f32[256]{0:T(256)S(1)}, f32[256]{0:T(256)S(1)}, f32[1536,256]{1,0:T(8,128)S(1)}) fusion(f32[1536]{0:T(1024)S(1)} %broadcast_bitcast_fusion, f32[256]{0:T(256)S(1)} %copy-done, f32[1536,256]{1,0:T(8,128)S(1)} %convolution_add_fusion.1, bf16[1536,2304]{1,0:T(8,128)(2,1)S(1)} %bitcast.51, bf16[2304,256]{1,0:T(8,128)(2,1)S(1)} %bitcast.57), kind=kOutput, calls=%fused_computation.20 | convolution fusion | flops 1815477760 | bytes 11412480 | tf_op jit(solution)/shard_map/dot_general | solution.py:70
  21.2 0.2 add_convert_fusion.1
  21.5 0.3 copy-done.3
  22.0 0.6 %gather_fusion = bf16[2,6,8,2,8,256]{5,4,3,2,1,0:T(8,128)(2,1)S(1)} fusion(bf16[6,2,8,2,8,256]{5,4,3,2,1,0:T(8,128)(2,1)S(1)} %add_convert_fusion.1, s32[1024]{0:T(1024)S(1)} %get-tuple-element.39), kind=kCustom, calls=%fused_computation.2 | custom fusion | bytes 1572872 | tf_op jit(solution)/shard_map/jit(_take)/gather | solution.py:93
  23.6 1.0 %pad_maximum_fusion = bf16[16,104,256]{2,1,0:T(8,128)(2,1)} fusion(bf16[16,8,256]{2,1,0:T(8,128)(2,1)S(1)} %broadcast_in_dim.110, bf16[16,96,256]{2,1,0:T(8,128)(2,1)S(1)} %bitcast.54), kind=kLoop, calls=%fused_computation.44 | loop fusion | flops 1703936 | bytes 1703936 | tf_op jit(solution)/shard_map/concatenate | solution.py:103
  24.6 6.6 %all-to-all-start = ((bf16[16,104,256]{2,1,0:T(8,128)(2,1)}), bf16[16,104,256]{2,1,0:T(8,128)(2,1)S(1)}, u32[]{:S(2)}, u32[]{:S(2)}) async-start(bf16[16,104,256]{2,1,0:T(8,128)(2,1)} %pad_maximum_fusion), calls=%async_computation | async-start | bytes 1703936 | tf_op jit(solution)/shard_map/all_to_all | solution.py:104
  31.3 20.8 %all-to-all-done = bf16[16,104,256]{2,1,0:T(8,128)(2,1)S(1)} async-done(((bf16[16,104,256]{2,1,0:T(8,128)(2,1)}), bf16[16,104,256]{2,1,0:T(8,128)(2,1)S(1)}, u32[]{:S(2)}, u32[]{:S(2)}) %all-to-all-start) | async-done | bytes 852000 | tf_op jit(solution)/shard_map/all_to_all | solution.py:104
  52.1 0.6 %gather_fusion.3 = f32[32,256]{1,0:T(8,128)S(1)} fusion(f32[16,256]{1,0:T(8,128)S(1)} %get-tuple-element.30, s32[1024]{0:T(1024)S(1)} %get-tuple-element.38), kind=kCustom, calls=%fused_computation.1.clone | custom fusion | bytes 65664 | tf_op jit(solution)/shard_map/jit(_take)/gather | solution.py:121
  52.7 0.6 %gather_fusion.2 = f32[32,256]{1,0:T(8,128)S(1)} fusion(f32[16,256]{1,0:T(8,128)S(1)} %get-tuple-element.29, s32[1024]{0:T(1024)S(1)} %get-tuple-element.38), kind=kCustom, calls=%fused_computation.clone | custom fusion | bytes 65664 | tf_op jit(solution)/shard_map/jit(_take)/gather | solution.py:120
  53.4 0.6 %gather_fusion.1 = bf16[32,2,8,256]{3,2,1,0:T(8,128)(2,1)S(1)} fusion(bf16[96,2,8,256]{3,2,1,0:T(8,128)(2,1)S(1)} %bitcast.56, s32[1024]{0:T(1024)S(1)} %pad_clamp_fusion.1), kind=kCustom, calls=%fused_computation.3 | custom fusion | bytes 524416 | tf_op jit(solution)/shard_map/jit(_take)/gather | solution.py:119
  54.0 0.3 multiply_convert_fusion
  54.3 0.7 %copy.26 = bf16[2,32,8,256]{3,2,1,0:T(8,128)(2,1)} copy(bf16[2,32,8,256]{3,2,0,1:T(8,128)(2,1)S(1)} %get-tuple-element.18) | data formatting | bytes 524288
  55.1 0.7 %copy.27 = bf16[2,32,8,256]{3,2,1,0:T(8,128)(2,1)} copy(bf16[2,32,8,256]{3,2,0,1:T(8,128)(2,1)S(1)} %get-tuple-element.17) | data formatting | bytes 524288
  (63 shorter events, 3.9 us)
Async XLA Ops:
  16.7 2.2 %copy-start = (f32[256]{0:T(256)S(1)}, f32[256]{0:T(256)}, u32[]{:S(2)}) copy-start(f32[256]{0:T(256)} %param.17) | copy-start | bytes 3076
  21.2 0.7 %copy-start.3 = (s32[16]{0:T(128)S(1)}, s32[16]{0:T(128)}, u32[]{:S(2)}) copy-start(s32[16]{0:T(128)} %param.13) | copy-start | bytes 196
  24.6 27.5 %all-to-all-start = ((bf16[16,104,256]{2,1,0:T(8,128)(2,1)}), bf16[16,104,256]{2,1,0:T(8,128)(2,1)S(1)}, u32[]{:S(2)}, u32[]{:S(2)}) async-start(bf16[16,104,256]{2,1,0:T(8,128)(2,1)} %pad_maximum_fusion), calls=%async_computation | async-start | bytes 1703936 | tf_op jit(solution)/shard_map/all_to_all | solution.py:104
  31.2 22.9 %copy-start.1 = (f32[256]{0:T(256)S(1)}, f32[256]{0:T(256)}, u32[]{:S(2)}) copy-start(f32[256]{0:T(256)} %param.19) | copy-start | bytes 3076
  31.2 22.9 %copy-start.2 = (f32[256]{0:T(256)S(1)}, f32[256]{0:T(256)}, u32[]{:S(2)}) copy-start(f32[256]{0:T(256)} %param.18) | copy-start | bytes 3076

commit v8 on v7

--- a/solution.py
+++ b/solution.py
@@ -66,14 +66,16 @@
         axis=-1,
     ).reshape(frames + 2, frame_rows * columns, 9 * channels)
     kernel = conv_weight.reshape(3, 9 * channels, -1)
+    spread_out = [
+        jnp.dot(
+            unfolded.reshape(-1, 9 * channels), kernel[frame_lag], preferred_element_type=jnp.float32
+        ).reshape(frames + 2, frame_rows * columns, -1)
+        for frame_lag in range(3)
+    ]
     conv = conv_bias + sum(
-        jnp.dot(
-            unfolded[frame_lag : frame_lag + frames].reshape(-1, 9 * channels),
-            kernel[frame_lag],
-            preferred_element_type=jnp.float32,
-        )
-        for frame_lag in range(3)
-    ).reshape(frames, frame_rows, columns, -1)
+        spread_out[frame_lag][frame_lag : frame_lag + frames] for frame_lag in range(3)
+    )
+    conv = conv.reshape(frames, frame_rows, columns, -1)
     block_out = conv.astype(jnp.bfloat16)
     per_group = channels // GROUPS
     grouped = block_out.astype(jnp.float32).reshape(frames, frame_rows * columns, GROUPS, per_group)
@@ -91,8 +93,8 @@
     lag_of = (jnp.arange(classes, dtype=jnp.int32)[:, None] - (starts // NRB)[None, :] % classes) % classes
     pick = jnp.sum(jnp.where(clip_order[None, :] == device, lag_of, 0), axis=1)
     tiles = jnp.take(tiles, pick, axis=1)
-    tiles = jnp.transpose(tiles, (1, 2, 0, 3, 4, 5)).reshape(
-        devices, per_dest * tile_rows * columns, channels
+    tiles = jnp.transpose(tiles, (1, 2, 3, 0, 4, 5)).reshape(
+        devices, tile_rows * per_dest * columns, channels
     )
     stats = jnp.stack([clip_mean, clip_inverse], 0)
     stats = jnp.repeat(stats, per_group, axis=1)
@@ -103,11 +105,15 @@
     outgoing = jnp.concatenate([tiles, stat_rows], 1)
     received = lax.all_to_all(outgoing, "tile", split_axis=0, concat_axis=0, tiled=True)
     block_part = received[:, : per_dest * tile_rows * columns].reshape(
-        devices * per_dest, tile_rows, columns, channels
+        devices, tile_rows, per_dest, columns, channels
     )
     stat_part = received[:, per_dest * tile_rows * columns :].astype(jnp.float32)
     src_mean = stat_part[:, 0] + stat_part[:, 2]
     src_inverse = stat_part[:, 1] + stat_part[:, 3]
+    normed_part = (block_part.astype(jnp.float32) - src_mean[:, None, None, None, :]) * src_inverse[
+        :, None, None, None, :
+    ] * out_scale + out_offset
+    normed_part = jax.nn.silu(normed_part).astype(jnp.bfloat16)
 
     local_slot = jnp.arange(worker_tiles, dtype=jnp.int32)
     tile_id = local_slot * devices + device
@@ -115,15 +121,12 @@
     at_place = placed[:, None] == positions[None, :]
     clip_id = jnp.sum(jnp.where(at_place, clip_order[None, :], 0), axis=1)
     within = tile_id - jnp.sum(jnp.where(at_place, starts[None, :], 0), axis=1)
-    take_from = clip_id * per_dest + within // NRB // classes
-    mine = jnp.take(block_part, take_from, axis=0)
-    tile_mean = jnp.take(src_mean, clip_id, axis=0)
-    tile_inverse = jnp.take(src_inverse, clip_id, axis=0)
-    normed = (mine.astype(jnp.float32) - tile_mean[:, None, None, :]) * tile_inverse[
-        :, None, None, :
-    ] * out_scale + out_offset
-    normed = jax.nn.silu(normed).astype(jnp.bfloat16)
-    return (jnp.transpose(mine, (1, 0, 2, 3)), jnp.transpose(normed, (1, 0, 2, 3)))
+    row_of = jnp.arange(tile_rows, dtype=jnp.int32)[:, None]
+    take_from = (clip_id[None, :] * tile_rows + row_of) * per_dest + (within // NRB // classes)[None, :]
+    rows_all = devices * tile_rows * per_dest
+    block_mine = jnp.take(block_part.reshape(rows_all, columns, channels), take_from, axis=0)
+    normed_mine = jnp.take(normed_part.reshape(rows_all, columns, channels), take_from, axis=0)
+    return (block_mine, normed_mine)
 
 
 def solution(mesh):

time: 56.1 us -> 52.3 us (0.932)
  local copies, waits for them, and re-layouts: 10.7 us -> 6.44 us
  other arithmetic: 9.52 us -> 10.3 us
    slice x1, local copies, waits for them, and re-layouts: 2.21 us -> 0.34 us  [local(): kernel[frame_lag]]
    slice x2 -> x0, local copies, waits for them, and re-layouts: 1.74 us -> none  [the longest x1 1.74 us: local(): unfolded[frame_lag:frame_lag + frames].reshape(-1, 9 * channels)]
    select_n x3, other arithmetic: 0.11 us -> 0.96 us  [the longest x1 0.93 us: local(): jnp.take(normed_part.reshape(rows_all, columns, channels), take_from, axi...]
    gather x3 -> x2, local copies, waits for them, and re-layouts: 1.77 us -> 1.19 us  [the longest x1 0.6 us: local(): jnp.take(block_part.reshape(rows_all, columns, channels), take_from, axis=0)]
    unnamed x18 -> x21, local copies, waits for them, and re-layouts: 2.94 us -> 2.74 us
  transfers between devices with their start and end apart: 1 -> 1, of which waited for: 1 -> 1; matrix products, arithmetic and copies ran while one was open for 0% -> 1% of each run, Pallas kernels for 0% -> 0%
where the time goes in v8:
time: 52.3 us; the launch traced here: 52 us
  waiting for transfers between devices  20.5 us (39%)
  other arithmetic  10.3 us (20%)
  starting transfers between devices  6.61 us (13%)
  local copies, waits for them, and re-layouts  6.44 us (12%)
  matrix products  6.42 us (12%)
  between operations  1.68 us (3%)
    all_to_all x1, waiting for transfers between devices, local(): lax.all_to_all(outgoing, 'tile', split_axis=0, concat_axis=0, tiled=True)  20.5 us
    all_to_all x1, starting transfers between devices, local(): lax.all_to_all(outgoing, 'tile', split_axis=0, concat_axis=0, tiled=True)  6.61 us
    dot_general x3, matrix products, local(): jnp.dot(unfolded.reshape(-1, 9 * channels), kernel[frame_lag], preferred_...  6.42 us
    unnamed x21, local copies, waits for them, and re-layouts  2.74 us
    reduce_sum x2, other arithmetic, normalize(): second = jnp.sum(jnp.sum(flat * flat, axis=1) * live_mask, axis=0)  1.47 us
    reduce_sum x1, other arithmetic, local(): own_count = jnp.sum(jnp.where(positions == device, frame_counts, 0))  1.37 us
    convert_element_type x1, other arithmetic, local(): normalize(latents.astype(jnp.float32), own_count, norm_scale, norm_offset)  1.24 us
  transfers between devices with their start and end apart: 1, of which 1 were waited for; matrix products, arithmetic and copies ran while one was open for 1% of the time, Pallas kernels for 0%

profile of v8, /device:TPU:9, one launch (start us, length us, event | category | flops | bytes accessed | tf_op | source)
XLA Modules:
  0.0 52.0 jit_solution(3732808716280061939)
XLA Ops:
  0.6 1.4 %fusion.38 = s32[]{:T(128)} fusion(s32[16]{0:T(128)} %param.12, s32[]{:T(128)S(6)} %axis_index.12), kind=kLoop, calls=%fused_computation.104 | loop fusion | flops 47 | bytes 72 | tf_op jit(solution)/shard_map/reduce_sum | solution.py:54
  2.0 0.6 %compare_convert_fusion = f32[12]{0:T(128)S(1)} fusion(s32[]{:T(128)} %fusion.38), kind=kLoop, calls=%fused_computation.84 | loop fusion | flops 24 | bytes 52 | tf_op jit(solution)/shard_map/convert_element_type | solution.py:18
  3.3 0.9 %select_reduce_fusion.2 = s32[16]{0:T(128)S(1)} fusion(s32[16]{0:T(128)} %param.12, s32[16]{0:T(128)} %param.13), kind=kLoop, calls=%fused_computation.65 | loop fusion | flops 752 | bytes 192 | tf_op jit(solution)/shard_map/reduce_sum | solution.py:52
  4.2 0.7 %broadcast_compare_fusion = pred[16]{0:T(512)(128)(4,1)S(1)} fusion(s32[16]{0:T(128)} %param.13, s32[]{:T(128)S(6)} %axis_index.12), kind=kLoop, calls=%fused_computation.117 | loop fusion | flops 16 | bytes 84 | tf_op jit(solution)/shard_map/eq | solution.py:94
  5.2 1.4 %fusion.24 = (f32[12,256]{1,0:T(8,128)S(1)}, f32[12,256]{1,0:T(8,128)S(1)}) fusion(bf16[12,16,8,256]{3,2,1,0:T(8,128)(2,1)} %param.11), kind=kLoop, calls=%fused_computation.37 | loop fusion | flops 1566720 | bytes 811008 | tf_op jit(solution)/shard_map/reduce_sum | solution.py:21
  7.6 1.2 %fusion.23 = bf16[12,16,8,256]{3,2,1,0:T(8,128)(2,1)S(1)} fusion(bf16[12,16,8,256]{3,2,1,0:T(8,128)(2,1)S(1)} %copy-done.1, f32[256]{0:T(256)} %param.15, f32[256]{0:T(256)} %param.14, f32[256]{0:T(256)S(1)} %mul.167, f32[256]{0:T(256)S(1)} %sub.102), kind=kLoop, calls=%fused_computation.36 | loop fusion | flops 3932160 | bytes 1576960 | tf_op jit(solution)/shard_map/convert_element_type | solution.py:56
  8.8 0.2 fusion.25
  9.3 0.2 fusion.28
  9.6 0.2 fusion.30
  9.8 0.2 fusion.31
  10.3 1.5 %copy-done = bf16[3,3,3,256,256]{4,3,2,1,0:T(8,128)(2,1)S(1)} copy-done((bf16[3,3,3,256,256]{4,3,2,1,0:T(8,128)(2,1)S(1)}, bf16[3,3,3,256,256]{4,3,2,1,0:T(8,128)(2,1)}, u32[]{:S(2)}) %copy-start) | copy-done | bytes 3538968
  11.8 0.3 fusion.43
  12.1 2.1 %fusion.2 = f32[1536,256]{1,0:T(8,128)S(1)} fusion(bf16[2304,256]{1,0:T(8,128)(2,1)S(1)} %bitcast.41, bf16[1792,2304]{1,0:T(8,128)(2,1)S(1)} %bitcast.44), kind=kOutput, calls=%fused_computation.5 | convolution fusion | flops 1811939328 | bytes 9830400 | tf_op jit(solution)/shard_map/dot_general | solution.py:70
  14.2 2.1 %fusion.6 = f32[1536,256]{1,0:T(8,128)S(1)} fusion(f32[1536,256]{1,0:T(8,128)S(1)} %fusion.2, bf16[2304,256]{1,0:T(8,128)(2,1)S(1)} %bitcast.40, bf16[1792,2304]{1,0:T(8,128)(2,1)S(1)} %bitcast.45), kind=kOutput, calls=%fused_computation.18 | convolution fusion | flops 1812332544 | bytes 11403264 | tf_op jit(solution)/shard_map/dot_general | solution.py:70
  16.3 2.3 %fusion.12 = (f32[256]{0:T(256)S(1)}, f32[256]{0:T(256)S(1)}, f32[1536,256]{1,0:T(8,128)S(1)}) fusion(f32[1536]{0:T(1024)S(1)} %broadcast_bitcast_fusion, f32[256]{0:T(256)S(1)} %copy-done.2, f32[1536,256]{1,0:T(8,128)S(1)} %fusion.6, bf16[2304,256]{1,0:T(8,128)(2,1)S(1)} %bitcast.39, bf16[1792,2304]{1,0:T(8,128)(2,1)S(1)} %bitcast.46), kind=kOutput, calls=%fused_computation.25 | convolution fusion | flops 1815477760 | bytes 11414528 | tf_op jit(solution)/shard_map/dot_general | solution.py:70
  18.6 0.2 add_convert_fusion.1
  18.8 0.6 %gather_fusion = bf16[2,6,8,2,8,256]{5,4,3,2,1,0:T(8,128)(2,1)S(1)} fusion(bf16[6,2,8,2,8,256]{5,4,3,2,1,0:T(8,128)(2,1)S(1)} %add_convert_fusion.1, s32[1024]{0:T(1024)S(1)} %pad_clamp_fusion.1), kind=kCustom, calls=%fused_computation.2 | custom fusion | bytes 1572872 | tf_op jit(solution)/shard_map/jit(_take)/gather | solution.py:95
  20.5 1.0 %pad_maximum_fusion = bf16[16,104,256]{2,1,0:T(8,128)(2,1)} fusion(bf16[16,8,256]{2,1,0:T(8,128)(2,1)S(1)} %broadcast_in_dim.100, bf16[16,96,256]{2,1,0:T(8,128)(2,1)S(1)} %bitcast.37), kind=kLoop, calls=%fused_computation.50 | loop fusion | flops 1703936 | bytes 1703936 | tf_op jit(solution)/shard_map/concatenate | solution.py:105
  21.5 6.6 %all-to-all-start = ((bf16[16,104,256]{2,1,0:T(8,128)(2,1)}), bf16[16,104,256]{2,1,0:T(8,128)(2,1)S(1)}, u32[]{:S(2)}, u32[]{:S(2)}) async-start(bf16[16,104,256]{2,1,0:T(8,128)(2,1)} %pad_maximum_fusion), calls=%async_computation | async-start | bytes 1703936 | tf_op jit(solution)/shard_map/all_to_all | solution.py:106
  28.4 20.5 %all-to-all-done = bf16[16,104,256]{2,1,0:T(8,128)(2,1)S(1)} async-done(((bf16[16,104,256]{2,1,0:T(8,128)(2,1)}), bf16[16,104,256]{2,1,0:T(8,128)(2,1)S(1)}, u32[]{:S(2)}, u32[]{:S(2)}) %all-to-all-start) | async-done | bytes 852000 | tf_op jit(solution)/shard_map/all_to_all | solution.py:106
  49.2 0.6 %gather_fusion.1 = bf16[64,8,256]{2,1,0:T(8,128)(2,1)S(1)} fusion(bf16[192,8,256]{2,1,0:T(8,128)(2,1)S(1)} %bitcast.35, s32[1024]{0:T(1024)S(1)} %pad_clamp_fusion), kind=kCustom, calls=%fused_computation.clone | custom fusion | bytes 524544 | tf_op jit(solution)/shard_map/jit(_take)/gather | solution.py:127
  49.9 0.5 %multiply_convert_fusion = bf16[192,8,256]{2,1,0:T(8,128)(2,1)S(1)} fusion(bf16[192,8,256]{2,1,0:T(8,128)(2,1)S(1)} %bitcast.36, f32[256]{0:T(256)S(1)} %copy-done.3, f32[256]{0:T(256)S(1)} %copy-done.4, f32[192,256]{1,0:T(8,128)S(1)} %mul.187, f32[192,256]{1,0:T(8,128)S(1)} %sub.113), kind=kLoop, calls=%fused_computation.38 | loop fusion | flops 3932160 | bytes 1968128 | tf_op jit(solution)/shard_map/convert_element_type | solution.py:116
  50.4 0.6 %gather_fusion.2 = bf16[64,8,256]{2,1,0:T(8,128)(2,1)S(1)} fusion(bf16[192,8,256]{2,1,0:T(8,128)(2,1)S(1)} %multiply_convert_fusion, s32[1024]{0:T(1024)S(1)} %pad_clamp_fusion), kind=kCustom, calls=%fused_computation.1.clone | custom fusion | bytes 524544 | tf_op jit(solution)/shard_map/jit(_take)/gather | solution.py:128
  51.0 0.9 %broadcast_select_fusion = (bf16[2,32,8,256]{3,2,1,0:T(8,128)(2,1)}, bf16[2,32,8,256]{3,2,1,0:T(8,128)(2,1)}) fusion(bf16[2,32,8,256]{3,2,1,0:T(8,128)(2,1)S(1)} %bitcast.43, pred[2,32]{1,0:T(4,128)(4,1)S(1)} %compare_and_fusion, bf16[2,32,8,256]{3,2,1,0:T(8,128)(2,1)S(1)} %bitcast.42), kind=kLoop, calls=%fused_computation.52 | loop fusion | flops 262144 | bytes 1048640 | tf_op jit(solution)/shard_map/jit(_take)/select_n | solution.py:128
  (68 shorter events, 3.5 us)
Async XLA Ops:
  0.6 6.9 %copy-start.1 = (bf16[12,16,8,256]{3,2,1,0:T(8,128)(2,1)S(1)}, bf16[12,16,8,256]{3,2,1,0:T(8,128)(2,1)}, u32[]{:S(2)}) copy-start(bf16[12,16,8,256]{3,2,1,0:T(8,128)(2,1)} %param.11) | copy-start | bytes 2359300
  9.8 2.0 %copy-start = (bf16[3,3,3,256,256]{4,3,2,1,0:T(8,128)(2,1)S(1)}, bf16[3,3,3,256,256]{4,3,2,1,0:T(8,128)(2,1)}, u32[]{:S(2)}) copy-start(bf16[3,3,3,256,256]{4,3,2,1,0:T(8,128)(2,1)} %param.16) | copy-start | bytes 10616836
  14.2 2.1 %copy-start.2 = (f32[256]{0:T(256)S(1)}, f32[256]{0:T(256)}, u32[]{:S(2)}) copy-start(f32[256]{0:T(256)} %param.17) | copy-start | bytes 3076
  20.5 7.7 %copy-start.5 = (s32[16]{0:T(128)S(1)}, s32[16]{0:T(128)}, u32[]{:S(2)}) copy-start(s32[16]{0:T(128)} %param.13) | copy-start | bytes 196
  21.5 27.5 %all-to-all-start = ((bf16[16,104,256]{2,1,0:T(8,128)(2,1)}), bf16[16,104,256]{2,1,0:T(8,128)(2,1)S(1)}, u32[]{:S(2)}, u32[]{:S(2)}) async-start(bf16[16,104,256]{2,1,0:T(8,128)(2,1)} %pad_maximum_fusion), calls=%async_computation | async-start | bytes 1703936 | tf_op jit(solution)/shard_map/all_to_all | solution.py:106
  49.0 0.8 %copy-start.3 = (f32[256]{0:T(256)S(1)}, f32[256]{0:T(256)}, u32[]{:S(2)}) copy-start(f32[256]{0:T(256)} %param.19) | copy-start | bytes 3076
  49.1 0.8 %copy-start.4 = (f32[256]{0:T(256)S(1)}, f32[256]{0:T(256)}, u32[]{:S(2)}) copy-start(f32[256]{0:T(256)} %param.18) | copy-start | bytes 3076

commit v9 on v8

--- a/solution.py
+++ b/solution.py
@@ -47,6 +47,8 @@
     classes = devices // NRB
     per_dest = (frames + classes - 1) // classes
     worker_tiles = MEANF * NRB
+    meta = lax.optimization_barrier(jnp.stack([frame_counts, clip_order], 0))
+    frame_counts, clip_order = meta[0], meta[1]
     positions = jnp.arange(frame_counts.shape[0], dtype=jnp.int32)
     chosen = clip_order[:, None] == positions[None, :]
     ordered = jnp.sum(jnp.where(chosen, frame_counts[None, :], 0), axis=1)

time: 52.3 us -> 51 us (0.975)
  other arithmetic: 10.3 us -> 8.95 us
    another operation x3 -> x4, other arithmetic: 0.16 us -> 0.91 us  [the longest x1 0.75 us: local(): meta = lax.optimization_barrier(jnp.stack([frame_counts, clip_order], 0))]
    reduce_sum x1, other arithmetic: 1.37 us -> 0.63 us  [local(): own_count = jnp.sum(jnp.where(positions == device, frame_counts, 0))]
    reduce_sum x1, other arithmetic: 0.85 us -> 0.18 us  [local(): ordered = jnp.sum(jnp.where(chosen, frame_counts[None, :], 0), axis=1)]
    eq x1 -> x0, other arithmetic: 0.66 us -> none  [local(): pick = jnp.sum(jnp.where(clip_order[None, :] == device, lag_of, 0), axis=1)]
    unnamed x21 -> x19, local copies, waits for them, and re-layouts: 2.74 us -> 2.74 us
where the time goes in v9:
time: 51 us; the launch traced here: 50.7 us
  waiting for transfers between devices  20.5 us (40%)
  other arithmetic  8.95 us (18%)
  starting transfers between devices  6.61 us (13%)
  local copies, waits for them, and re-layouts  6.45 us (13%)
  matrix products  6.42 us (13%)
  between operations  1.7 us (3%)
    all_to_all x1, waiting for transfers between devices, local(): lax.all_to_all(outgoing, 'tile', split_axis=0, concat_axis=0, tiled=True)  20.5 us
    all_to_all x1, starting transfers between devices, local(): lax.all_to_all(outgoing, 'tile', split_axis=0, concat_axis=0, tiled=True)  6.61 us
    dot_general x3, matrix products, local(): jnp.dot(unfolded.reshape(-1, 9 * channels), kernel[frame_lag], preferred_...  6.42 us
    unnamed x19, local copies, waits for them, and re-layouts  2.74 us
    reduce_sum x2, other arithmetic, normalize(): second = jnp.sum(jnp.sum(flat * flat, axis=1) * live_mask, axis=0)  1.47 us
    convert_element_type x1, other arithmetic, local(): normalize(latents.astype(jnp.float32), own_count, norm_scale, norm_offset)  1.24 us
  transfers between devices with their start and end apart: 1, of which 1 were waited for; matrix products, arithmetic and copies ran while one was open for 1% of the time, Pallas kernels for 0%

profile of v9, /device:TPU:9, one launch (start us, length us, event | category | flops | bytes accessed | tf_op | source)
XLA Modules:
  0.0 50.7 jit_solution(9530653956107888499)
XLA Ops:
  0.6 0.8 %pad_add_fusion = s32[2,16]{1,0:T(2,128)S(1)} fusion(s32[1,16]{1,0:T(1,128)} %bitcast.58, s32[1,16]{1,0:T(1,128)} %bitcast.59), kind=kLoop, calls=%fused_computation.102 | loop fusion | flops 32 | bytes 256 | tf_op jit(solution)/shard_map/stack | solution.py:50
  1.4 0.6 %fusion.38 = s32[]{:T(128)} fusion(s32[]{:T(128)S(6)} %axis_index.12, s32[2,16]{1,0:T(2,128)S(1)} %pad_add_fusion), kind=kLoop, calls=%fused_computation.106 | loop fusion | flops 47 | bytes 72 | tf_op jit(solution)/shard_map/reduce_sum | solution.py:56
  2.0 0.6 %compare_convert_fusion = f32[12]{0:T(128)S(1)} fusion(s32[]{:T(128)} %fusion.38), kind=kLoop, calls=%fused_computation.84 | loop fusion | flops 24 | bytes 52 | tf_op jit(solution)/shard_map/convert_element_type | solution.py:18
  4.0 1.4 %fusion.24 = (f32[12,256]{1,0:T(8,128)S(1)}, f32[12,256]{1,0:T(8,128)S(1)}) fusion(bf16[12,16,8,256]{3,2,1,0:T(8,128)(2,1)} %param.11), kind=kLoop, calls=%fused_computation.37 | loop fusion | flops 1566720 | bytes 811008 | tf_op jit(solution)/shard_map/reduce_sum | solution.py:21
  6.3 1.2 %fusion.23 = bf16[12,16,8,256]{3,2,1,0:T(8,128)(2,1)S(1)} fusion(bf16[12,16,8,256]{3,2,1,0:T(8,128)(2,1)S(1)} %copy-done.1, f32[256]{0:T(256)} %param.15, f32[256]{0:T(256)} %param.14, f32[256]{0:T(256)S(1)} %mul.167, f32[256]{0:T(256)S(1)} %sub.102), kind=kLoop, calls=%fused_computation.36 | loop fusion | flops 3932160 | bytes 1576960 | tf_op jit(solution)/shard_map/convert_element_type | solution.py:58
  7.5 0.2 fusion.25
  7.8 0.2 fusion.27
  8.0 0.2 fusion.28
  8.3 0.2 fusion.30
  8.8 0.2 fusion.33
  9.0 1.5 %copy-done = bf16[3,3,3,256,256]{4,3,2,1,0:T(8,128)(2,1)S(1)} copy-done((bf16[3,3,3,256,256]{4,3,2,1,0:T(8,128)(2,1)S(1)}, bf16[3,3,3,256,256]{4,3,2,1,0:T(8,128)(2,1)}, u32[]{:S(2)}) %copy-start) | copy-done | bytes 3538968
  10.5 0.3 fusion.43
  10.8 2.1 %fusion.2 = f32[1536,256]{1,0:T(8,128)S(1)} fusion(bf16[2304,256]{1,0:T(8,128)(2,1)S(1)} %bitcast.51, bf16[1792,2304]{1,0:T(8,128)(2,1)S(1)} %bitcast.54), kind=kOutput, calls=%fused_computation.5 | convolution fusion | flops 1811939328 | bytes 9830400 | tf_op jit(solution)/shard_map/dot_general | solution.py:72
  12.9 2.1 %fusion.6 = f32[1536,256]{1,0:T(8,128)S(1)} fusion(f32[1536,256]{1,0:T(8,128)S(1)} %fusion.2, bf16[2304,256]{1,0:T(8,128)(2,1)S(1)} %bitcast.50, bf16[1792,2304]{1,0:T(8,128)(2,1)S(1)} %bitcast.55), kind=kOutput, calls=%fused_computation.18 | convolution fusion | flops 1812332544 | bytes 11403264 | tf_op jit(solution)/shard_map/dot_general | solution.py:72
  15.0 2.3 %fusion.12 = (f32[256]{0:T(256)S(1)}, f32[256]{0:T(256)S(1)}, f32[1536,256]{1,0:T(8,128)S(1)}) fusion(f32[1536]{0:T(1024)S(1)} %broadcast_bitcast_fusion, f32[256]{0:T(256)S(1)} %copy-done.2, f32[1536,256]{1,0:T(8,128)S(1)} %fusion.6, bf16[2304,256]{1,0:T(8,128)(2,1)S(1)} %bitcast.49, bf16[1792,2304]{1,0:T(8,128)(2,1)S(1)} %bitcast.56), kind=kOutput, calls=%fused_computation.25 | convolution fusion | flops 1815477760 | bytes 11414528 | tf_op jit(solution)/shard_map/dot_general | solution.py:72
  17.3 0.2 add_convert_fusion.1
  17.6 0.6 %gather_fusion = bf16[2,6,8,2,8,256]{5,4,3,2,1,0:T(8,128)(2,1)S(1)} fusion(bf16[6,2,8,2,8,256]{5,4,3,2,1,0:T(8,128)(2,1)S(1)} %add_convert_fusion.1, s32[1024]{0:T(1024)S(1)} %pad_clamp_fusion.1), kind=kCustom, calls=%fused_computation.2 | custom fusion | bytes 1572872 | tf_op jit(solution)/shard_map/jit(_take)/gather | solution.py:97
  19.2 1.0 %pad_maximum_fusion = bf16[16,104,256]{2,1,0:T(8,128)(2,1)} fusion(bf16[16,8,256]{2,1,0:T(8,128)(2,1)S(1)} %broadcast_in_dim.102, bf16[16,96,256]{2,1,0:T(8,128)(2,1)S(1)} %bitcast.47), kind=kLoop, calls=%fused_computation.50 | loop fusion | flops 1703936 | bytes 1703936 | tf_op jit(solution)/shard_map/concatenate | solution.py:107
  20.2 6.6 %all-to-all-start = ((bf16[16,104,256]{2,1,0:T(8,128)(2,1)}), bf16[16,104,256]{2,1,0:T(8,128)(2,1)S(1)}, u32[]{:S(2)}, u32[]{:S(2)}) async-start(bf16[16,104,256]{2,1,0:T(8,128)(2,1)} %pad_maximum_fusion), calls=%async_computation | async-start | bytes 1703936 | tf_op jit(solution)/shard_map/all_to_all | solution.py:108
  27.1 20.5 %all-to-all-done = bf16[16,104,256]{2,1,0:T(8,128)(2,1)S(1)} async-done(((bf16[16,104,256]{2,1,0:T(8,128)(2,1)}), bf16[16,104,256]{2,1,0:T(8,128)(2,1)S(1)}, u32[]{:S(2)}, u32[]{:S(2)}) %all-to-all-start) | async-done | bytes 852000 | tf_op jit(solution)/shard_map/all_to_all | solution.py:108
  48.0 0.6 %gather_fusion.1 = bf16[64,8,256]{2,1,0:T(8,128)(2,1)S(1)} fusion(bf16[192,8,256]{2,1,0:T(8,128)(2,1)S(1)} %bitcast.45, s32[1024]{0:T(1024)S(1)} %pad_clamp_fusion), kind=kCustom, calls=%fused_computation.clone | custom fusion | bytes 524544 | tf_op jit(solution)/shard_map/jit(_take)/gather | solution.py:129
  48.6 0.5 %multiply_convert_fusion = bf16[192,8,256]{2,1,0:T(8,128)(2,1)S(1)} fusion(bf16[192,8,256]{2,1,0:T(8,128)(2,1)S(1)} %bitcast.46, f32[256]{0:T(256)S(1)} %copy-done.3, f32[256]{0:T(256)S(1)} %copy-done.4, f32[192,256]{1,0:T(8,128)S(1)} %mul.187, f32[192,256]{1,0:T(8,128)S(1)} %sub.113), kind=kLoop, calls=%fused_computation.38 | loop fusion | flops 3932160 | bytes 1968128 | tf_op jit(solution)/shard_map/convert_element_type | solution.py:118
  49.1 0.6 %gather_fusion.2 = bf16[64,8,256]{2,1,0:T(8,128)(2,1)S(1)} fusion(bf16[192,8,256]{2,1,0:T(8,128)(2,1)S(1)} %multiply_convert_fusion, s32[1024]{0:T(1024)S(1)} %pad_clamp_fusion), kind=kCustom, calls=%fused_computation.1.clone | custom fusion | bytes 524544 | tf_op jit(solution)/shard_map/jit(_take)/gather | solution.py:130
  49.7 0.9 %broadcast_select_fusion = (bf16[2,32,8,256]{3,2,1,0:T(8,128)(2,1)}, bf16[2,32,8,256]{3,2,1,0:T(8,128)(2,1)}) fusion(bf16[2,32,8,256]{3,2,1,0:T(8,128)(2,1)S(1)} %bitcast.53, pred[2,32]{1,0:T(4,128)(4,1)S(1)} %compare_and_fusion, bf16[2,32,8,256]{3,2,1,0:T(8,128)(2,1)S(1)} %bitcast.52), kind=kLoop, calls=%fused_computation.52 | loop fusion | flops 262144 | bytes 1048640 | tf_op jit(solution)/shard_map/jit(_take)/select_n | solution.py:130
  (68 shorter events, 3.5 us)
Async XLA Ops:
  0.6 5.6 %copy-start.1 = (bf16[12,16,8,256]{3,2,1,0:T(8,128)(2,1)S(1)}, bf16[12,16,8,256]{3,2,1,0:T(8,128)(2,1)}, u32[]{:S(2)}) copy-start(bf16[12,16,8,256]{3,2,1,0:T(8,128)(2,1)} %param.11) | copy-start | bytes 2359300
  8.5 2.0 %copy-start = (bf16[3,3,3,256,256]{4,3,2,1,0:T(8,128)(2,1)S(1)}, bf16[3,3,3,256,256]{4,3,2,1,0:T(8,128)(2,1)}, u32[]{:S(2)}) copy-start(bf16[3,3,3,256,256]{4,3,2,1,0:T(8,128)(2,1)} %param.16) | copy-start | bytes 10616836
  12.9 2.1 %copy-start.2 = (f32[256]{0:T(256)S(1)}, f32[256]{0:T(256)}, u32[]{:S(2)}) copy-start(f32[256]{0:T(256)} %param.17) | copy-start | bytes 3076
  20.2 27.5 %all-to-all-start = ((bf16[16,104,256]{2,1,0:T(8,128)(2,1)}), bf16[16,104,256]{2,1,0:T(8,128)(2,1)S(1)}, u32[]{:S(2)}, u32[]{:S(2)}) async-start(bf16[16,104,256]{2,1,0:T(8,128)(2,1)} %pad_maximum_fusion), calls=%async_computation | async-start | bytes 1703936 | tf_op jit(solution)/shard_map/all_to_all | solution.py:108
  47.8 0.8 %copy-start.3 = (f32[256]{0:T(256)S(1)}, f32[256]{0:T(256)}, u32[]{:S(2)}) copy-start(f32[256]{0:T(256)} %param.19) | copy-start | bytes 3076
  47.8 0.8 %copy-start.4 = (f32[256]{0:T(256)S(1)}, f32[256]{0:T(256)}, u32[]{:S(2)}) copy-start(f32[256]{0:T(256)} %param.18) | copy-start | bytes 3076

commit v10 on v9

--- a/solution.py
+++ b/solution.py
@@ -94,7 +94,7 @@
     tiles = tiles.reshape(per_dest, classes, NRB, tile_rows, columns, channels)
     lag_of = (jnp.arange(classes, dtype=jnp.int32)[:, None] - (starts // NRB)[None, :] % classes) % classes
     pick = jnp.sum(jnp.where(clip_order[None, :] == device, lag_of, 0), axis=1)
-    tiles = jnp.take(tiles, pick, axis=1)
+    tiles = jnp.take(tiles, pick, axis=1, mode="clip")
     tiles = jnp.transpose(tiles, (1, 2, 3, 0, 4, 5)).reshape(
         devices, tile_rows * per_dest * columns, channels
     )
@@ -126,8 +126,8 @@
     row_of = jnp.arange(tile_rows, dtype=jnp.int32)[:, None]
     take_from = (clip_id[None, :] * tile_rows + row_of) * per_dest + (within // NRB // classes)[None, :]
     rows_all = devices * tile_rows * per_dest
-    block_mine = jnp.take(block_part.reshape(rows_all, columns, channels), take_from, axis=0)
-    normed_mine = jnp.take(normed_part.reshape(rows_all, columns, channels), take_from, axis=0)
+    block_mine = jnp.take(block_part.reshape(rows_all, columns, channels), take_from, axis=0, mode="clip")
+    normed_mine = jnp.take(normed_part.reshape(rows_all, columns, channels), take_from, axis=0, mode="clip")
     return (block_mine, normed_mine)
 
 

time: 51 us -> 51.3 us (level)
  local copies, waits for them, and re-layouts: 6.45 us -> 7.85 us
  other arithmetic: 8.95 us -> 7.86 us
    select_n x4 -> x0, other arithmetic: 1.08 us -> none  [the longest x1 0.93 us: local(): jnp.take(normed_part.reshape(rows_all, columns, channels), take_from, axi...]
    gather x2, local copies, waits for them, and re-layouts: 1.19 us -> 1.9 us  [the longest x1 1.3 us: local(): jnp.take(block_part.reshape(rows_all, columns, channels), take_from, axis...]
    gather x1, local copies, waits for them, and re-layouts: 0.6 us -> 1.3 us  [local(): jnp.take(normed_part.reshape(rows_all, columns, channels), take_from, axi...]
where the time goes in v10:
time: 51.3 us; the launch traced here: 50.9 us
  waiting for transfers between devices  20.6 us (40%)
  other arithmetic  7.86 us (15%)
  local copies, waits for them, and re-layouts  7.85 us (15%)
  starting transfers between devices  6.61 us (13%)
  matrix products  6.42 us (13%)
  between operations  1.65 us (3%)
    all_to_all x1, waiting for transfers between devices, local(): lax.all_to_all(outgoing, 'tile', split_axis=0, concat_axis=0, tiled=True)  20.6 us
    all_to_all x1, starting transfers between devices, local(): lax.all_to_all(outgoing, 'tile', split_axis=0, concat_axis=0, tiled=True)  6.61 us
    dot_general x3, matrix products, local(): jnp.dot(unfolded.reshape(-1, 9 * channels), kernel[frame_lag], preferred_...  6.42 us
    unnamed x19, local copies, waits for them, and re-layouts  2.74 us
    reduce_sum x2, other arithmetic, normalize(): second = jnp.sum(jnp.sum(flat * flat, axis=1) * live_mask, axis=0)  1.47 us
    gather x1, local copies, waits for them, and re-layouts, local(): jnp.take(block_part.reshape(rows_all, columns, channels), take_from, axis...  1.3 us
    gather x1, local copies, waits for them, and re-layouts, local(): jnp.take(normed_part.reshape(rows_all, columns, channels), take_from, axi...  1.3 us
    convert_element_type x1, other arithmetic, local(): normalize(latents.astype(jnp.float32), own_count, norm_scale, norm_offset)  1.24 us
  transfers between devices with their start and end apart: 1, of which 1 were waited for; matrix products, arithmetic and copies ran while one was open for 1% of the time, Pallas kernels for 0%

profile of v10, /device:TPU:9, one launch (start us, length us, event | category | flops | bytes accessed | tf_op | source)
XLA Modules:
  0.0 50.9 jit_solution(733535648448775255)
XLA Ops:
  0.6 0.8 %pad_add_fusion = s32[2,16]{1,0:T(2,128)S(1)} fusion(s32[1,16]{1,0:T(1,128)} %bitcast.56, s32[1,16]{1,0:T(1,128)} %bitcast.57), kind=kLoop, calls=%fused_computation.94 | loop fusion | flops 32 | bytes 256 | tf_op jit(solution)/shard_map/stack | solution.py:50
  1.4 0.6 %fusion.38 = s32[]{:T(128)} fusion(s32[]{:T(128)S(6)} %axis_index.12, s32[2,16]{1,0:T(2,128)S(1)} %pad_add_fusion), kind=kLoop, calls=%fused_computation.99 | loop fusion | flops 47 | bytes 72 | tf_op jit(solution)/shard_map/reduce_sum | solution.py:56
  2.0 0.6 %compare_convert_fusion = f32[12]{0:T(128)S(1)} fusion(s32[]{:T(128)} %fusion.38), kind=kLoop, calls=%fused_computation.81 | loop fusion | flops 24 | bytes 52 | tf_op jit(solution)/shard_map/convert_element_type | solution.py:18
  3.4 1.4 %fusion.24 = (f32[12,256]{1,0:T(8,128)S(1)}, f32[12,256]{1,0:T(8,128)S(1)}) fusion(bf16[12,16,8,256]{3,2,1,0:T(8,128)(2,1)} %param.9), kind=kLoop, calls=%fused_computation.37 | loop fusion | flops 1566720 | bytes 811008 | tf_op jit(solution)/shard_map/reduce_sum | solution.py:21
  5.7 1.2 %fusion.23 = bf16[12,16,8,256]{3,2,1,0:T(8,128)(2,1)S(1)} fusion(bf16[12,16,8,256]{3,2,1,0:T(8,128)(2,1)S(1)} %copy-done.1, f32[256]{0:T(256)} %param.13, f32[256]{0:T(256)} %param.12, f32[256]{0:T(256)S(1)} %mul.173, f32[256]{0:T(256)S(1)} %sub.97), kind=kLoop, calls=%fused_computation.36 | loop fusion | flops 3932160 | bytes 1576960 | tf_op jit(solution)/shard_map/convert_element_type | solution.py:58
  6.9 0.2 fusion.25
  7.2 0.2 fusion.27
  7.4 0.2 fusion.28
  7.7 0.2 fusion.30
  7.9 0.2 fusion.31
  8.2 0.2 fusion.33
  8.4 1.5 %copy-done = bf16[3,3,3,256,256]{4,3,2,1,0:T(8,128)(2,1)S(1)} copy-done((bf16[3,3,3,256,256]{4,3,2,1,0:T(8,128)(2,1)S(1)}, bf16[3,3,3,256,256]{4,3,2,1,0:T(8,128)(2,1)}, u32[]{:S(2)}) %copy-start) | copy-done | bytes 3538968
  9.9 0.3 fusion.42
  10.2 2.1 %fusion.2 = f32[1536,256]{1,0:T(8,128)S(1)} fusion(bf16[2304,256]{1,0:T(8,128)(2,1)S(1)} %bitcast.49, bf16[1792,2304]{1,0:T(8,128)(2,1)S(1)} %bitcast.52), kind=kOutput, calls=%fused_computation.5 | convolution fusion | flops 1811939328 | bytes 9830400 | tf_op jit(solution)/shard_map/dot_general | solution.py:72
  12.3 2.1 %fusion.6 = f32[1536,256]{1,0:T(8,128)S(1)} fusion(f32[1536,256]{1,0:T(8,128)S(1)} %fusion.2, bf16[2304,256]{1,0:T(8,128)(2,1)S(1)} %bitcast.48, bf16[1792,2304]{1,0:T(8,128)(2,1)S(1)} %bitcast.53), kind=kOutput, calls=%fused_computation.18 | convolution fusion | flops 1812332544 | bytes 11403264 | tf_op jit(solution)/shard_map/dot_general | solution.py:72
  14.5 2.3 %fusion.12 = (f32[256]{0:T(256)S(1)}, f32[256]{0:T(256)S(1)}, f32[1536,256]{1,0:T(8,128)S(1)}) fusion(f32[1536]{0:T(1024)S(1)} %broadcast_bitcast_fusion, f32[256]{0:T(256)S(1)} %copy-done.2, f32[1536,256]{1,0:T(8,128)S(1)} %fusion.6, bf16[2304,256]{1,0:T(8,128)(2,1)S(1)} %bitcast.47, bf16[1792,2304]{1,0:T(8,128)(2,1)S(1)} %bitcast.54), kind=kOutput, calls=%fused_computation.25 | convolution fusion | flops 1815477760 | bytes 11414528 | tf_op jit(solution)/shard_map/dot_general | solution.py:72
  16.7 0.2 add_convert_fusion.1
  17.5 0.6 %gather_fusion = bf16[2,6,8,2,8,256]{5,4,3,2,1,0:T(8,128)(2,1)S(1)} fusion(bf16[6,2,8,2,8,256]{5,4,3,2,1,0:T(8,128)(2,1)S(1)} %add_convert_fusion.1, s32[1024]{0:T(1024)S(1)} %pad_clamp_fusion.1), kind=kCustom, calls=%fused_computation | custom fusion | bytes 1572872 | tf_op jit(solution)/shard_map/jit(_take)/gather | solution.py:97
  19.0 1.0 %pad_maximum_fusion = bf16[16,104,256]{2,1,0:T(8,128)(2,1)} fusion(bf16[16,8,256]{2,1,0:T(8,128)(2,1)S(1)} %broadcast_in_dim.89, bf16[16,96,256]{2,1,0:T(8,128)(2,1)S(1)} %bitcast.45), kind=kLoop, calls=%fused_computation.50 | loop fusion | flops 1703936 | bytes 1703936 | tf_op jit(solution)/shard_map/concatenate | solution.py:107
  20.0 6.6 %all-to-all-start = ((bf16[16,104,256]{2,1,0:T(8,128)(2,1)}), bf16[16,104,256]{2,1,0:T(8,128)(2,1)S(1)}, u32[]{:S(2)}, u32[]{:S(2)}) async-start(bf16[16,104,256]{2,1,0:T(8,128)(2,1)} %pad_maximum_fusion), calls=%async_computation | async-start | bytes 1703936 | tf_op jit(solution)/shard_map/all_to_all | solution.py:108
  26.9 20.6 %all-to-all-done = bf16[16,104,256]{2,1,0:T(8,128)(2,1)S(1)} async-done(((bf16[16,104,256]{2,1,0:T(8,128)(2,1)}), bf16[16,104,256]{2,1,0:T(8,128)(2,1)S(1)}, u32[]{:S(2)}, u32[]{:S(2)}) %all-to-all-start) | async-done | bytes 852000 | tf_op jit(solution)/shard_map/all_to_all | solution.py:108
  47.8 1.3 %gather_fusion.1 = bf16[64,8,256]{2,1,0:T(8,128)(2,1)} fusion(bf16[192,8,256]{2,1,0:T(8,128)(2,1)S(1)} %bitcast.42, s32[1024]{0:T(1024)S(1)} %pad_clamp_fusion), kind=kCustom, calls=%fused_computation.1 | custom fusion | bytes 524544 | tf_op jit(solution)/shard_map/jit(_take)/gather | solution.py:129
  49.1 0.5 %multiply_convert_fusion = bf16[192,8,256]{2,1,0:T(8,128)(2,1)S(1)} fusion(bf16[192,8,256]{2,1,0:T(8,128)(2,1)S(1)} %bitcast.43, f32[256]{0:T(256)S(1)} %copy-done.3, f32[256]{0:T(256)S(1)} %copy-done.4, f32[192,256]{1,0:T(8,128)S(1)} %mul.194, f32[192,256]{1,0:T(8,128)S(1)} %sub.113), kind=kLoop, calls=%fused_computation.38 | loop fusion | flops 3932160 | bytes 1968128 | tf_op jit(solution)/shard_map/convert_element_type | solution.py:118
  49.6 1.3 %gather_fusion.2 = bf16[64,8,256]{2,1,0:T(8,128)(2,1)} fusion(bf16[192,8,256]{2,1,0:T(8,128)(2,1)S(1)} %multiply_convert_fusion, s32[1024]{0:T(1024)S(1)} %pad_clamp_fusion), kind=kCustom, calls=%fused_computation.2 | custom fusion | bytes 524544 | tf_op jit(solution)/shard_map/jit(_take)/gather | solution.py:130
  (63 shorter events, 3.1 us)
Async XLA Ops:
  0.6 5.0 %copy-start.1 = (bf16[12,16,8,256]{3,2,1,0:T(8,128)(2,1)S(1)}, bf16[12,16,8,256]{3,2,1,0:T(8,128)(2,1)}, u32[]{:S(2)}) copy-start(bf16[12,16,8,256]{3,2,1,0:T(8,128)(2,1)} %param.9) | copy-start | bytes 2359300
  7.9 2.0 %copy-start = (bf16[3,3,3,256,256]{4,3,2,1,0:T(8,128)(2,1)S(1)}, bf16[3,3,3,256,256]{4,3,2,1,0:T(8,128)(2,1)}, u32[]{:S(2)}) copy-start(bf16[3,3,3,256,256]{4,3,2,1,0:T(8,128)(2,1)} %param.14) | copy-start | bytes 10616836
  12.3 2.1 %copy-start.2 = (f32[256]{0:T(256)S(1)}, f32[256]{0:T(256)}, u32[]{:S(2)}) copy-start(f32[256]{0:T(256)} %param.15) | copy-start | bytes 3076
  20.0 27.5 %all-to-all-start = ((bf16[16,104,256]{2,1,0:T(8,128)(2,1)}), bf16[16,104,256]{2,1,0:T(8,128)(2,1)S(1)}, u32[]{:S(2)}, u32[]{:S(2)}) async-start(bf16[16,104,256]{2,1,0:T(8,128)(2,1)} %pad_maximum_fusion), calls=%async_computation | async-start | bytes 1703936 | tf_op jit(solution)/shard_map/all_to_all | solution.py:108
  47.6 1.5 %copy-start.3 = (f32[256]{0:T(256)S(1)}, f32[256]{0:T(256)}, u32[]{:S(2)}) copy-start(f32[256]{0:T(256)} %param.17) | copy-start | bytes 3076
  47.6 1.5 %copy-start.4 = (f32[256]{0:T(256)S(1)}, f32[256]{0:T(256)}, u32[]{:S(2)}) copy-start(f32[256]{0:T(256)} %param.16) | copy-start | bytes 3076

commit v11 on v10

--- a/solution.py
+++ b/solution.py
@@ -1,6 +1,10 @@
+import functools
+
 import jax
 import jax.numpy as jnp
 from jax import lax
+from jax.experimental import pallas as pl
+from jax.experimental.pallas import tpu as pltpu
 from jax.sharding import PartitionSpec as P
 
 GROUPS = 32
@@ -27,6 +31,75 @@
         GROUPS, -1
     ) + offsets.reshape(GROUPS, -1)
     return jax.nn.silu(normed).reshape(values.shape)
+
+
+def conv_body(act_ref, w_hbm, b_ref, o_ref, s1_ref, s2_ref, w_vmem, unfolded, sems, *, frame_rows, columns):
+    positions = frame_rows * columns
+    rows, channels = act_ref.shape
+    frames = rows // positions
+    copies = [pltpu.make_async_copy(w_hbm.at[lag], w_vmem.at[lag], sems.at[lag]) for lag in range(3)]
+    for copy in copies:
+        copy.start()
+    values = act_ref[...].astype(jnp.float32)
+    flat = lax.broadcasted_iota(jnp.int32, (rows, channels), 0)
+    column = flat % columns
+    row = (flat // columns) % frame_rows
+    unfolded[0 : 2 * positions, :] = jnp.zeros((2 * positions, 9 * channels), unfolded.dtype)
+    for row_tap in range(3):
+        for col_tap in range(3):
+            offset = (row_tap - 1) * columns + (col_tap - 1)
+            moved = values if offset == 0 else pltpu.roll(values, (-offset) % rows, 0)
+            keep = (
+                (row + row_tap - 1 >= 0)
+                & (row + row_tap - 1 < frame_rows)
+                & (column + col_tap - 1 >= 0)
+                & (column + col_tap - 1 < columns)
+            )
+            tap = row_tap * 3 + col_tap
+            unfolded[2 * positions :, tap * channels : (tap + 1) * channels] = jnp.where(
+                keep, moved, 0.0
+            ).astype(unfolded.dtype)
+    acc = jnp.broadcast_to(b_ref[...], (rows, o_ref.shape[-1]))
+    for lag in range(3):
+        copies[lag].wait()
+        acc = acc + jnp.dot(
+            unfolded[lag * positions : lag * positions + rows, :],
+            w_vmem[lag],
+            preferred_element_type=jnp.float32,
+        )
+    out = acc.astype(o_ref.dtype)
+    o_ref[...] = out
+    value = out.astype(jnp.float32).reshape(frames, positions, -1)
+    s1_ref[...] = jnp.sum(value, axis=1, keepdims=True)
+    s2_ref[...] = jnp.sum(value * value, axis=1, keepdims=True)
+
+
+def conv_call(active, kernel, bias):
+    frames, frame_rows, columns, channels = active.shape
+    positions = frame_rows * columns
+    out_channels = kernel.shape[-1]
+    vmem = pl.BlockSpec(memory_space=pltpu.VMEM)
+    return pl.pallas_call(
+        functools.partial(conv_body, frame_rows=frame_rows, columns=columns),
+        out_shape=(
+            jax.ShapeDtypeStruct((frames * positions, out_channels), jnp.bfloat16),
+            jax.ShapeDtypeStruct((frames, 1, out_channels), jnp.float32),
+            jax.ShapeDtypeStruct((frames, 1, out_channels), jnp.float32),
+        ),
+        in_specs=[vmem, pl.BlockSpec(memory_space=pltpu.HBM), vmem],
+        out_specs=(vmem, vmem, vmem),
+        scratch_shapes=[
+            pltpu.VMEM(kernel.shape, kernel.dtype),
+            pltpu.VMEM(((frames + 2) * positions, 9 * channels), jnp.bfloat16),
+            pltpu.SemaphoreType.DMA((3,)),
+        ],
+        compiler_params=pltpu.CompilerParams(vmem_limit_bytes=48 * 1024 * 1024),
+        cost_estimate=pl.CostEstimate(
+            flops=2 * frames * positions * 3 * kernel.shape[1] * out_channels,
+            transcendentals=0,
+            bytes_accessed=active.size * 2 + kernel.size * 2 + frames * positions * out_channels * 2,
+        ),
+    )(active.reshape(frames * positions, channels), kernel, bias.reshape(1, out_channels))
 
 
 def local(
@@ -58,33 +131,15 @@
     active = normalize(latents.astype(jnp.float32), own_count, norm_scale, norm_offset).astype(
         jnp.bfloat16
     )
-    padded = jnp.pad(active, ((2, 0), (1, 1), (1, 1), (0, 0)))
-    unfolded = jnp.concatenate(
-        [
-            padded[:, row_tap : row_tap + frame_rows, col_tap : col_tap + columns]
-            for row_tap in range(3)
-            for col_tap in range(3)
-        ],
-        axis=-1,
-    ).reshape(frames + 2, frame_rows * columns, 9 * channels)
-    kernel = conv_weight.reshape(3, 9 * channels, -1)
-    spread_out = [
-        jnp.dot(
-            unfolded.reshape(-1, 9 * channels), kernel[frame_lag], preferred_element_type=jnp.float32
-        ).reshape(frames + 2, frame_rows * columns, -1)
-        for frame_lag in range(3)
-    ]
-    conv = conv_bias + sum(
-        spread_out[frame_lag][frame_lag : frame_lag + frames] for frame_lag in range(3)
-    )
-    conv = conv.reshape(frames, frame_rows, columns, -1)
-    block_out = conv.astype(jnp.bfloat16)
+    conv_flat, frame_first, frame_second = conv_call(
+        active, conv_weight.reshape(3, 9 * channels, -1), conv_bias
+    )
+    block_out = conv_flat.reshape(frames, frame_rows, columns, channels)
     per_group = channels // GROUPS
-    grouped = block_out.astype(jnp.float32).reshape(frames, frame_rows * columns, GROUPS, per_group)
-    live_mask = (jnp.arange(frames) < own_count).astype(jnp.float32)[:, None, None, None]
+    live_mask = (jnp.arange(frames) < own_count).astype(jnp.float32)[:, None]
     members = own_count.astype(jnp.float32) * (frame_rows * columns * per_group)
-    first_sum = jnp.sum(grouped * live_mask, axis=(0, 1, 3))
-    second_sum = jnp.sum(grouped * grouped * live_mask, axis=(0, 1, 3))
+    first_sum = jnp.sum(jnp.sum(frame_first[:, 0] * live_mask, axis=0).reshape(GROUPS, per_group), axis=1)
+    second_sum = jnp.sum(jnp.sum(frame_second[:, 0] * live_mask, axis=0).reshape(GROUPS, per_group), axis=1)
     clip_mean = first_sum / members
     clip_spread = second_sum / members - clip_mean * clip_mean
     clip_inverse = lax.rsqrt(clip_spread + eps)

time: 51.3 us -> 55.8 us (1.088)
  Pallas kernels: 0 us -> 12.1 us
  matrix products: 6.42 us -> 0 us
  local copies, waits for them, and re-layouts: 7.85 us -> 6.54 us
    pallas_call x0 -> x1, Pallas kernels: none -> 12.1 us  [conv_call(): pl.pallas_call(functools.partial(conv_body, frame_rows=frame_rows, column...]
    dot_general x3 -> x0, matrix products: 6.42 us -> none  [local(): jnp.dot(unfolded.reshape(-1, 9 * channels), kernel[frame_lag], preferred_...]
    unnamed x19 -> x9, local copies, waits for them, and re-layouts: 2.74 us -> 2.02 us
where the time goes in v11:
time: 55.8 us; the launch traced here: 55.4 us
  waiting for transfers between devices  20.6 us (37%)
  Pallas kernels  12.1 us (22%)
  other arithmetic  8.1 us (15%)
  starting transfers between devices  6.61 us (12%)
  local copies, waits for them, and re-layouts  6.54 us (12%)
  between operations  1.53 us (3%)
    all_to_all x1, waiting for transfers between devices, local(): lax.all_to_all(outgoing, 'tile', split_axis=0, concat_axis=0, tiled=True)  20.6 us
    pallas_call x1, Pallas kernels, conv_call(): pl.pallas_call(functools.partial(conv_body, frame_rows=frame_rows, column...  12.1 us
    all_to_all x1, starting transfers between devices, local(): lax.all_to_all(outgoing, 'tile', split_axis=0, concat_axis=0, tiled=True)  6.61 us
    unnamed x9, local copies, waits for them, and re-layouts  2.02 us
    convert_element_type x1, other arithmetic, local(): normalize(latents.astype(jnp.float32), own_count, norm_scale, norm_offset)  1.7 us
    reduce_sum x2, other arithmetic, normalize(): second = jnp.sum(jnp.sum(flat * flat, axis=1) * live_mask, axis=0)  1.47 us
    gather x1, local copies, waits for them, and re-layouts, local(): jnp.take(block_part.reshape(rows_all, columns, channels), take_from, axis...  1.3 us
    gather x1, local copies, waits for them, and re-layouts, local(): jnp.take(normed_part.reshape(rows_all, columns, channels), take_from, axi...  1.3 us
  transfers between devices with their start and end apart: 1, of which 1 were waited for; matrix products, arithmetic and copies ran while one was open for 1% of the time, Pallas kernels for 0%

profile of v11, /device:TPU:9, one launch (start us, length us, event | category | flops | bytes accessed | tf_op | source)
XLA Modules:
  0.0 55.4 jit_solution(14833224465236685618)
XLA Ops:
  0.6 0.7 %pad_add_fusion = s32[2,16]{1,0:T(2,128)S(1)} fusion(s32[1,16]{1,0:T(1,128)} %bitcast.55, s32[1,16]{1,0:T(1,128)} %bitcast.56), kind=kLoop, calls=%fused_computation.64 | loop fusion | flops 32 | bytes 256 | tf_op jit(solution)/shard_map/stack | solution.py:123
  1.3 0.6 %fusion.16 = s32[]{:T(128)} fusion(s32[]{:T(128)S(6)} %axis_index.12, s32[2,16]{1,0:T(2,128)S(1)} %pad_add_fusion), kind=kLoop, calls=%fused_computation.69 | loop fusion | flops 47 | bytes 72 | tf_op jit(solution)/shard_map/reduce_sum | solution.py:129
  2.0 0.6 %compare_convert_fusion = f32[12]{0:T(128)S(1)} fusion(s32[]{:T(128)} %fusion.16), kind=kLoop, calls=%fused_computation.51 | loop fusion | flops 24 | bytes 52 | tf_op jit(solution)/shard_map/convert_element_type | solution.py:22
  3.3 1.4 %fusion.9 = (f32[12,256]{1,0:T(8,128)S(1)}, f32[12,256]{1,0:T(8,128)S(1)}) fusion(bf16[12,16,8,256]{3,2,1,0:T(8,128)(2,1)} %param.9), kind=kLoop, calls=%fused_computation.15 | loop fusion | flops 1566720 | bytes 811008 | tf_op jit(solution)/shard_map/reduce_sum | solution.py:25
  4.9 0.1 reduce_sum.147
  5.1 0.1 reduce_sum.150
  5.3 0.1 mul.161
  5.4 0.1 sub.97
  5.5 1.7 %fusion.8 = bf16[12,16,8,256]{3,2,1,0:T(8,128)(2,1)S(1)} fusion(bf16[12,16,8,256]{3,2,1,0:T(8,128)(2,1)} %param.9, f32[256]{0:T(256)} %param.13, f32[256]{0:T(256)} %param.12, f32[256]{0:T(256)S(1)} %mul.161, f32[256]{0:T(256)S(1)} %sub.97), kind=kLoop, calls=%fused_computation.14 | loop fusion | flops 3932160 | bytes 1576960 | tf_op jit(solution)/shard_map/convert_element_type | solution.py:131
  7.3 2.0 %copy-done = bf16[3,3,3,256,256]{4,3,2,1,0:T(8,128)(2,1)S(1)} copy-done((bf16[3,3,3,256,256]{4,3,2,1,0:T(8,128)(2,1)S(1)}, bf16[3,3,3,256,256]{4,3,2,1,0:T(8,128)(2,1)}, u32[]{:S(2)}) %copy-start) | copy-done | bytes 3538968
  9.3 12.1 %shard_map.104 = (bf16[1536,256]{1,0:T(8,128)(2,1)S(1)}, f32[12,1,256]{2,1,0:T(1,128)S(1)}, f32[12,1,256]{2,1,0:T(1,128)S(1)}) custom-call(bf16[1536,256]{1,0:T(8,128)(2,1)S(1)} %bitcast.45, bf16[3,2304,256]{2,1,0:T(8,128)(2,1)S(1)} %bitcast.46, f32[1,256]{1,0:T(1,128)S(1)} %bitcast.47), custom_call_target="tpu_custom_call" | custom-call | flops 5435817984 | bytes 5111808 | tf_op jit(solution)/shard_map/pallas_call | solution.py:82
  21.5 0.1 reduce_sum.154
  21.7 0.1 reduce_sum.156
  22.0 0.1 reshape.320
  22.1 0.2 select_reduce_fusion.2
  22.4 0.1 reduce.2
  22.5 0.1 fusion.15
  22.7 0.6 %gather_fusion = bf16[2,6,8,2,8,256]{5,4,3,2,1,0:T(8,128)(2,1)S(1)} fusion(bf16[6,2,8,2,8,256]{5,4,3,2,1,0:T(8,128)(2,1)S(1)} %bitcast.44, s32[1024]{0:T(1024)S(1)} %pad_clamp_fusion.1), kind=kCustom, calls=%fused_computation | custom fusion | bytes 1572872 | tf_op jit(solution)/shard_map/jit(_take)/gather | solution.py:152
  23.5 1.0 %pad_maximum_fusion = bf16[16,104,256]{2,1,0:T(8,128)(2,1)} fusion(bf16[16,8,256]{2,1,0:T(8,128)(2,1)S(1)} %broadcast_in_dim.88, bf16[16,96,256]{2,1,0:T(8,128)(2,1)S(1)} %bitcast.51), kind=kLoop, calls=%fused_computation.17 | loop fusion | flops 1703936 | bytes 1703936 | tf_op jit(solution)/shard_map/concatenate | solution.py:162
  24.5 6.6 %all-to-all-start = ((bf16[16,104,256]{2,1,0:T(8,128)(2,1)}), bf16[16,104,256]{2,1,0:T(8,128)(2,1)S(1)}, u32[]{:S(2)}, u32[]{:S(2)}) async-start(bf16[16,104,256]{2,1,0:T(8,128)(2,1)} %pad_maximum_fusion), calls=%async_computation | async-start | bytes 1703936 | tf_op jit(solution)/shard_map/all_to_all | solution.py:163
  31.4 20.6 %all-to-all-done = bf16[16,104,256]{2,1,0:T(8,128)(2,1)S(1)} async-done(((bf16[16,104,256]{2,1,0:T(8,128)(2,1)}), bf16[16,104,256]{2,1,0:T(8,128)(2,1)S(1)}, u32[]{:S(2)}, u32[]{:S(2)}) %all-to-all-start) | async-done | bytes 852000 | tf_op jit(solution)/shard_map/all_to_all | solution.py:163
  52.3 1.3 %gather_fusion.1 = bf16[64,8,256]{2,1,0:T(8,128)(2,1)} fusion(bf16[192,8,256]{2,1,0:T(8,128)(2,1)S(1)} %bitcast.48, s32[1024]{0:T(1024)S(1)} %pad_clamp_fusion), kind=kCustom, calls=%fused_computation.1 | custom fusion | bytes 524544 | tf_op jit(solution)/shard_map/jit(_take)/gather | solution.py:184
  53.6 0.5 multiply_convert_fusion
  54.1 1.3 %gather_fusion.2 = bf16[64,8,256]{2,1,0:T(8,128)(2,1)} fusion(bf16[192,8,256]{2,1,0:T(8,128)(2,1)S(1)} %multiply_convert_fusion, s32[1024]{0:T(1024)S(1)} %pad_clamp_fusion), kind=kCustom, calls=%fused_computation.2 | custom fusion | bytes 524544 | tf_op jit(solution)/shard_map/jit(_take)/gather | solution.py:185
  (48 shorter events, 1.7 us)
Async XLA Ops:
  0.6 6.6 %copy-start.1 = (f32[256]{0:T(256)S(1)}, f32[256]{0:T(256)}, u32[]{:S(2)}) copy-start(f32[256]{0:T(256)} %param.15) | copy-start | bytes 3076
  7.2 2.0 %copy-start = (bf16[3,3,3,256,256]{4,3,2,1,0:T(8,128)(2,1)S(1)}, bf16[3,3,3,256,256]{4,3,2,1,0:T(8,128)(2,1)}, u32[]{:S(2)}) copy-start(bf16[3,3,3,256,256]{4,3,2,1,0:T(8,128)(2,1)} %param.14) | copy-start | bytes 10616836
  24.5 27.5 %all-to-all-start = ((bf16[16,104,256]{2,1,0:T(8,128)(2,1)}), bf16[16,104,256]{2,1,0:T(8,128)(2,1)S(1)}, u32[]{:S(2)}, u32[]{:S(2)}) async-start(bf16[16,104,256]{2,1,0:T(8,128)(2,1)} %pad_maximum_fusion), calls=%async_computation | async-start | bytes 1703936 | tf_op jit(solution)/shard_map/all_to_all | solution.py:163
  52.1 1.5 %copy-start.2 = (f32[256]{0:T(256)S(1)}, f32[256]{0:T(256)}, u32[]{:S(2)}) copy-start(f32[256]{0:T(256)} %param.17) | copy-start | bytes 3076
  52.1 1.5 %copy-start.3 = (f32[256]{0:T(256)S(1)}, f32[256]{0:T(256)}, u32[]{:S(2)}) copy-start(f32[256]{0:T(256)} %param.16) | copy-start | bytes 3076

commit v12 on v9

--- a/solution.py
+++ b/solution.py
@@ -94,7 +94,12 @@
     tiles = tiles.reshape(per_dest, classes, NRB, tile_rows, columns, channels)
     lag_of = (jnp.arange(classes, dtype=jnp.int32)[:, None] - (starts // NRB)[None, :] % classes) % classes
     pick = jnp.sum(jnp.where(clip_order[None, :] == device, lag_of, 0), axis=1)
-    tiles = jnp.take(tiles, pick, axis=1)
+    chosen = jnp.broadcast_to(tiles[:, 0:1], tiles.shape)
+    for lag in range(1, classes):
+        chosen = jnp.where(
+            (pick == lag)[None, :, None, None, None, None], tiles[:, lag : lag + 1], chosen
+        )
+    tiles = chosen
     tiles = jnp.transpose(tiles, (1, 2, 3, 0, 4, 5)).reshape(
         devices, tile_rows * per_dest * columns, channels
     )

time: 51 us -> 50.8 us (level)
    gather x1 -> x0, local copies, waits for them, and re-layouts: 0.6 us -> none  [local(): tiles = jnp.take(tiles, pick, axis=1)]
where the time goes in v12:
time: 50.8 us; the launch traced here: 50.4 us
  waiting for transfers between devices  20.5 us (40%)
  other arithmetic  8.95 us (18%)
  starting transfers between devices  6.61 us (13%)
  matrix products  6.43 us (13%)
  local copies, waits for them, and re-layouts  6.21 us (12%)
  between operations  1.71 us (3%)
    all_to_all x1, waiting for transfers between devices, local(): lax.all_to_all(outgoing, 'tile', split_axis=0, concat_axis=0, tiled=True)  20.5 us
    all_to_all x1, starting transfers between devices, local(): lax.all_to_all(outgoing, 'tile', split_axis=0, concat_axis=0, tiled=True)  6.61 us
    dot_general x3, matrix products, local(): jnp.dot(unfolded.reshape(-1, 9 * channels), kernel[frame_lag], preferred_...  6.43 us
    unnamed x19, local copies, waits for them, and re-layouts  2.74 us
    reduce_sum x2, other arithmetic, normalize(): second = jnp.sum(jnp.sum(flat * flat, axis=1) * live_mask, axis=0)  1.47 us
    convert_element_type x1, other arithmetic, local(): normalize(latents.astype(jnp.float32), own_count, norm_scale, norm_offset)  1.24 us
  transfers between devices with their start and end apart: 1, of which 1 were waited for; matrix products, arithmetic and copies ran while one was open for 1% of the time, Pallas kernels for 0%

profile of v12, /device:TPU:9, one launch (start us, length us, event | category | flops | bytes accessed | tf_op | source)
XLA Modules:
  0.0 50.4 jit_solution(6698981312078533657)
XLA Ops:
  0.6 0.8 %pad_add_fusion = s32[2,16]{1,0:T(2,128)S(1)} fusion(s32[1,16]{1,0:T(1,128)} %bitcast.62, s32[1,16]{1,0:T(1,128)} %bitcast.63), kind=kLoop, calls=%fused_computation.99 | loop fusion | flops 32 | bytes 256 | tf_op jit(solution)/shard_map/stack | solution.py:50
  1.4 0.6 %fusion.38 = s32[]{:T(128)} fusion(s32[]{:T(128)S(6)} %axis_index.12, s32[2,16]{1,0:T(2,128)S(1)} %pad_add_fusion), kind=kLoop, calls=%fused_computation.103 | loop fusion | flops 47 | bytes 72 | tf_op jit(solution)/shard_map/reduce_sum | solution.py:56
  2.0 0.6 %compare_convert_fusion = f32[12]{0:T(128)S(1)} fusion(s32[]{:T(128)} %fusion.38), kind=kLoop, calls=%fused_computation.82 | loop fusion | flops 24 | bytes 52 | tf_op jit(solution)/shard_map/convert_element_type | solution.py:18
  3.4 1.4 %fusion.24 = (f32[12,256]{1,0:T(8,128)S(1)}, f32[12,256]{1,0:T(8,128)S(1)}) fusion(bf16[12,16,8,256]{3,2,1,0:T(8,128)(2,1)} %param.11), kind=kLoop, calls=%fused_computation.36 | loop fusion | flops 1566720 | bytes 811008 | tf_op jit(solution)/shard_map/reduce_sum | solution.py:21
  5.7 1.2 %fusion.23 = bf16[12,16,8,256]{3,2,1,0:T(8,128)(2,1)S(1)} fusion(bf16[12,16,8,256]{3,2,1,0:T(8,128)(2,1)S(1)} %copy-done.1, f32[256]{0:T(256)} %param.15, f32[256]{0:T(256)} %param.14, f32[256]{0:T(256)S(1)} %mul.167, f32[256]{0:T(256)S(1)} %sub.102), kind=kLoop, calls=%fused_computation.35 | loop fusion | flops 3932160 | bytes 1576960 | tf_op jit(solution)/shard_map/convert_element_type | solution.py:58
  6.9 0.2 fusion.25
  7.2 0.2 fusion.27
  7.4 0.2 fusion.28
  7.7 0.2 fusion.30
  7.9 0.2 fusion.31
  8.2 0.2 fusion.33
  8.4 1.5 %copy-done = bf16[3,3,3,256,256]{4,3,2,1,0:T(8,128)(2,1)S(1)} copy-done((bf16[3,3,3,256,256]{4,3,2,1,0:T(8,128)(2,1)S(1)}, bf16[3,3,3,256,256]{4,3,2,1,0:T(8,128)(2,1)}, u32[]{:S(2)}) %copy-start) | copy-done | bytes 3538968
  9.9 0.3 fusion.42
  10.2 2.1 %fusion.2 = f32[1536,256]{1,0:T(8,128)S(1)} fusion(bf16[2304,256]{1,0:T(8,128)(2,1)S(1)} %bitcast.55, bf16[1792,2304]{1,0:T(8,128)(2,1)S(1)} %bitcast.58), kind=kOutput, calls=%fused_computation.4 | convolution fusion | flops 1811939328 | bytes 9830400 | tf_op jit(solution)/shard_map/dot_general | solution.py:72
  12.3 2.1 %fusion.6 = f32[1536,256]{1,0:T(8,128)S(1)} fusion(f32[1536,256]{1,0:T(8,128)S(1)} %fusion.2, bf16[2304,256]{1,0:T(8,128)(2,1)S(1)} %bitcast.54, bf16[1792,2304]{1,0:T(8,128)(2,1)S(1)} %bitcast.59), kind=kOutput, calls=%fused_computation.17 | convolution fusion | flops 1812332544 | bytes 11403264 | tf_op jit(solution)/shard_map/dot_general | solution.py:72
  14.5 2.3 %fusion.12 = (f32[256]{0:T(256)S(1)}, f32[256]{0:T(256)S(1)}, f32[1536,256]{1,0:T(8,128)S(1)}) fusion(f32[1536]{0:T(1024)S(1)} %broadcast_bitcast_fusion, f32[256]{0:T(256)S(1)} %copy-done.2, f32[1536,256]{1,0:T(8,128)S(1)} %fusion.6, bf16[2304,256]{1,0:T(8,128)(2,1)S(1)} %bitcast.53, bf16[1792,2304]{1,0:T(8,128)(2,1)S(1)} %bitcast.60), kind=kOutput, calls=%fused_computation.24 | convolution fusion | flops 1815477760 | bytes 11414528 | tf_op jit(solution)/shard_map/dot_general | solution.py:72
  16.7 0.2 add_convert_fusion.1
  19.0 1.0 %pad_maximum_fusion = bf16[16,104,256]{2,1,0:T(8,128)(2,1)} fusion(bf16[16,8,256]{2,1,0:T(8,128)(2,1)S(1)} %broadcast_in_dim.139, bf16[16,96,256]{2,1,0:T(8,128)(2,1)S(1)} %broadcast_select_fusion), kind=kLoop, calls=%fused_computation.49 | loop fusion | flops 1703936 | bytes 1703936 | tf_op jit(solution)/shard_map/concatenate | solution.py:112
  19.9 6.6 %all-to-all-start = ((bf16[16,104,256]{2,1,0:T(8,128)(2,1)}), bf16[16,104,256]{2,1,0:T(8,128)(2,1)S(1)}, u32[]{:S(2)}, u32[]{:S(2)}) async-start(bf16[16,104,256]{2,1,0:T(8,128)(2,1)} %pad_maximum_fusion), calls=%async_computation | async-start | bytes 1703936 | tf_op jit(solution)/shard_map/all_to_all | solution.py:113
  26.9 20.5 %all-to-all-done = bf16[16,104,256]{2,1,0:T(8,128)(2,1)S(1)} async-done(((bf16[16,104,256]{2,1,0:T(8,128)(2,1)}), bf16[16,104,256]{2,1,0:T(8,128)(2,1)S(1)}, u32[]{:S(2)}, u32[]{:S(2)}) %all-to-all-start) | async-done | bytes 852000 | tf_op jit(solution)/shard_map/all_to_all | solution.py:113
  47.7 0.6 %gather_fusion = bf16[64,8,256]{2,1,0:T(8,128)(2,1)S(1)} fusion(bf16[192,8,256]{2,1,0:T(8,128)(2,1)S(1)} %bitcast.48, s32[1024]{0:T(1024)S(1)} %pad_clamp_fusion), kind=kCustom, calls=%fused_computation.clone | custom fusion | bytes 524544 | tf_op jit(solution)/shard_map/jit(_take)/gather | solution.py:134
  48.4 0.5 %multiply_convert_fusion = bf16[192,8,256]{2,1,0:T(8,128)(2,1)S(1)} fusion(bf16[192,8,256]{2,1,0:T(8,128)(2,1)S(1)} %bitcast.49, f32[256]{0:T(256)S(1)} %copy-done.3, f32[256]{0:T(256)S(1)} %copy-done.4, f32[192,256]{1,0:T(8,128)S(1)} %mul.187, f32[192,256]{1,0:T(8,128)S(1)} %sub.113), kind=kLoop, calls=%fused_computation.37 | loop fusion | flops 3932160 | bytes 1968128 | tf_op jit(solution)/shard_map/convert_element_type | solution.py:123
  48.9 0.6 %gather_fusion.1 = bf16[64,8,256]{2,1,0:T(8,128)(2,1)S(1)} fusion(bf16[192,8,256]{2,1,0:T(8,128)(2,1)S(1)} %multiply_convert_fusion, s32[1024]{0:T(1024)S(1)} %pad_clamp_fusion), kind=kCustom, calls=%fused_computation.1.clone | custom fusion | bytes 524544 | tf_op jit(solution)/shard_map/jit(_take)/gather | solution.py:135
  49.5 0.9 %broadcast_select_fusion.1 = (bf16[2,32,8,256]{3,2,1,0:T(8,128)(2,1)}, bf16[2,32,8,256]{3,2,1,0:T(8,128)(2,1)}) fusion(bf16[2,32,8,256]{3,2,1,0:T(8,128)(2,1)S(1)} %bitcast.57, pred[2,32]{1,0:T(4,128)(4,1)S(1)} %compare_and_fusion, bf16[2,32,8,256]{3,2,1,0:T(8,128)(2,1)S(1)} %bitcast.56), kind=kLoop, calls=%fused_computation.53 | loop fusion | flops 262144 | bytes 1048640 | tf_op jit(solution)/shard_map/jit(_take)/select_n | solution.py:135
  (71 shorter events, 3.7 us)
Async XLA Ops:
  0.6 5.0 %copy-start.1 = (bf16[12,16,8,256]{3,2,1,0:T(8,128)(2,1)S(1)}, bf16[12,16,8,256]{3,2,1,0:T(8,128)(2,1)}, u32[]{:S(2)}) copy-start(bf16[12,16,8,256]{3,2,1,0:T(8,128)(2,1)} %param.11) | copy-start | bytes 2359300
  7.9 2.0 %copy-start = (bf16[3,3,3,256,256]{4,3,2,1,0:T(8,128)(2,1)S(1)}, bf16[3,3,3,256,256]{4,3,2,1,0:T(8,128)(2,1)}, u32[]{:S(2)}) copy-start(bf16[3,3,3,256,256]{4,3,2,1,0:T(8,128)(2,1)} %param.16) | copy-start | bytes 10616836
  12.3 2.1 %copy-start.2 = (f32[256]{0:T(256)S(1)}, f32[256]{0:T(256)}, u32[]{:S(2)}) copy-start(f32[256]{0:T(256)} %param.17) | copy-start | bytes 3076
  19.9 27.5 %all-to-all-start = ((bf16[16,104,256]{2,1,0:T(8,128)(2,1)}), bf16[16,104,256]{2,1,0:T(8,128)(2,1)S(1)}, u32[]{:S(2)}, u32[]{:S(2)}) async-start(bf16[16,104,256]{2,1,0:T(8,128)(2,1)} %pad_maximum_fusion), calls=%async_computation | async-start | bytes 1703936 | tf_op jit(solution)/shard_map/all_to_all | solution.py:113
  47.5 0.8 %copy-start.3 = (f32[256]{0:T(256)S(1)}, f32[256]{0:T(256)}, u32[]{:S(2)}) copy-start(f32[256]{0:T(256)} %param.19) | copy-start | bytes 3076
  47.5 0.8 %copy-start.4 = (f32[256]{0:T(256)S(1)}, f32[256]{0:T(256)}, u32[]{:S(2)}) copy-start(f32[256]{0:T(256)} %param.18) | copy-start | bytes 3076

commit v13 on v12

--- a/solution.py
+++ b/solution.py
@@ -11,12 +11,12 @@
 eps = 1e-06
 
 
-def normalize(values, frame_count, scaling, offsets):
+def normalize(values, live_frames, scaling, offsets):
     frames = values.shape[0]
     channels = values.shape[-1]
     flat = values.reshape(frames, -1, channels)
-    live_mask = (jnp.arange(frames) < frame_count).astype(jnp.float32)[:, None]
-    members = frame_count.astype(jnp.float32) * flat.shape[1] * (channels // GROUPS)
+    live_mask = live_frames[:, None]
+    members = jnp.sum(live_frames) * flat.shape[1] * (channels // GROUPS)
     first = jnp.sum(jnp.sum(flat, axis=1) * live_mask, axis=0)
     second = jnp.sum(jnp.sum(flat * flat, axis=1) * live_mask, axis=0)
     group_mean = jnp.sum(first.reshape(GROUPS, -1), axis=1) / members
@@ -53,9 +53,17 @@
     chosen = clip_order[:, None] == positions[None, :]
     ordered = jnp.sum(jnp.where(chosen, frame_counts[None, :], 0), axis=1)
     starts = (jnp.cumsum(ordered) - ordered) * NRB
-    own_count = jnp.sum(jnp.where(positions == device, frame_counts, 0))
+    live_frames = jnp.sum(
+        jnp.where(
+            (positions[None, :] == device)
+            & (jnp.arange(latents.shape[0], dtype=jnp.int32)[:, None] < frame_counts[None, :]),
+            1.0,
+            0.0,
+        ),
+        axis=1,
+    )
 
-    active = normalize(latents.astype(jnp.float32), own_count, norm_scale, norm_offset).astype(
+    active = normalize(latents.astype(jnp.float32), live_frames, norm_scale, norm_offset).astype(
         jnp.bfloat16
     )
     padded = jnp.pad(active, ((2, 0), (1, 1), (1, 1), (0, 0)))
@@ -81,8 +89,8 @@
     block_out = conv.astype(jnp.bfloat16)
     per_group = channels // GROUPS
     grouped = block_out.astype(jnp.float32).reshape(frames, frame_rows * columns, GROUPS, per_group)
-    live_mask = (jnp.arange(frames) < own_count).astype(jnp.float32)[:, None, None, None]
-    members = own_count.astype(jnp.float32) * (frame_rows * columns * per_group)
+    live_mask = live_frames[:, None, None, None]
+    members = jnp.sum(live_frames) * (frame_rows * columns * per_group)
     first_sum = jnp.sum(grouped * live_mask, axis=(0, 1, 3))
     second_sum = jnp.sum(grouped * grouped * live_mask, axis=(0, 1, 3))
     clip_mean = first_sum / members

time: 50.8 us -> 50.1 us (0.986)
  other arithmetic: 8.95 us -> 8.28 us
    convert_element_type x2 -> x1, other arithmetic: 1.89 us -> 1.24 us  [local(): normalize(latents.astype(jnp.float32), live_frames, norm_scale, norm_offset)]
where the time goes in v13:
time: 50.1 us; the launch traced here: 49.8 us
  waiting for transfers between devices  20.5 us (41%)
  other arithmetic  8.28 us (17%)
  starting transfers between devices  6.61 us (13%)
  matrix products  6.43 us (13%)
  local copies, waits for them, and re-layouts  6.2 us (12%)
  between operations  1.72 us (3%)
    all_to_all x1, waiting for transfers between devices, local(): lax.all_to_all(outgoing, 'tile', split_axis=0, concat_axis=0, tiled=True)  20.5 us
    all_to_all x1, starting transfers between devices, local(): lax.all_to_all(outgoing, 'tile', split_axis=0, concat_axis=0, tiled=True)  6.61 us
    dot_general x3, matrix products, local(): jnp.dot(unfolded.reshape(-1, 9 * channels), kernel[frame_lag], preferred_...  6.43 us
    unnamed x19, local copies, waits for them, and re-layouts  2.74 us
    reduce_sum x2, other arithmetic, normalize(): second = jnp.sum(jnp.sum(flat * flat, axis=1) * live_mask, axis=0)  1.47 us
    convert_element_type x1, other arithmetic, local(): normalize(latents.astype(jnp.float32), live_frames, norm_scale, norm_offset)  1.24 us
  transfers between devices with their start and end apart: 1, of which 1 were waited for; matrix products, arithmetic and copies ran while one was open for 1% of the time, Pallas kernels for 0%

profile of v13, /device:TPU:9, one launch (start us, length us, event | category | flops | bytes accessed | tf_op | source)
XLA Modules:
  0.0 49.8 jit_solution(12821280899558843936)
XLA Ops:
  0.6 0.8 %pad_add_fusion = s32[2,16]{1,0:T(2,128)S(1)} fusion(s32[1,16]{1,0:T(1,128)} %bitcast.60, s32[1,16]{1,0:T(1,128)} %bitcast.61), kind=kLoop, calls=%fused_computation.101 | loop fusion | flops 32 | bytes 256 | tf_op jit(solution)/shard_map/stack | solution.py:50
  1.4 1.4 %fusion.24 = (f32[12,256]{1,0:T(8,128)S(1)}, f32[12,256]{1,0:T(8,128)S(1)}) fusion(bf16[12,16,8,256]{3,2,1,0:T(8,128)(2,1)} %param.11), kind=kLoop, calls=%fused_computation.36 | loop fusion | flops 1566720 | bytes 811008 | tf_op jit(solution)/shard_map/reduce_sum | solution.py:21
  2.8 0.6 %select_reduce_fusion = (f32[]{:T(128)}, f32[12]{0:T(128)S(1)}) fusion(s32[16]{0:T(128)S(1)} %get-tuple-element.27, pred[16]{0:T(512)(128)(4,1)S(1)} %iota_compare_fusion.3), kind=kLoop, calls=%fused_computation.62 | loop fusion | flops 947 | bytes 132 | tf_op jit(solution)/shard_map/reduce_sum | solution.py:19
  5.0 1.2 %fusion.23 = bf16[12,16,8,256]{3,2,1,0:T(8,128)(2,1)S(1)} fusion(bf16[12,16,8,256]{3,2,1,0:T(8,128)(2,1)S(1)} %copy-done.1, f32[256]{0:T(256)} %param.15, f32[256]{0:T(256)} %param.14, f32[256]{0:T(256)S(1)} %mul.167, f32[256]{0:T(256)S(1)} %sub.102), kind=kLoop, calls=%fused_computation.35 | loop fusion | flops 3932160 | bytes 1576960 | tf_op jit(solution)/shard_map/convert_element_type | solution.py:66
  6.3 0.2 fusion.25
  6.5 0.2 fusion.27
  6.7 0.2 fusion.28
  7.0 0.2 fusion.30
  7.2 0.2 fusion.31
  7.5 0.2 fusion.33
  7.7 1.5 %copy-done = bf16[3,3,3,256,256]{4,3,2,1,0:T(8,128)(2,1)S(1)} copy-done((bf16[3,3,3,256,256]{4,3,2,1,0:T(8,128)(2,1)S(1)}, bf16[3,3,3,256,256]{4,3,2,1,0:T(8,128)(2,1)}, u32[]{:S(2)}) %copy-start) | copy-done | bytes 3538968
  9.2 0.3 fusion.42
  9.6 2.1 %fusion.2 = f32[1536,256]{1,0:T(8,128)S(1)} fusion(bf16[2304,256]{1,0:T(8,128)(2,1)S(1)} %bitcast.53, bf16[1792,2304]{1,0:T(8,128)(2,1)S(1)} %bitcast.56), kind=kOutput, calls=%fused_computation.4 | convolution fusion | flops 1811939328 | bytes 9830400 | tf_op jit(solution)/shard_map/dot_general | solution.py:80
  11.7 2.1 %fusion.6 = f32[1536,256]{1,0:T(8,128)S(1)} fusion(f32[1536,256]{1,0:T(8,128)S(1)} %fusion.2, bf16[2304,256]{1,0:T(8,128)(2,1)S(1)} %bitcast.52, bf16[1792,2304]{1,0:T(8,128)(2,1)S(1)} %bitcast.57), kind=kOutput, calls=%fused_computation.17 | convolution fusion | flops 1812332544 | bytes 11403264 | tf_op jit(solution)/shard_map/dot_general | solution.py:80
  13.8 2.3 %fusion.12 = (f32[256]{0:T(256)S(1)}, f32[256]{0:T(256)S(1)}, f32[1536,256]{1,0:T(8,128)S(1)}) fusion(f32[1536]{0:T(1024)S(1)} %broadcast_bitcast_fusion, f32[256]{0:T(256)S(1)} %copy-done.2, f32[1536,256]{1,0:T(8,128)S(1)} %fusion.6, bf16[2304,256]{1,0:T(8,128)(2,1)S(1)} %bitcast.51, bf16[1792,2304]{1,0:T(8,128)(2,1)S(1)} %bitcast.58), kind=kOutput, calls=%fused_computation.24 | convolution fusion | flops 1815477760 | bytes 11414528 | tf_op jit(solution)/shard_map/dot_general | solution.py:80
  16.0 0.2 add_convert_fusion.1
  16.4 0.2 select_reduce_fusion.4
  18.3 1.0 %pad_maximum_fusion = bf16[16,104,256]{2,1,0:T(8,128)(2,1)} fusion(bf16[16,8,256]{2,1,0:T(8,128)(2,1)S(1)} %broadcast_in_dim.149, bf16[16,96,256]{2,1,0:T(8,128)(2,1)S(1)} %broadcast_select_fusion), kind=kLoop, calls=%fused_computation.49 | loop fusion | flops 1703936 | bytes 1703936 | tf_op jit(solution)/shard_map/concatenate | solution.py:120
  19.3 6.6 %all-to-all-start = ((bf16[16,104,256]{2,1,0:T(8,128)(2,1)}), bf16[16,104,256]{2,1,0:T(8,128)(2,1)S(1)}, u32[]{:S(2)}, u32[]{:S(2)}) async-start(bf16[16,104,256]{2,1,0:T(8,128)(2,1)} %pad_maximum_fusion), calls=%async_computation | async-start | bytes 1703936 | tf_op jit(solution)/shard_map/all_to_all | solution.py:121
  26.2 20.5 %all-to-all-done = bf16[16,104,256]{2,1,0:T(8,128)(2,1)S(1)} async-done(((bf16[16,104,256]{2,1,0:T(8,128)(2,1)}), bf16[16,104,256]{2,1,0:T(8,128)(2,1)S(1)}, u32[]{:S(2)}, u32[]{:S(2)}) %all-to-all-start) | async-done | bytes 852000 | tf_op jit(solution)/shard_map/all_to_all | solution.py:121
  47.1 0.6 %gather_fusion = bf16[64,8,256]{2,1,0:T(8,128)(2,1)S(1)} fusion(bf16[192,8,256]{2,1,0:T(8,128)(2,1)S(1)} %bitcast.46, s32[1024]{0:T(1024)S(1)} %pad_clamp_fusion), kind=kCustom, calls=%fused_computation.clone | custom fusion | bytes 524544 | tf_op jit(solution)/shard_map/jit(_take)/gather | solution.py:142
  47.7 0.5 %multiply_convert_fusion = bf16[192,8,256]{2,1,0:T(8,128)(2,1)S(1)} fusion(bf16[192,8,256]{2,1,0:T(8,128)(2,1)S(1)} %bitcast.47, f32[256]{0:T(256)S(1)} %copy-done.3, f32[256]{0:T(256)S(1)} %copy-done.4, f32[192,256]{1,0:T(8,128)S(1)} %mul.187, f32[192,256]{1,0:T(8,128)S(1)} %sub.113), kind=kLoop, calls=%fused_computation.37 | loop fusion | flops 3932160 | bytes 1968128 | tf_op jit(solution)/shard_map/convert_element_type | solution.py:131
  48.2 0.6 %gather_fusion.1 = bf16[64,8,256]{2,1,0:T(8,128)(2,1)S(1)} fusion(bf16[192,8,256]{2,1,0:T(8,128)(2,1)S(1)} %multiply_convert_fusion, s32[1024]{0:T(1024)S(1)} %pad_clamp_fusion), kind=kCustom, calls=%fused_computation.1.clone | custom fusion | bytes 524544 | tf_op jit(solution)/shard_map/jit(_take)/gather | solution.py:143
  48.8 0.9 %broadcast_select_fusion.1 = (bf16[2,32,8,256]{3,2,1,0:T(8,128)(2,1)}, bf16[2,32,8,256]{3,2,1,0:T(8,128)(2,1)}) fusion(bf16[2,32,8,256]{3,2,1,0:T(8,128)(2,1)S(1)} %bitcast.55, pred[2,32]{1,0:T(4,128)(4,1)S(1)} %compare_and_fusion, bf16[2,32,8,256]{3,2,1,0:T(8,128)(2,1)S(1)} %bitcast.54), kind=kLoop, calls=%fused_computation.53 | loop fusion | flops 262144 | bytes 1048640 | tf_op jit(solution)/shard_map/jit(_take)/select_n | solution.py:143
  (71 shorter events, 3.5 us)
Async XLA Ops:
  0.6 4.4 %copy-start.1 = (bf16[12,16,8,256]{3,2,1,0:T(8,128)(2,1)S(1)}, bf16[12,16,8,256]{3,2,1,0:T(8,128)(2,1)}, u32[]{:S(2)}) copy-start(bf16[12,16,8,256]{3,2,1,0:T(8,128)(2,1)} %param.11) | copy-start | bytes 2359300
  7.2 2.0 %copy-start = (bf16[3,3,3,256,256]{4,3,2,1,0:T(8,128)(2,1)S(1)}, bf16[3,3,3,256,256]{4,3,2,1,0:T(8,128)(2,1)}, u32[]{:S(2)}) copy-start(bf16[3,3,3,256,256]{4,3,2,1,0:T(8,128)(2,1)} %param.16) | copy-start | bytes 10616836
  11.6 2.1 %copy-start.2 = (f32[256]{0:T(256)S(1)}, f32[256]{0:T(256)}, u32[]{:S(2)}) copy-start(f32[256]{0:T(256)} %param.17) | copy-start | bytes 3076
  19.3 27.5 %all-to-all-start = ((bf16[16,104,256]{2,1,0:T(8,128)(2,1)}), bf16[16,104,256]{2,1,0:T(8,128)(2,1)S(1)}, u32[]{:S(2)}, u32[]{:S(2)}) async-start(bf16[16,104,256]{2,1,0:T(8,128)(2,1)} %pad_maximum_fusion), calls=%async_computation | async-start | bytes 1703936 | tf_op jit(solution)/shard_map/all_to_all | solution.py:121
  46.9 0.8 %copy-start.3 = (f32[256]{0:T(256)S(1)}, f32[256]{0:T(256)}, u32[]{:S(2)}) copy-start(f32[256]{0:T(256)} %param.19) | copy-start | bytes 3076
  46.9 0.8 %copy-start.4 = (f32[256]{0:T(256)S(1)}, f32[256]{0:T(256)}, u32[]{:S(2)}) copy-start(f32[256]{0:T(256)} %param.18) | copy-start | bytes 3076

commit v14 on v13

--- a/solution.py
+++ b/solution.py
@@ -139,9 +139,9 @@
     row_of = jnp.arange(tile_rows, dtype=jnp.int32)[:, None]
     take_from = (clip_id[None, :] * tile_rows + row_of) * per_dest + (within // NRB // classes)[None, :]
     rows_all = devices * tile_rows * per_dest
-    block_mine = jnp.take(block_part.reshape(rows_all, columns, channels), take_from, axis=0)
-    normed_mine = jnp.take(normed_part.reshape(rows_all, columns, channels), take_from, axis=0)
-    return (block_mine, normed_mine)
+    both = jnp.stack([block_part, normed_part], 0).reshape(2 * rows_all, columns, channels)
+    picked = jnp.take(both, jnp.stack([take_from, take_from + rows_all], 0), axis=0, mode="clip")
+    return (picked[0], picked[1])
 
 
 def solution(mesh):

time: 50.1 us -> 49.6 us (0.990)
  other arithmetic: 8.28 us -> 7.52 us
    select_n x2 -> x0, other arithmetic: 0.94 us -> none  [the longest x1 0.93 us: local(): jnp.take(normed_part.reshape(rows_all, columns, channels), take_from, axi...]
    slice x0 -> x1, local copies, waits for them, and re-layouts: none -> 0.82 us  [local(): return (picked[0], picked[1])]
    gather x2 -> x1, local copies, waits for them, and re-layouts: 1.19 us -> 0.65 us  [local(): jnp.take(both, jnp.stack([take_from, take_from + rows_all], 0), axis=0, m...]
where the time goes in v14:
time: 49.6 us; the launch traced here: 49.3 us
  waiting for transfers between devices  20.5 us (41%)
  other arithmetic  7.52 us (15%)
  starting transfers between devices  6.74 us (14%)
  matrix products  6.43 us (13%)
  local copies, waits for them, and re-layouts  6.38 us (13%)
  between operations  1.67 us (3%)
    all_to_all x1, waiting for transfers between devices, local(): lax.all_to_all(outgoing, 'tile', split_axis=0, concat_axis=0, tiled=True)  20.5 us
    all_to_all x1, starting transfers between devices, local(): lax.all_to_all(outgoing, 'tile', split_axis=0, concat_axis=0, tiled=True)  6.74 us
    dot_general x3, matrix products, local(): jnp.dot(unfolded.reshape(-1, 9 * channels), kernel[frame_lag], preferred_...  6.43 us
    unnamed x19, local copies, waits for them, and re-layouts  2.73 us
    reduce_sum x2, other arithmetic, normalize(): second = jnp.sum(jnp.sum(flat * flat, axis=1) * live_mask, axis=0)  1.47 us
    convert_element_type x1, other arithmetic, local(): normalize(latents.astype(jnp.float32), live_frames, norm_scale, norm_offset)  1.24 us
  transfers between devices with their start and end apart: 1, of which 1 were waited for; matrix products, arithmetic and copies ran while one was open for 1% of the time, Pallas kernels for 0%

profile of v14, /device:TPU:9, one launch (start us, length us, event | category | flops | bytes accessed | tf_op | source)
XLA Modules:
  0.0 49.3 jit_solution(2825413839810121752)
XLA Ops:
  0.6 0.8 %pad_add_fusion.1 = s32[2,16]{1,0:T(2,128)S(1)} fusion(s32[1,16]{1,0:T(1,128)} %bitcast.62, s32[1,16]{1,0:T(1,128)} %bitcast.63), kind=kLoop, calls=%fused_computation.98 | loop fusion | flops 32 | bytes 256 | tf_op jit(solution)/shard_map/stack | solution.py:50
  1.4 1.4 %fusion.24 = (f32[12,256]{1,0:T(8,128)S(1)}, f32[12,256]{1,0:T(8,128)S(1)}) fusion(bf16[12,16,8,256]{3,2,1,0:T(8,128)(2,1)} %param.9), kind=kLoop, calls=%fused_computation.35 | loop fusion | flops 1566720 | bytes 811008 | tf_op jit(solution)/shard_map/reduce_sum | solution.py:21
  2.8 0.6 %select_reduce_fusion = (f32[]{:T(128)}, f32[12]{0:T(128)S(1)}) fusion(s32[16]{0:T(128)S(1)} %get-tuple-element.30, pred[16]{0:T(512)(128)(4,1)S(1)} %iota_compare_fusion.3), kind=kLoop, calls=%fused_computation.60 | loop fusion | flops 947 | bytes 132 | tf_op jit(solution)/shard_map/reduce_sum | solution.py:19
  5.0 1.2 %fusion.23 = bf16[12,16,8,256]{3,2,1,0:T(8,128)(2,1)S(1)} fusion(bf16[12,16,8,256]{3,2,1,0:T(8,128)(2,1)S(1)} %copy-done.1, f32[256]{0:T(256)} %param.13, f32[256]{0:T(256)} %param.12, f32[256]{0:T(256)S(1)} %mul.192, f32[256]{0:T(256)S(1)} %sub.104), kind=kLoop, calls=%fused_computation.34 | loop fusion | flops 3932160 | bytes 1576960 | tf_op jit(solution)/shard_map/convert_element_type | solution.py:66
  6.3 0.2 fusion.25
  6.5 0.2 fusion.27
  6.7 0.2 fusion.28
  7.0 0.2 fusion.30
  7.2 0.2 fusion.31
  7.5 0.2 fusion.33
  7.7 1.5 %copy-done = bf16[3,3,3,256,256]{4,3,2,1,0:T(8,128)(2,1)S(1)} copy-done((bf16[3,3,3,256,256]{4,3,2,1,0:T(8,128)(2,1)S(1)}, bf16[3,3,3,256,256]{4,3,2,1,0:T(8,128)(2,1)}, u32[]{:S(2)}) %copy-start) | copy-done | bytes 3538968
  9.2 0.3 fusion.42
  9.6 2.1 %fusion.2 = f32[1536,256]{1,0:T(8,128)S(1)} fusion(bf16[2304,256]{1,0:T(8,128)(2,1)S(1)} %bitcast.55, bf16[1792,2304]{1,0:T(8,128)(2,1)S(1)} %bitcast.58), kind=kOutput, calls=%fused_computation.3 | convolution fusion | flops 1811939328 | bytes 9830400 | tf_op jit(solution)/shard_map/dot_general | solution.py:80
  11.7 2.1 %fusion.6 = f32[1536,256]{1,0:T(8,128)S(1)} fusion(f32[1536,256]{1,0:T(8,128)S(1)} %fusion.2, bf16[2304,256]{1,0:T(8,128)(2,1)S(1)} %bitcast.54, bf16[1792,2304]{1,0:T(8,128)(2,1)S(1)} %bitcast.59), kind=kOutput, calls=%fused_computation.16 | convolution fusion | flops 1812332544 | bytes 11403264 | tf_op jit(solution)/shard_map/dot_general | solution.py:80
  13.8 2.3 %fusion.12 = (f32[256]{0:T(256)S(1)}, f32[256]{0:T(256)S(1)}, f32[1536,256]{1,0:T(8,128)S(1)}) fusion(f32[1536]{0:T(1024)S(1)} %broadcast_bitcast_fusion, f32[256]{0:T(256)S(1)} %copy-done.2, f32[1536,256]{1,0:T(8,128)S(1)} %fusion.6, bf16[2304,256]{1,0:T(8,128)(2,1)S(1)} %bitcast.53, bf16[1792,2304]{1,0:T(8,128)(2,1)S(1)} %bitcast.60), kind=kOutput, calls=%fused_computation.23 | convolution fusion | flops 1815477760 | bytes 11414528 | tf_op jit(solution)/shard_map/dot_general | solution.py:80
  16.0 0.2 add_convert_fusion.1
  16.4 0.2 select_reduce_fusion.4
  18.3 1.0 %pad_maximum_fusion.1 = bf16[16,104,256]{2,1,0:T(8,128)(2,1)} fusion(bf16[16,8,256]{2,1,0:T(8,128)(2,1)S(1)} %broadcast_in_dim.144, bf16[16,96,256]{2,1,0:T(8,128)(2,1)S(1)} %broadcast_select_fusion), kind=kLoop, calls=%fused_computation.49 | loop fusion | flops 1703936 | bytes 1703936 | tf_op jit(solution)/shard_map/concatenate | solution.py:120
  19.3 6.7 %all-to-all-start = ((bf16[16,104,256]{2,1,0:T(8,128)(2,1)}), bf16[16,104,256]{2,1,0:T(8,128)(2,1)S(1)}, u32[]{:S(2)}, u32[]{:S(2)}) async-start(bf16[16,104,256]{2,1,0:T(8,128)(2,1)} %pad_maximum_fusion.1), calls=%async_computation | async-start | bytes 1703936 | tf_op jit(solution)/shard_map/all_to_all | solution.py:121
  26.4 20.5 %all-to-all-done = bf16[16,104,256]{2,1,0:T(8,128)(2,1)S(1)} async-done(((bf16[16,104,256]{2,1,0:T(8,128)(2,1)}), bf16[16,104,256]{2,1,0:T(8,128)(2,1)S(1)}, u32[]{:S(2)}, u32[]{:S(2)}) %all-to-all-start) | async-done | bytes 852000 | tf_op jit(solution)/shard_map/all_to_all | solution.py:121
  47.1 0.6 %multiply_convert_fusion = bf16[1,16,2,6,8,256]{5,4,3,2,1,0:T(8,128)(2,1)S(1)} fusion(bf16[1,16,2,6,8,256]{5,4,3,2,1,0:T(8,128)(2,1)S(1)} %bitcast.47, f32[256]{0:T(256)S(1)} %copy-done.3, f32[256]{0:T(256)S(1)} %copy-done.4, f32[16,256]{1,0:T(8,128)S(1)} %get-tuple-element.32, f32[16,256]{1,0:T(8,128)S(1)} %get-tuple-element.33), kind=kLoop, calls=%fused_computation.37 | loop fusion | flops 3932160 | bytes 1607680 | tf_op jit(solution)/shard_map/convert_element_type | solution.py:131
  47.6 0.1 pad_maximum_fusion
  47.8 0.6 %gather_fusion = bf16[128,8,256]{2,1,0:T(8,128)(2,1)S(1)} fusion(bf16[384,8,256]{2,1,0:T(8,128)(2,1)S(1)} %bitcast.51, s32[1024]{0:T(1024)S(1)} %pad_clamp_fusion), kind=kCustom, calls=%fused_computation | custom fusion | bytes 1049088 | tf_op jit(solution)/shard_map/jit(_take)/gather | solution.py:143
  48.4 0.8 %fusion.43 = (bf16[64,8,256]{2,1,0:T(8,128)(2,1)}, bf16[64,8,256]{2,1,0:T(8,128)(2,1)}) fusion(bf16[128,8,256]{2,1,0:T(8,128)(2,1)S(1)} %gather_fusion), kind=kLoop, calls=%fused_computation.120 | loop fusion | bytes 1048576 | tf_op jit(solution)/shard_map/slice | solution.py:144
  (67 shorter events, 3.4 us)
Async XLA Ops:
  0.6 4.4 %copy-start.1 = (bf16[12,16,8,256]{3,2,1,0:T(8,128)(2,1)S(1)}, bf16[12,16,8,256]{3,2,1,0:T(8,128)(2,1)}, u32[]{:S(2)}) copy-start(bf16[12,16,8,256]{3,2,1,0:T(8,128)(2,1)} %param.9) | copy-start | bytes 2359300
  7.2 2.0 %copy-start = (bf16[3,3,3,256,256]{4,3,2,1,0:T(8,128)(2,1)S(1)}, bf16[3,3,3,256,256]{4,3,2,1,0:T(8,128)(2,1)}, u32[]{:S(2)}) copy-start(bf16[3,3,3,256,256]{4,3,2,1,0:T(8,128)(2,1)} %param.14) | copy-start | bytes 10616836
  11.6 2.1 %copy-start.2 = (f32[256]{0:T(256)S(1)}, f32[256]{0:T(256)}, u32[]{:S(2)}) copy-start(f32[256]{0:T(256)} %param.15) | copy-start | bytes 3076
  19.3 27.8 %copy-start.3 = (f32[256]{0:T(256)S(1)}, f32[256]{0:T(256)}, u32[]{:S(2)}) copy-start(f32[256]{0:T(256)} %param.17) | copy-start | bytes 3076
  19.3 27.8 %copy-start.4 = (f32[256]{0:T(256)S(1)}, f32[256]{0:T(256)}, u32[]{:S(2)}) copy-start(f32[256]{0:T(256)} %param.16) | copy-start | bytes 3076
  19.3 27.6 %all-to-all-start = ((bf16[16,104,256]{2,1,0:T(8,128)(2,1)}), bf16[16,104,256]{2,1,0:T(8,128)(2,1)S(1)}, u32[]{:S(2)}, u32[]{:S(2)}) async-start(bf16[16,104,256]{2,1,0:T(8,128)(2,1)} %pad_maximum_fusion.1), calls=%async_computation | async-start | bytes 1703936 | tf_op jit(solution)/shard_map/all_to_all | solution.py:121

commit v15 on v14

--- a/solution.py
+++ b/solution.py
@@ -76,14 +76,14 @@
         axis=-1,
     ).reshape(frames + 2, frame_rows * columns, 9 * channels)
     kernel = conv_weight.reshape(3, 9 * channels, -1)
-    spread_out = [
-        jnp.dot(
-            unfolded.reshape(-1, 9 * channels), kernel[frame_lag], preferred_element_type=jnp.float32
-        ).reshape(frames + 2, frame_rows * columns, -1)
-        for frame_lag in range(3)
-    ]
+    spread_out = lax.dot_general(
+        unfolded.reshape(-1, 9 * channels),
+        kernel,
+        (((1,), (1,)), ((), ())),
+        preferred_element_type=jnp.float32,
+    ).reshape(frames + 2, frame_rows * columns, 3, -1)
     conv = conv_bias + sum(
-        spread_out[frame_lag][frame_lag : frame_lag + frames] for frame_lag in range(3)
+        spread_out[frame_lag : frame_lag + frames, :, frame_lag] for frame_lag in range(3)
     )
     conv = conv.reshape(frames, frame_rows, columns, -1)
     block_out = conv.astype(jnp.bfloat16)

time: 49.6 us -> 75.8 us (1.53)
  local copies, waits for them, and re-layouts: 6.38 us -> 20.4 us
  other arithmetic: 7.52 us -> 18.9 us
    broadcast_in_dim x4, local copies, waits for them, and re-layouts: 0.26 us -> 2.57 us  [local(): jnp.where((pick == lag)[None, :, None, None, None, None], tiles[:, lag:la...]
    gather x1, local copies, waits for them, and re-layouts: 0.65 us -> 2.86 us  [local(): jnp.take(both, jnp.stack([take_from, take_from + rows_all], 0), axis=0, m...]
    broadcast_in_dim x3, local copies, waits for them, and re-layouts: 0.17 us -> 1.91 us  [local(): chosen = jnp.broadcast_to(tiles[:, 0:1], tiles.shape)]
    reduce_sum x1 -> x2, other arithmetic: 0.12 us -> 1.8 us  [local(): first_sum = jnp.sum(grouped * live_mask, axis=(0, 1, 3))]
    reshape x1, local copies, waits for them, and re-layouts: 0.08 us -> 1.38 us  [normalize(): second.reshape(GROUPS, -1)]
    sub x2, local copies, waits for them, and re-layouts: 0.16 us -> 1.38 us  [normalize(): grouped - group_mean[:, None]]
    rsqrt x1, other arithmetic: 0.01 us -> 1.18 us  [normalize(): inverse = lax.rsqrt(spread + eps)]
    another operation x1, other arithmetic: 0.15 us -> 1.29 us  [local(): jnp.stack([block_part, normed_part], 0)]
  transfers between devices with their start and end apart: 1 -> 1, of which waited for: 1 -> 1; matrix products, arithmetic and copies ran while one was open for 1% -> 0% of each run, Pallas kernels for 0% -> 0%
where the time goes in v15:
time: 75.8 us; the launch traced here: 75 us
  waiting for transfers between devices  20.6 us (27%)
  local copies, waits for them, and re-layouts  20.4 us (27%)
  other arithmetic  18.9 us (25%)
  starting transfers between devices  6.75 us (9%)
  matrix products  6.74 us (9%)
  between operations  1.65 us (2%)
    all_to_all x1, waiting for transfers between devices, local(): lax.all_to_all(outgoing, 'tile', split_axis=0, concat_axis=0, tiled=True)  20.6 us
    all_to_all x1, starting transfers between devices, local(): lax.all_to_all(outgoing, 'tile', split_axis=0, concat_axis=0, tiled=True)  6.75 us
    dot_general x1, matrix products, local(): lax.dot_general(unfolded.reshape(-1, 9 * channels), kernel, (((1,), (1,))...  6.74 us
    gather x1, local copies, waits for them, and re-layouts, local(): jnp.take(both, jnp.stack([take_from, take_from + rows_all], 0), axis=0, m...  2.86 us
    broadcast_in_dim x4, local copies, waits for them, and re-layouts, local(): jnp.where((pick == lag)[None, :, None, None, None, None], tiles[:, lag:la...  2.57 us
    reduce_sum x2, other arithmetic, normalize(): second = jnp.sum(jnp.sum(flat * flat, axis=1) * live_mask, axis=0)  2.03 us
    broadcast_in_dim x3, local copies, waits for them, and re-layouts, local(): chosen = jnp.broadcast_to(tiles[:, 0:1], tiles.shape)  1.91 us
    slice x1, local copies, waits for them, and re-layouts, local(): return (picked[0], picked[1])  1.85 us
  transfers between devices with their start and end apart: 1, of which 1 were waited for; matrix products, arithmetic and copies ran while one was open for 0% of the time, Pallas kernels for 0%

profile of v15, /device:TPU:9, one launch (start us, length us, event | category | flops | bytes accessed | tf_op | source)
XLA Modules:
  0.0 75.0 jit_solution(10834156425786432430)
XLA Ops:
  0.6 0.8 %pad_add_fusion.1 = s32[2,16]{1,0:T(2,128)S(1)} fusion(s32[1,16]{1,0:T(1,128)} %bitcast.59, s32[1,16]{1,0:T(1,128)} %bitcast.60), kind=kLoop, calls=%fused_computation.93 | loop fusion | flops 32 | bytes 256 | tf_op jit(solution)/shard_map/stack | solution.py:50
  2.6 1.4 %fusion.14 = (f32[12,256]{1,0:T(8,128)S(1)}, f32[12,256]{1,0:T(8,128)S(1)}) fusion(bf16[12,16,8,256]{3,2,1,0:T(8,128)(2,1)} %param.9), kind=kLoop, calls=%fused_computation.29 | loop fusion | flops 1566720 | bytes 811008 | tf_op jit(solution)/shard_map/reduce_sum | solution.py:21
  5.3 0.8 %reshape.418 = f32[32,8]{1,0:T(8,128)S(1)} reshape(f32[256]{0:T(256)} %get-tuple-element.11) | data formatting | bytes 2048 | tf_op jit(solution)/shard_map/reshape | solution.py:22
  6.1 1.4 %reshape.419 = f32[32,8]{1,0:T(8,128)} reshape(f32[256]{0:T(256)} %get-tuple-element.10) | data formatting | bytes 2048 | tf_op jit(solution)/shard_map/reshape | solution.py:23
  8.1 0.8 %reduce_sum.162 = f32[32]{0:T(128)S(1)} reduce(f32[32,8]{1,0:T(8,128)} %reshape.419, f32[]{:T(128)} %constant.85.clone.1), dimensions={1}, to_apply=%region_10.11 | reduce | flops 224 | bytes 1156 | tf_op jit(solution)/shard_map/reduce_sum | solution.py:23
  9.6 1.2 %add_rsqrt_fusion = (f32[32]{0:T(128)S(1)}, f32[32]{0:T(128)}) fusion(f32[32]{0:T(128)S(1)} %reduce_sum.162, f32[]{:T(128)S(6)} %mul.183, f32[32]{0:T(128)} %reduce_sum.158), kind=kLoop, calls=%fused_computation.105 | loop fusion | flops 160 | bytes 516 | tf_op jit(solution)/shard_map/rsqrt | solution.py:24
  12.9 1.7 %fusion.13 = bf16[12,16,8,256]{3,2,1,0:T(8,128)(2,1)S(1)} fusion(bf16[12,16,8,256]{3,2,1,0:T(8,128)(2,1)} %param.9, f32[256]{0:T(256)} %param.13, f32[256]{0:T(256)} %param.12, f32[256]{0:T(256)} %mul.188, f32[256]{0:T(256)} %sub.104), kind=kLoop, calls=%fused_computation.28 | loop fusion | flops 3932160 | bytes 1576960 | tf_op jit(solution)/shard_map/convert_element_type | solution.py:66
  16.1 6.7 %fusion = f32[14,128,3,256]{3,1,2,0:T(8,128)S(1)} fusion(bf16[3,2304,256,1]{2,1,0,3:T(8,128)(2,1)S(1)} %bitcast.49, bf16[14,16,8,2304]{3,2,1,0:T(8,128)(2,1)S(1)} %fusion.23), kind=kOutput, calls=%fused_computation.1 | convolution fusion | flops 6341787648 | bytes 17301504 | tf_op jit(solution)/shard_map/dot_general | solution.py:79
  22.9 1.2 %fusion.2 = (f32[256]{0:T(256)}, f32[256]{0:T(256)}, f32[12,128,1,256]{3,1,2,0:T(8,128)S(1)}) fusion(f32[12]{0:T(128)S(1)} %copy-done.2, f32[256]{0:T(256)S(1)} %copy-done.3, f32[14,128,3,256]{3,1,2,0:T(8,128)S(1)} %fusion), kind=kLoop, calls=%fused_computation.17 | loop fusion | flops 3931648 | bytes 6294576 | tf_op jit(solution)/shard_map/reduce_sum | solution.py:94
  24.4 0.8 %copy.18 = bf16[8,2,6,8,256]{4,3,2,1,0:T(8,128)(2,1)} copy(bf16[8,2,6,8,256]{4,3,1,0,2:T(8,128)(2,1)S(1)} %get-tuple-element.18) | data formatting | bytes 786432 | tf_op jit(solution)/shard_map/jit(_where)/broadcast_in_dim | solution.py:107
  25.2 0.8 %copy.19 = bf16[8,2,6,8,256]{4,3,2,1,0:T(8,128)(2,1)} copy(bf16[8,2,6,8,256]{4,3,1,0,2:T(8,128)(2,1)S(1)} %get-tuple-element.17) | data formatting | bytes 786432 | tf_op jit(solution)/shard_map/broadcast_in_dim | solution.py:105
  26.8 1.2 %and_select_fusion.3 = (s32[16]{0:T(128)S(1)}, s32[16]{0:T(128)}) fusion(s32[16]{0:T(128)S(1)} %reduce.7, s32[16]{0:T(128)} %copy-done.7), kind=kLoop, calls=%fused_computation.79 | loop fusion | flops 448 | bytes 256 | tf_op jit(solution)/shard_map/jit(remainder)/select_n | solution.py:103
  28.0 0.8 %fusion.28 = s32[2]{0:T(128)S(1)} fusion(pred[16]{0:T(512)(128)(4,1)} %compare_bitcast_fusion, s32[16]{0:T(128)S(1)} %get-tuple-element.12), kind=kLoop, calls=%fused_computation.96 | loop fusion | flops 446 | bytes 88 | tf_op jit(solution)/shard_map/reduce_sum | solution.py:104
  34.3 0.8 %reshape.421 = f32[2,256]{1,0:T(2,128)S(1)} reshape(f32[2,32,8]{2,1,0:T(8,128)} %broadcast_in_dim.142) | data formatting | bytes 4096 | tf_op jit(solution)/shard_map/reshape | solution.py:115
  35.2 1.1 %broadcast_in_dim.136 = bf16[2,8,2,6,8,256]{5,4,3,2,1,0:T(8,128)(2,1)S(1)} broadcast(bf16[8,2,6,8,256]{4,3,2,1,0:T(8,128)(2,1)} %copy.18), dimensions={1,2,3,4,5} | broadcast | bytes 1179648 | tf_op jit(solution)/shard_map/jit(_where)/broadcast_in_dim | solution.py:107
  36.3 1.1 %broadcast_in_dim.140 = bf16[2,8,2,6,8,256]{5,4,3,2,1,0:T(8,128)(2,1)S(1)} broadcast(bf16[8,2,6,8,256]{4,3,2,1,0:T(8,128)(2,1)} %copy.19), dimensions={1,2,3,4,5} | broadcast | bytes 1179648 | tf_op jit(solution)/shard_map/broadcast_in_dim | solution.py:105
  37.6 1.0 %pad_maximum_fusion.1 = bf16[16,104,256]{2,1,0:T(8,128)(2,1)} fusion(bf16[16,8,256]{2,1,0:T(8,128)(2,1)S(1)} %broadcast_in_dim.144, bf16[16,96,256]{2,1,0:T(8,128)(2,1)S(1)} %broadcast_select_fusion), kind=kLoop, calls=%fused_computation.45 | loop fusion | flops 1703936 | bytes 1703936 | tf_op jit(solution)/shard_map/concatenate | solution.py:120
  38.6 6.7 %all-to-all-start = ((bf16[16,104,256]{2,1,0:T(8,128)(2,1)}), bf16[16,104,256]{2,1,0:T(8,128)(2,1)}, u32[]{:S(2)}, u32[]{:S(2)}) async-start(bf16[16,104,256]{2,1,0:T(8,128)(2,1)} %pad_maximum_fusion.1), calls=%async_computation | async-start | bytes 1703936 | tf_op jit(solution)/shard_map/all_to_all | solution.py:121
  45.7 20.6 %all-to-all-done = bf16[16,104,256]{2,1,0:T(8,128)(2,1)} async-done(((bf16[16,104,256]{2,1,0:T(8,128)(2,1)}), bf16[16,104,256]{2,1,0:T(8,128)(2,1)}, u32[]{:S(2)}, u32[]{:S(2)}) %all-to-all-start) | async-done | bytes 852000 | tf_op jit(solution)/shard_map/all_to_all | solution.py:121
  66.3 0.8 %slice_convert_fusion = f32[16,8,256]{2,1,0:T(8,128)S(1)} fusion(bf16[16,104,256]{2,1,0:T(8,128)(2,1)} %all-to-all-done), kind=kLoop, calls=%fused_computation.49 | loop fusion | flops 32768 | bytes 196608 | tf_op jit(solution)/shard_map/convert_element_type | solution.py:125
  67.2 1.2 %slice.105 = bf16[16,96,256]{2,1,0:T(8,128)(2,1)S(1)} slice(bf16[16,104,256]{2,1,0:T(8,128)(2,1)} %all-to-all-done), slice={[0:16], [0:96], [0:256]} | slice | bytes 1572864 | tf_op jit(solution)/shard_map/slice | solution.py:122
  69.0 1.3 %pad_maximum_fusion = bf16[2,16,2,6,8,256]{5,4,3,2,1,0:T(8,128)(2,1)} fusion(bf16[1,16,2,6,8,256]{5,4,3,2,1,0:T(8,128)(2,1)S(1)} %multiply_convert_fusion, bf16[1,16,2,6,8,256]{5,4,3,2,1,0:T(8,128)(2,1)S(1)} %bitcast.51), kind=kLoop, calls=%fused_computation.32 | loop fusion | flops 786432 | bytes 3145728 | tf_op jit(solution)/shard_map/stack | solution.py:142
  70.3 2.9 %gather_fusion = bf16[128,8,256]{2,1,0:T(8,128)(2,1)} fusion(bf16[384,8,256]{2,1,0:T(8,128)(2,1)} %bitcast.55, s32[1024]{0:T(1024)S(1)} %pad_clamp_fusion), kind=kCustom, calls=%fused_computation | custom fusion | bytes 1049088 | tf_op jit(solution)/shard_map/jit(_take)/gather | solution.py:143
  73.2 1.9 %fusion.32 = (bf16[64,8,256]{2,1,0:T(8,128)(2,1)}, bf16[64,8,256]{2,1,0:T(8,128)(2,1)}) fusion(bf16[128,8,256]{2,1,0:T(8,128)(2,1)} %gather_fusion), kind=kLoop, calls=%fused_computation.114 | loop fusion | bytes 1048576 | tf_op jit(solution)/shard_map/slice | solution.py:144
  (80 shorter events, 14.5 us)
Async XLA Ops:
  0.6 15.4 %copy-start = (bf16[3,3,3,256,256]{4,3,2,1,0:T(8,128)(2,1)S(1)}, bf16[3,3,3,256,256]{4,3,2,1,0:T(8,128)(2,1)}, u32[]{:S(2)}) copy-start(bf16[3,3,3,256,256]{4,3,2,1,0:T(8,128)(2,1)} %param.14) | copy-start | bytes 10616836
  2.0 3.3 %copy-start.8 = (s32[16]{0:T(128)}, s32[16]{0:T(128)S(1)}, u32[]{:S(2)}) copy-start(s32[16]{0:T(128)S(1)} %get-tuple-element.28) | copy-start | bytes 196
  4.7 0.7 copy-start.1
  16.1 6.8 %copy-start.2 = (f32[12]{0:T(128)S(1)}, f32[12]{0:T(128)}, u32[]{:S(2)}) copy-start(f32[12]{0:T(128)} %copy-done.1) | copy-start | bytes 148
  16.1 6.8 %copy-start.3 = (f32[256]{0:T(256)S(1)}, f32[256]{0:T(256)}, u32[]{:S(2)}) copy-start(f32[256]{0:T(256)} %param.15) | copy-start | bytes 3076
  24.3 1.6 %copy-start.4 = (s32[16]{0:T(128)S(1)}, s32[16]{0:T(128)}, u32[]{:S(2)}) copy-start(s32[16]{0:T(128)} %get-tuple-element.27) | copy-start | bytes 196
  24.3 1.6 %copy-start.9 = (s32[16]{0:T(128)S(1)}, s32[16]{0:T(128)}, u32[]{:S(2)}) copy-start(s32[16]{0:T(128)} %copy-done.8) | copy-start | bytes 196
  26.1 0.5 copy-start.7
  32.3 5.1 %copy-start.12 = (pred[16]{0:T(512)(128)(4,1)S(1)}, pred[16]{0:T(512)(128)(4,1)}, u32[]{:S(2)}) copy-start(pred[16]{0:T(512)(128)(4,1)} %broadcast_in_dim.130) | copy-start | bytes 52
  37.6 7.7 %copy-start.6 = (s32[16]{0:T(128)S(1)}, s32[16]{0:T(128)}, u32[]{:S(2)}) copy-start(s32[16]{0:T(128)} %get-tuple-element.13) | copy-start | bytes 196
  37.6 7.9 %copy-start.5 = (s32[16]{0:T(128)S(1)}, s32[16]{0:T(128)}, u32[]{:S(2)}) copy-start(s32[16]{0:T(128)} %get-tuple-element.27) | copy-start | bytes 196
  38.6 29.8 %copy-start.10 = (f32[256]{0:T(256)S(1)}, f32[256]{0:T(256)}, u32[]{:S(2)}) copy-start(f32[256]{0:T(256)} %param.17) | copy-start | bytes 3076
  38.6 29.8 %copy-start.11 = (f32[256]{0:T(256)S(1)}, f32[256]{0:T(256)}, u32[]{:S(2)}) copy-start(f32[256]{0:T(256)} %param.16) | copy-start | bytes 3076
  38.6 27.7 %all-to-all-start = ((bf16[16,104,256]{2,1,0:T(8,128)(2,1)}), bf16[16,104,256]{2,1,0:T(8,128)(2,1)}, u32[]{:S(2)}, u32[]{:S(2)}) async-start(bf16[16,104,256]{2,1,0:T(8,128)(2,1)} %pad_maximum_fusion.1), calls=%async_computation | async-start | bytes 1703936 | tf_op jit(solution)/shard_map/all_to_all | solution.py:121

commit v16 on v15

--- a/solution.py
+++ b/solution.py
@@ -76,14 +76,15 @@
         axis=-1,
     ).reshape(frames + 2, frame_rows * columns, 9 * channels)
     kernel = conv_weight.reshape(3, 9 * channels, -1)
+    flat_in = unfolded.reshape(-1, 9 * channels)
     spread_out = lax.dot_general(
-        unfolded.reshape(-1, 9 * channels),
+        jnp.broadcast_to(flat_in[None], (3,) + flat_in.shape),
         kernel,
-        (((1,), (1,)), ((), ())),
+        (((2,), (1,)), ((0,), (0,))),
         preferred_element_type=jnp.float32,
-    ).reshape(frames + 2, frame_rows * columns, 3, -1)
+    ).reshape(3, frames + 2, frame_rows * columns, -1)
     conv = conv_bias + sum(
-        spread_out[frame_lag : frame_lag + frames, :, frame_lag] for frame_lag in range(3)
+        spread_out[frame_lag, frame_lag : frame_lag + frames] for frame_lag in range(3)
     )
     conv = conv.reshape(frames, frame_rows, columns, -1)
     block_out = conv.astype(jnp.bfloat16)

time: 75.8 us -> 75.8 us (level)
  no operation moved by 1% of the time
where the time goes in v16:
time: 75.8 us; the launch traced here: 75 us
  waiting for transfers between devices  20.6 us (27%)
  local copies, waits for them, and re-layouts  20.4 us (27%)
  other arithmetic  18.9 us (25%)
  matrix products  6.76 us (9%)
  starting transfers between devices  6.74 us (9%)
  between operations  1.65 us (2%)
    all_to_all x1, waiting for transfers between devices, local(): lax.all_to_all(outgoing, 'tile', split_axis=0, concat_axis=0, tiled=True)  20.6 us
    dot_general x1, matrix products, local(): lax.dot_general(jnp.broadcast_to(flat_in[None], (3,) + flat_in.shape), ke...  6.76 us
    all_to_all x1, starting transfers between devices, local(): lax.all_to_all(outgoing, 'tile', split_axis=0, concat_axis=0, tiled=True)  6.74 us
    gather x1, local copies, waits for them, and re-layouts, local(): jnp.take(both, jnp.stack([take_from, take_from + rows_all], 0), axis=0, m...  2.86 us
    broadcast_in_dim x4, local copies, waits for them, and re-layouts, local(): jnp.where((pick == lag)[None, :, None, None, None, None], tiles[:, lag:la...  2.57 us
    reduce_sum x2, other arithmetic, normalize(): second = jnp.sum(jnp.sum(flat * flat, axis=1) * live_mask, axis=0)  2.03 us
    broadcast_in_dim x3, local copies, waits for them, and re-layouts, local(): chosen = jnp.broadcast_to(tiles[:, 0:1], tiles.shape)  1.91 us
    slice x1, local copies, waits for them, and re-layouts, local(): return (picked[0], picked[1])  1.85 us
  transfers between devices with their start and end apart: 1, of which 1 were waited for; matrix products, arithmetic and copies ran while one was open for 0% of the time, Pallas kernels for 0%

profile of v16, /device:TPU:9, one launch (start us, length us, event | category | flops | bytes accessed | tf_op | source)
XLA Modules:
  0.0 75.0 jit_solution(17440989225116251335)
XLA Ops:
  0.6 0.8 %pad_add_fusion.1 = s32[2,16]{1,0:T(2,128)S(1)} fusion(s32[1,16]{1,0:T(1,128)} %bitcast.54, s32[1,16]{1,0:T(1,128)} %bitcast.55), kind=kLoop, calls=%fused_computation.93 | loop fusion | flops 32 | bytes 256 | tf_op jit(solution)/shard_map/stack | solution.py:50
  2.6 1.4 %fusion.14 = (f32[12,256]{1,0:T(8,128)S(1)}, f32[12,256]{1,0:T(8,128)S(1)}) fusion(bf16[12,16,8,256]{3,2,1,0:T(8,128)(2,1)} %param.9), kind=kLoop, calls=%fused_computation.29 | loop fusion | flops 1566720 | bytes 811008 | tf_op jit(solution)/shard_map/reduce_sum | solution.py:21
  5.3 0.8 %reshape.419 = f32[32,8]{1,0:T(8,128)S(1)} reshape(f32[256]{0:T(256)} %get-tuple-element.11) | data formatting | bytes 2048 | tf_op jit(solution)/shard_map/reshape | solution.py:22
  6.1 1.4 %reshape.420 = f32[32,8]{1,0:T(8,128)} reshape(f32[256]{0:T(256)} %get-tuple-element.10) | data formatting | bytes 2048 | tf_op jit(solution)/shard_map/reshape | solution.py:23
  8.1 0.8 %reduce_sum.162 = f32[32]{0:T(128)S(1)} reduce(f32[32,8]{1,0:T(8,128)} %reshape.420, f32[]{:T(128)} %constant.85.clone.1), dimensions={1}, to_apply=%region_10.11 | reduce | flops 224 | bytes 1156 | tf_op jit(solution)/shard_map/reduce_sum | solution.py:23
  9.6 1.2 %add_rsqrt_fusion = (f32[32]{0:T(128)S(1)}, f32[32]{0:T(128)}) fusion(f32[32]{0:T(128)S(1)} %reduce_sum.162, f32[]{:T(128)S(6)} %mul.183, f32[32]{0:T(128)} %reduce_sum.158), kind=kLoop, calls=%fused_computation.105 | loop fusion | flops 160 | bytes 516 | tf_op jit(solution)/shard_map/rsqrt | solution.py:24
  12.9 1.7 %fusion.13 = bf16[12,16,8,256]{3,2,1,0:T(8,128)(2,1)S(1)} fusion(bf16[12,16,8,256]{3,2,1,0:T(8,128)(2,1)} %param.9, f32[256]{0:T(256)} %param.13, f32[256]{0:T(256)} %param.12, f32[256]{0:T(256)} %mul.188, f32[256]{0:T(256)} %sub.104), kind=kLoop, calls=%fused_computation.28 | loop fusion | flops 3932160 | bytes 1576960 | tf_op jit(solution)/shard_map/convert_element_type | solution.py:66
  16.1 6.8 %fusion = f32[3,1792,256]{2,1,0:T(8,128)S(1)} fusion(bf16[3,2304,256]{2,1,0:T(8,128)(2,1)S(1)} %bitcast.42, bf16[1792,2304]{1,0:T(8,128)(2,1)S(1)} %bitcast.52), kind=kOutput, calls=%fused_computation.1 | convolution fusion | flops 6341787648 | bytes 17301504 | tf_op jit(solution)/shard_map/dot_general | solution.py:80
  22.9 1.2 %fusion.2 = (f32[256]{0:T(256)}, f32[256]{0:T(256)}, f32[1,12,128,256]{3,2,1,0:T(8,128)S(1)}) fusion(f32[12]{0:T(128)S(1)} %copy-done.2, f32[256]{0:T(256)S(1)} %copy-done.3, f32[3,14,128,256]{3,2,1,0:T(8,128)S(1)} %bitcast.46), kind=kLoop, calls=%fused_computation.17 | loop fusion | flops 3931648 | bytes 6294576 | tf_op jit(solution)/shard_map/reduce_sum | solution.py:95
  24.4 0.8 %copy.18 = bf16[8,2,6,8,256]{4,3,2,1,0:T(8,128)(2,1)} copy(bf16[8,2,6,8,256]{4,3,1,0,2:T(8,128)(2,1)S(1)} %get-tuple-element.18) | data formatting | bytes 786432 | tf_op jit(solution)/shard_map/jit(_where)/broadcast_in_dim | solution.py:108
  25.2 0.8 %copy.19 = bf16[8,2,6,8,256]{4,3,2,1,0:T(8,128)(2,1)} copy(bf16[8,2,6,8,256]{4,3,1,0,2:T(8,128)(2,1)S(1)} %get-tuple-element.17) | data formatting | bytes 786432 | tf_op jit(solution)/shard_map/broadcast_in_dim | solution.py:106
  26.8 1.2 %and_select_fusion.3 = (s32[16]{0:T(128)S(1)}, s32[16]{0:T(128)}) fusion(s32[16]{0:T(128)S(1)} %reduce.7, s32[16]{0:T(128)} %copy-done.7), kind=kLoop, calls=%fused_computation.79 | loop fusion | flops 448 | bytes 256 | tf_op jit(solution)/shard_map/jit(remainder)/select_n | solution.py:104
  28.0 0.8 %fusion.28 = s32[2]{0:T(128)S(1)} fusion(pred[16]{0:T(512)(128)(4,1)} %compare_bitcast_fusion, s32[16]{0:T(128)S(1)} %get-tuple-element.12), kind=kLoop, calls=%fused_computation.96 | loop fusion | flops 446 | bytes 88 | tf_op jit(solution)/shard_map/reduce_sum | solution.py:105
  34.3 0.8 %reshape.423 = f32[2,256]{1,0:T(2,128)S(1)} reshape(f32[2,32,8]{2,1,0:T(8,128)} %broadcast_in_dim.151) | data formatting | bytes 4096 | tf_op jit(solution)/shard_map/reshape | solution.py:116
  35.2 1.1 %broadcast_in_dim.145 = bf16[2,8,2,6,8,256]{5,4,3,2,1,0:T(8,128)(2,1)S(1)} broadcast(bf16[8,2,6,8,256]{4,3,2,1,0:T(8,128)(2,1)} %copy.18), dimensions={1,2,3,4,5} | broadcast | bytes 1179648 | tf_op jit(solution)/shard_map/jit(_where)/broadcast_in_dim | solution.py:108
  36.3 1.1 %broadcast_in_dim.149 = bf16[2,8,2,6,8,256]{5,4,3,2,1,0:T(8,128)(2,1)S(1)} broadcast(bf16[8,2,6,8,256]{4,3,2,1,0:T(8,128)(2,1)} %copy.19), dimensions={1,2,3,4,5} | broadcast | bytes 1179648 | tf_op jit(solution)/shard_map/broadcast_in_dim | solution.py:106
  37.6 1.0 %pad_maximum_fusion.1 = bf16[16,104,256]{2,1,0:T(8,128)(2,1)} fusion(bf16[16,8,256]{2,1,0:T(8,128)(2,1)S(1)} %broadcast_in_dim.153, bf16[16,96,256]{2,1,0:T(8,128)(2,1)S(1)} %broadcast_select_fusion), kind=kLoop, calls=%fused_computation.45 | loop fusion | flops 1703936 | bytes 1703936 | tf_op jit(solution)/shard_map/concatenate | solution.py:121
  38.6 6.7 %all-to-all-start = ((bf16[16,104,256]{2,1,0:T(8,128)(2,1)}), bf16[16,104,256]{2,1,0:T(8,128)(2,1)}, u32[]{:S(2)}, u32[]{:S(2)}) async-start(bf16[16,104,256]{2,1,0:T(8,128)(2,1)} %pad_maximum_fusion.1), calls=%async_computation | async-start | bytes 1703936 | tf_op jit(solution)/shard_map/all_to_all | solution.py:122
  45.7 20.6 %all-to-all-done = bf16[16,104,256]{2,1,0:T(8,128)(2,1)} async-done(((bf16[16,104,256]{2,1,0:T(8,128)(2,1)}), bf16[16,104,256]{2,1,0:T(8,128)(2,1)}, u32[]{:S(2)}, u32[]{:S(2)}) %all-to-all-start) | async-done | bytes 852000 | tf_op jit(solution)/shard_map/all_to_all | solution.py:122
  66.3 0.8 %slice_convert_fusion = f32[16,8,256]{2,1,0:T(8,128)S(1)} fusion(bf16[16,104,256]{2,1,0:T(8,128)(2,1)} %all-to-all-done), kind=kLoop, calls=%fused_computation.49 | loop fusion | flops 32768 | bytes 196608 | tf_op jit(solution)/shard_map/convert_element_type | solution.py:126
  67.2 1.2 %slice.105 = bf16[16,96,256]{2,1,0:T(8,128)(2,1)S(1)} slice(bf16[16,104,256]{2,1,0:T(8,128)(2,1)} %all-to-all-done), slice={[0:16], [0:96], [0:256]} | slice | bytes 1572864 | tf_op jit(solution)/shard_map/slice | solution.py:123
  69.0 1.3 %pad_maximum_fusion = bf16[2,16,2,6,8,256]{5,4,3,2,1,0:T(8,128)(2,1)} fusion(bf16[1,16,2,6,8,256]{5,4,3,2,1,0:T(8,128)(2,1)S(1)} %multiply_convert_fusion, bf16[1,16,2,6,8,256]{5,4,3,2,1,0:T(8,128)(2,1)S(1)} %bitcast.44), kind=kLoop, calls=%fused_computation.32 | loop fusion | flops 786432 | bytes 3145728 | tf_op jit(solution)/shard_map/stack | solution.py:143
  70.3 2.9 %gather_fusion = bf16[128,8,256]{2,1,0:T(8,128)(2,1)} fusion(bf16[384,8,256]{2,1,0:T(8,128)(2,1)} %bitcast.49, s32[1024]{0:T(1024)S(1)} %pad_clamp_fusion), kind=kCustom, calls=%fused_computation | custom fusion | bytes 1049088 | tf_op jit(solution)/shard_map/jit(_take)/gather | solution.py:144
  73.2 1.9 %fusion.32 = (bf16[64,8,256]{2,1,0:T(8,128)(2,1)}, bf16[64,8,256]{2,1,0:T(8,128)(2,1)}) fusion(bf16[128,8,256]{2,1,0:T(8,128)(2,1)} %gather_fusion), kind=kLoop, calls=%fused_computation.114 | loop fusion | bytes 1048576 | tf_op jit(solution)/shard_map/slice | solution.py:145
  (80 shorter events, 14.5 us)
Async XLA Ops:
  0.6 15.4 %copy-start = (bf16[3,3,3,256,256]{4,3,2,1,0:T(8,128)(2,1)S(1)}, bf16[3,3,3,256,256]{4,3,2,1,0:T(8,128)(2,1)}, u32[]{:S(2)}) copy-start(bf16[3,3,3,256,256]{4,3,2,1,0:T(8,128)(2,1)} %param.14) | copy-start | bytes 10616836
  2.0 3.3 %copy-start.8 = (s32[16]{0:T(128)}, s32[16]{0:T(128)S(1)}, u32[]{:S(2)}) copy-start(s32[16]{0:T(128)S(1)} %get-tuple-element.28) | copy-start | bytes 196
  4.7 0.7 copy-start.1
  16.1 6.8 %copy-start.2 = (f32[12]{0:T(128)S(1)}, f32[12]{0:T(128)}, u32[]{:S(2)}) copy-start(f32[12]{0:T(128)} %copy-done.1) | copy-start | bytes 148
  16.1 6.8 %copy-start.3 = (f32[256]{0:T(256)S(1)}, f32[256]{0:T(256)}, u32[]{:S(2)}) copy-start(f32[256]{0:T(256)} %param.15) | copy-start | bytes 3076
  24.3 1.6 %copy-start.4 = (s32[16]{0:T(128)S(1)}, s32[16]{0:T(128)}, u32[]{:S(2)}) copy-start(s32[16]{0:T(128)} %get-tuple-element.27) | copy-start | bytes 196
  24.3 1.6 %copy-start.9 = (s32[16]{0:T(128)S(1)}, s32[16]{0:T(128)}, u32[]{:S(2)}) copy-start(s32[16]{0:T(128)} %copy-done.8) | copy-start | bytes 196
  26.1 0.5 copy-start.7
  32.3 5.1 %copy-start.12 = (pred[16]{0:T(512)(128)(4,1)S(1)}, pred[16]{0:T(512)(128)(4,1)}, u32[]{:S(2)}) copy-start(pred[16]{0:T(512)(128)(4,1)} %broadcast_in_dim.137) | copy-start | bytes 52
  37.6 7.7 %copy-start.6 = (s32[16]{0:T(128)S(1)}, s32[16]{0:T(128)}, u32[]{:S(2)}) copy-start(s32[16]{0:T(128)} %get-tuple-element.13) | copy-start | bytes 196
  37.6 7.8 %copy-start.5 = (s32[16]{0:T(128)S(1)}, s32[16]{0:T(128)}, u32[]{:S(2)}) copy-start(s32[16]{0:T(128)} %get-tuple-element.27) | copy-start | bytes 196
  38.6 29.8 %copy-start.10 = (f32[256]{0:T(256)S(1)}, f32[256]{0:T(256)}, u32[]{:S(2)}) copy-start(f32[256]{0:T(256)} %param.17) | copy-start | bytes 3076
  38.6 29.8 %copy-start.11 = (f32[256]{0:T(256)S(1)}, f32[256]{0:T(256)}, u32[]{:S(2)}) copy-start(f32[256]{0:T(256)} %param.16) | copy-start | bytes 3076
  38.6 27.7 %all-to-all-start = ((bf16[16,104,256]{2,1,0:T(8,128)(2,1)}), bf16[16,104,256]{2,1,0:T(8,128)(2,1)}, u32[]{:S(2)}, u32[]{:S(2)}) async-start(bf16[16,104,256]{2,1,0:T(8,128)(2,1)} %pad_maximum_fusion.1), calls=%async_computation | async-start | bytes 1703936 | tf_op jit(solution)/shard_map/all_to_all | solution.py:122

commit v17 on v14

--- a/solution.py
+++ b/solution.py
@@ -66,7 +66,7 @@
     active = normalize(latents.astype(jnp.float32), live_frames, norm_scale, norm_offset).astype(
         jnp.bfloat16
     )
-    padded = jnp.pad(active, ((2, 0), (1, 1), (1, 1), (0, 0)))
+    padded = jnp.pad(active, ((0, 0), (1, 1), (1, 1), (0, 0)))
     unfolded = jnp.concatenate(
         [
             padded[:, row_tap : row_tap + frame_rows, col_tap : col_tap + columns]
@@ -74,17 +74,18 @@
             for col_tap in range(3)
         ],
         axis=-1,
-    ).reshape(frames + 2, frame_rows * columns, 9 * channels)
+    ).reshape(frames * frame_rows * columns, 9 * channels)
     kernel = conv_weight.reshape(3, 9 * channels, -1)
     spread_out = [
-        jnp.dot(
-            unfolded.reshape(-1, 9 * channels), kernel[frame_lag], preferred_element_type=jnp.float32
-        ).reshape(frames + 2, frame_rows * columns, -1)
+        jnp.pad(
+            jnp.dot(unfolded, kernel[frame_lag], preferred_element_type=jnp.float32).reshape(
+                frames, frame_rows * columns, -1
+            ),
+            ((2 - frame_lag, 0), (0, 0), (0, 0)),
+        )[:frames]
         for frame_lag in range(3)
     ]
-    conv = conv_bias + sum(
-        spread_out[frame_lag][frame_lag : frame_lag + frames] for frame_lag in range(3)
-    )
+    conv = conv_bias + sum(spread_out)
     conv = conv.reshape(frames, frame_rows, columns, -1)
     block_out = conv.astype(jnp.bfloat16)
     per_group = channels // GROUPS

time: 49.6 us -> 49.9 us (level)
    dot_general x3 -> x1, matrix products: 6.43 us -> 2 us  [local(): jnp.dot(unfolded, kernel[frame_lag], preferred_element_type=jnp.float32)]
    slice x0 -> x2, matrix products: none -> 4.21 us  [local(): jnp.pad(jnp.dot(unfolded, kernel[frame_lag], preferred_element_type=jnp.f...]
    unnamed x0 -> x1, other arithmetic: none -> 0.55 us
    unnamed x19 -> x22, local copies, waits for them, and re-layouts: 2.73 us -> 2.92 us
where the time goes in v17:
time: 49.9 us; the launch traced here: 49.5 us
  waiting for transfers between devices  20.5 us (41%)
  other arithmetic  7.83 us (16%)
  starting transfers between devices  6.74 us (14%)
  local copies, waits for them, and re-layouts  6.52 us (13%)
  matrix products  6.22 us (12%)
  between operations  1.68 us (3%)
    all_to_all x1, waiting for transfers between devices, local(): lax.all_to_all(outgoing, 'tile', split_axis=0, concat_axis=0, tiled=True)  20.5 us
    all_to_all x1, starting transfers between devices, local(): lax.all_to_all(outgoing, 'tile', split_axis=0, concat_axis=0, tiled=True)  6.74 us
    slice x2, matrix products, local(): jnp.pad(jnp.dot(unfolded, kernel[frame_lag], preferred_element_type=jnp.f...  4.21 us
    unnamed x22, local copies, waits for them, and re-layouts  2.92 us
    dot_general x1, matrix products, local(): jnp.dot(unfolded, kernel[frame_lag], preferred_element_type=jnp.float32)  2 us
    reduce_sum x2, other arithmetic, normalize(): second = jnp.sum(jnp.sum(flat * flat, axis=1) * live_mask, axis=0)  1.47 us
    convert_element_type x1, other arithmetic, local(): normalize(latents.astype(jnp.float32), live_frames, norm_scale, norm_offset)  1.24 us
  transfers between devices with their start and end apart: 1, of which 1 were waited for; matrix products, arithmetic and copies ran while one was open for 1% of the time, Pallas kernels for 0%

profile of v17, /device:TPU:9, one launch (start us, length us, event | category | flops | bytes accessed | tf_op | source)
XLA Modules:
  0.0 49.5 jit_solution(3649429856643478797)
XLA Ops:
  0.6 0.8 %pad_add_fusion.1 = s32[2,16]{1,0:T(2,128)S(1)} fusion(s32[1,16]{1,0:T(1,128)} %bitcast.73, s32[1,16]{1,0:T(1,128)} %bitcast.74), kind=kLoop, calls=%fused_computation.93 | loop fusion | flops 32 | bytes 256 | tf_op jit(solution)/shard_map/stack | solution.py:50
  1.4 1.4 %fusion.18 = (f32[12,256]{1,0:T(8,128)S(1)}, f32[12,256]{1,0:T(8,128)S(1)}) fusion(bf16[12,16,8,256]{3,2,1,0:T(8,128)(2,1)} %param.9), kind=kLoop, calls=%fused_computation.32 | loop fusion | flops 1566720 | bytes 811008 | tf_op jit(solution)/shard_map/reduce_sum | solution.py:21
  2.8 0.6 %select_reduce_fusion = (f32[]{:T(128)}, f32[12]{0:T(128)S(1)}) fusion(s32[16]{0:T(128)S(1)} %get-tuple-element.30, pred[16]{0:T(512)(128)(4,1)S(1)} %iota_compare_fusion.3), kind=kLoop, calls=%fused_computation.56 | loop fusion | flops 947 | bytes 132 | tf_op jit(solution)/shard_map/reduce_sum | solution.py:19
  4.9 1.2 %fusion.17 = bf16[12,16,8,256]{3,2,1,0:T(8,128)(2,1)S(1)} fusion(bf16[12,16,8,256]{3,2,1,0:T(8,128)(2,1)S(1)} %copy-done, f32[256]{0:T(256)} %param.13, f32[256]{0:T(256)} %param.12, f32[256]{0:T(256)S(1)} %mul.188, f32[256]{0:T(256)S(1)} %sub.104), kind=kLoop, calls=%fused_computation.31 | loop fusion | flops 3932160 | bytes 1576960 | tf_op jit(solution)/shard_map/convert_element_type | solution.py:66
  6.2 0.2 fusion.21
  6.5 0.2 fusion.23
  6.7 0.2 fusion.24
  6.8 0.3 copy-done.2
  7.1 0.5 %constant_dynamic-update-slice_fusion = bf16[12,16,8,2304]{3,2,1,0:T(8,128)(2,1)S(1)} fusion(bf16[12,16,8,2304]{3,2,1,0:T(8,128)(2,1)S(1)} %fusion.24, f32[256]{0:T(256)S(1)} %copy-done.2, f32[256]{0:T(256)S(1)} %copy-done.3, f32[256]{0:T(256)S(1)} %mul.188, f32[256]{0:T(256)S(1)} %sub.104, bf16[12,16,8,256]{3,2,1,0:T(8,128)(2,1)S(1)} %copy-done), kind=kLoop, calls=%fused_computation.49 | loop fusion | flops 3932160 | bytes 1576960
  7.7 0.2 fusion.25
  7.9 0.2 fusion.26
  8.2 0.2 fusion.28
  8.4 1.5 %copy-done.1 = bf16[3,3,3,256,256]{4,3,2,1,0:T(8,128)(2,1)S(1)} copy-done((bf16[3,3,3,256,256]{4,3,2,1,0:T(8,128)(2,1)S(1)}, bf16[3,3,3,256,256]{4,3,2,1,0:T(8,128)(2,1)}, u32[]{:S(2)}) %copy-start.1) | copy-done | bytes 3538968
  9.9 0.4 fusion.37
  10.3 2.0 %fusion.2 = f32[12,128,256]{2,1,0:T(8,128)S(1)} fusion(bf16[2304,256,1]{1,0,2:T(8,128)(2,1)S(1)} %bitcast.68, bf16[12,16,8,2304]{3,2,1,0:T(8,128)(2,1)S(1)} %fusion.28), kind=kOutput, calls=%fused_computation.3 | convolution fusion | flops 1660944384 | bytes 9830400 | tf_op jit(solution)/shard_map/slice | solution.py:80
  12.3 2.0 %fusion = f32[12,128,256]{2,1,0:T(8,128)S(1)} fusion(bf16[2304,256,1]{1,0,2:T(8,128)(2,1)S(1)} %bitcast.67, bf16[12,16,8,2304]{3,2,1,0:T(8,128)(2,1)S(1)} %fusion.28), kind=kOutput, calls=%fused_computation.1 | convolution fusion | flops 1811939328 | bytes 9830400 | tf_op jit(solution)/shard_map/dot_general | solution.py:81
  14.3 2.2 %fusion.6 = (f32[256]{0:T(256)S(1)}, f32[256]{0:T(256)S(1)}, bf16[12,128,256]{2,1,0:T(8,128)(2,1)S(1)}) fusion(f32[12]{0:T(128)S(1)} %get-tuple-element.7, f32[12,128,256]{2,1,0:T(8,128)S(1)} %fusion, f32[12,128,256]{2,1,0:T(8,128)S(1)} %fusion.2, bf16[2304,256,1]{1,0,2:T(8,128)(2,1)S(1)} %bitcast.66, bf16[12,16,8,2304]{3,2,1,0:T(8,128)(2,1)S(1)} %fusion.28, ...), kind=kOutput, calls=%fused_computation.20 | convolution fusion | flops 1513881088 | bytes 12192816 | tf_op jit(solution)/shard_map/slice | solution.py:80
  16.7 0.2 select_reduce_fusion.4
  18.6 1.0 %pad_maximum_fusion.1 = bf16[16,104,256]{2,1,0:T(8,128)(2,1)} fusion(bf16[16,8,256]{2,1,0:T(8,128)(2,1)S(1)} %broadcast_in_dim.144, bf16[16,96,256]{2,1,0:T(8,128)(2,1)S(1)} %broadcast_select_fusion), kind=kLoop, calls=%fused_computation.36 | loop fusion | flops 1703936 | bytes 1703936 | tf_op jit(solution)/shard_map/concatenate | solution.py:121
  19.5 6.7 %all-to-all-start = ((bf16[16,104,256]{2,1,0:T(8,128)(2,1)}), bf16[16,104,256]{2,1,0:T(8,128)(2,1)S(1)}, u32[]{:S(2)}, u32[]{:S(2)}) async-start(bf16[16,104,256]{2,1,0:T(8,128)(2,1)} %pad_maximum_fusion.1), calls=%async_computation | async-start | bytes 1703936 | tf_op jit(solution)/shard_map/all_to_all | solution.py:122
  26.6 20.5 %all-to-all-done = bf16[16,104,256]{2,1,0:T(8,128)(2,1)S(1)} async-done(((bf16[16,104,256]{2,1,0:T(8,128)(2,1)}), bf16[16,104,256]{2,1,0:T(8,128)(2,1)S(1)}, u32[]{:S(2)}, u32[]{:S(2)}) %all-to-all-start) | async-done | bytes 852000 | tf_op jit(solution)/shard_map/all_to_all | solution.py:122
  47.3 0.6 %multiply_convert_fusion = bf16[1,16,2,6,8,256]{5,4,3,2,1,0:T(8,128)(2,1)S(1)} fusion(bf16[1,16,2,6,8,256]{5,4,3,2,1,0:T(8,128)(2,1)S(1)} %bitcast.61, f32[256]{0:T(256)S(1)} %copy-done.4, f32[256]{0:T(256)S(1)} %copy-done.5, f32[16,256]{1,0:T(8,128)S(1)} %get-tuple-element.32, f32[16,256]{1,0:T(8,128)S(1)} %get-tuple-element.33), kind=kLoop, calls=%fused_computation.34 | loop fusion | flops 3932160 | bytes 1607680 | tf_op jit(solution)/shard_map/convert_element_type | solution.py:132
  48.0 0.6 %gather_fusion = bf16[128,8,256]{2,1,0:T(8,128)(2,1)S(1)} fusion(bf16[384,8,256]{2,1,0:T(8,128)(2,1)S(1)} %bitcast.65, s32[1024]{0:T(1024)S(1)} %pad_clamp_fusion), kind=kCustom, calls=%fused_computation | custom fusion | bytes 1049088 | tf_op jit(solution)/shard_map/jit(_take)/gather | solution.py:144
  48.7 0.8 %fusion.38 = (bf16[64,8,256]{2,1,0:T(8,128)(2,1)}, bf16[64,8,256]{2,1,0:T(8,128)(2,1)}) fusion(bf16[128,8,256]{2,1,0:T(8,128)(2,1)S(1)} %gather_fusion), kind=kLoop, calls=%fused_computation.115 | loop fusion | bytes 1048576 | tf_op jit(solution)/shard_map/slice | solution.py:145
  (69 shorter events, 3.4 us)
Async XLA Ops:
  0.6 4.3 %copy-start = (bf16[12,16,8,256]{3,2,1,0:T(8,128)(2,1)S(1)}, bf16[12,16,8,256]{3,2,1,0:T(8,128)(2,1)}, u32[]{:S(2)}) copy-start(bf16[12,16,8,256]{3,2,1,0:T(8,128)(2,1)} %param.9) | copy-start | bytes 2359300
  6.4 0.7 %copy-start.2 = (f32[256]{0:T(256)S(1)}, f32[256]{0:T(256)}, u32[]{:S(2)}) copy-start(f32[256]{0:T(256)} %param.13) | copy-start | bytes 3076
  6.5 0.7 %copy-start.3 = (f32[256]{0:T(256)S(1)}, f32[256]{0:T(256)}, u32[]{:S(2)}) copy-start(f32[256]{0:T(256)} %param.12) | copy-start | bytes 3076
  7.9 2.0 %copy-start.1 = (bf16[3,3,3,256,256]{4,3,2,1,0:T(8,128)(2,1)S(1)}, bf16[3,3,3,256,256]{4,3,2,1,0:T(8,128)(2,1)}, u32[]{:S(2)}) copy-start(bf16[3,3,3,256,256]{4,3,2,1,0:T(8,128)(2,1)} %param.14) | copy-start | bytes 10616836
  12.3 2.0 %copy-start.6 = (f32[256]{0:T(256)S(1)}, f32[256]{0:T(256)}, u32[]{:S(2)}) copy-start(f32[256]{0:T(256)} %param.15) | copy-start | bytes 3076
  19.5 27.8 %copy-start.4 = (f32[256]{0:T(256)S(1)}, f32[256]{0:T(256)}, u32[]{:S(2)}) copy-start(f32[256]{0:T(256)} %param.17) | copy-start | bytes 3076
  19.5 27.8 %copy-start.5 = (f32[256]{0:T(256)S(1)}, f32[256]{0:T(256)}, u32[]{:S(2)}) copy-start(f32[256]{0:T(256)} %param.16) | copy-start | bytes 3076
  19.5 27.6 %all-to-all-start = ((bf16[16,104,256]{2,1,0:T(8,128)(2,1)}), bf16[16,104,256]{2,1,0:T(8,128)(2,1)S(1)}, u32[]{:S(2)}, u32[]{:S(2)}) async-start(bf16[16,104,256]{2,1,0:T(8,128)(2,1)} %pad_maximum_fusion.1), calls=%async_computation | async-start | bytes 1703936 | tf_op jit(solution)/shard_map/all_to_all | solution.py:122

commit v18 on v13

--- a/solution.py
+++ b/solution.py
@@ -125,11 +125,6 @@
     stat_part = received[:, per_dest * tile_rows * columns :].astype(jnp.float32)
     src_mean = stat_part[:, 0] + stat_part[:, 2]
     src_inverse = stat_part[:, 1] + stat_part[:, 3]
-    normed_part = (block_part.astype(jnp.float32) - src_mean[:, None, None, None, :]) * src_inverse[
-        :, None, None, None, :
-    ] * out_scale + out_offset
-    normed_part = jax.nn.silu(normed_part).astype(jnp.bfloat16)
-
     local_slot = jnp.arange(worker_tiles, dtype=jnp.int32)
     tile_id = local_slot * devices + device
     placed = jnp.sum((starts[None, :] <= tile_id[:, None]).astype(jnp.int32), axis=1) - 1
@@ -139,8 +134,17 @@
     row_of = jnp.arange(tile_rows, dtype=jnp.int32)[:, None]
     take_from = (clip_id[None, :] * tile_rows + row_of) * per_dest + (within // NRB // classes)[None, :]
     rows_all = devices * tile_rows * per_dest
-    block_mine = jnp.take(block_part.reshape(rows_all, columns, channels), take_from, axis=0)
-    normed_mine = jnp.take(normed_part.reshape(rows_all, columns, channels), take_from, axis=0)
+    block_mine = jnp.take(block_part.reshape(rows_all, columns, channels), take_from, axis=0, mode="clip")
+    tile_mean = jnp.broadcast_to(src_mean[0], (worker_tiles, channels))
+    tile_inverse = jnp.broadcast_to(src_inverse[0], (worker_tiles, channels))
+    for source in range(1, devices):
+        hit = (clip_id == source)[:, None]
+        tile_mean = jnp.where(hit, src_mean[source], tile_mean)
+        tile_inverse = jnp.where(hit, src_inverse[source], tile_inverse)
+    normed_mine = (block_mine.astype(jnp.float32) - tile_mean[None, :, None, :]) * tile_inverse[
+        None, :, None, :
+    ] * out_scale + out_offset
+    normed_mine = jax.nn.silu(normed_mine).astype(jnp.bfloat16)
     return (block_mine, normed_mine)
 
 

time: 50.1 us -> 49.5 us (0.988)
  local copies, waits for them, and re-layouts: 6.2 us -> 5.52 us
    select_n x2, other arithmetic: 0.94 us -> 0.3 us  [the longest x1 0.15 us: local(): tile_mean = jnp.where(hit, src_mean[source], tile_mean)]
    gather x2 -> x1, local copies, waits for them, and re-layouts: 1.19 us -> 0.6 us  [local(): jnp.take(block_part.reshape(rows_all, columns, channels), take_from, axis...]
    unnamed x19 -> x18, local copies, waits for them, and re-layouts: 2.74 us -> 2.73 us
where the time goes in v18:
time: 49.5 us; the launch traced here: 49.1 us
  waiting for transfers between devices  20.5 us (41%)
  other arithmetic  8.38 us (17%)
  starting transfers between devices  6.61 us (13%)
  matrix products  6.43 us (13%)
  local copies, waits for them, and re-layouts  5.52 us (11%)
  between operations  1.69 us (3%)
    all_to_all x1, waiting for transfers between devices, local(): lax.all_to_all(outgoing, 'tile', split_axis=0, concat_axis=0, tiled=True)  20.5 us
    all_to_all x1, starting transfers between devices, local(): lax.all_to_all(outgoing, 'tile', split_axis=0, concat_axis=0, tiled=True)  6.61 us
    dot_general x3, matrix products, local(): jnp.dot(unfolded.reshape(-1, 9 * channels), kernel[frame_lag], preferred_...  6.43 us
    unnamed x18, local copies, waits for them, and re-layouts  2.73 us
    convert_element_type x1, other arithmetic, local(): normalize(latents.astype(jnp.float32), live_frames, norm_scale, norm_offset)  1.7 us
    reduce_sum x2, other arithmetic, normalize(): second = jnp.sum(jnp.sum(flat * flat, axis=1) * live_mask, axis=0)  1.47 us
  transfers between devices with their start and end apart: 1, of which 1 were waited for; matrix products, arithmetic and copies ran while one was open for 1% of the time, Pallas kernels for 0%

profile of v18, /device:TPU:9, one launch (start us, length us, event | category | flops | bytes accessed | tf_op | source)
XLA Modules:
  0.0 49.1 jit_solution(6495069853682616934)
XLA Ops:
  0.6 0.7 %pad_add_fusion = s32[2,16]{1,0:T(2,128)S(1)} fusion(s32[1,16]{1,0:T(1,128)} %bitcast.120, s32[1,16]{1,0:T(1,128)} %bitcast.121), kind=kLoop, calls=%fused_computation.96 | loop fusion | flops 32 | bytes 256 | tf_op jit(solution)/shard_map/stack | solution.py:50
  1.4 1.4 %fusion.24 = (f32[12,256]{1,0:T(8,128)S(1)}, f32[12,256]{1,0:T(8,128)S(1)}) fusion(bf16[12,16,8,256]{3,2,1,0:T(8,128)(2,1)} %param.9), kind=kLoop, calls=%fused_computation.35 | loop fusion | flops 1566720 | bytes 811008 | tf_op jit(solution)/shard_map/reduce_sum | solution.py:21
  2.7 0.6 %select_reduce_fusion = (f32[]{:T(128)}, f32[12]{0:T(128)S(1)}) fusion(s32[16]{0:T(128)S(1)} %get-tuple-element.58, pred[16]{0:T(512)(128)(4,1)S(1)} %iota_compare_fusion.3), kind=kLoop, calls=%fused_computation.59 | loop fusion | flops 947 | bytes 132 | tf_op jit(solution)/shard_map/reduce_sum | solution.py:19
  4.9 1.7 %fusion.23 = bf16[12,16,8,256]{3,2,1,0:T(8,128)(2,1)S(1)} fusion(bf16[12,16,8,256]{3,2,1,0:T(8,128)(2,1)} %param.9, f32[256]{0:T(256)} %param.13, f32[256]{0:T(256)} %param.12, f32[256]{0:T(256)S(1)} %mul.167, f32[256]{0:T(256)S(1)} %sub.96), kind=kLoop, calls=%fused_computation.34 | loop fusion | flops 3932160 | bytes 1576960 | tf_op jit(solution)/shard_map/convert_element_type | solution.py:66
  6.6 0.2 fusion.25
  6.9 0.2 fusion.27
  7.1 0.2 fusion.28
  7.4 0.2 fusion.30
  7.6 0.2 fusion.31
  7.9 0.2 fusion.33
  8.1 1.5 %copy-done = bf16[3,3,3,256,256]{4,3,2,1,0:T(8,128)(2,1)S(1)} copy-done((bf16[3,3,3,256,256]{4,3,2,1,0:T(8,128)(2,1)S(1)}, bf16[3,3,3,256,256]{4,3,2,1,0:T(8,128)(2,1)}, u32[]{:S(2)}) %copy-start) | copy-done | bytes 3538968
  9.6 0.3 fusion.42
  9.9 2.1 %fusion.2 = f32[1536,256]{1,0:T(8,128)S(1)} fusion(bf16[2304,256]{1,0:T(8,128)(2,1)S(1)} %bitcast.81, bf16[1792,2304]{1,0:T(8,128)(2,1)S(1)} %bitcast.84), kind=kOutput, calls=%fused_computation.3 | convolution fusion | flops 1811939328 | bytes 9830400 | tf_op jit(solution)/shard_map/dot_general | solution.py:80
  12.0 2.1 %fusion.6 = f32[1536,256]{1,0:T(8,128)S(1)} fusion(f32[1536,256]{1,0:T(8,128)S(1)} %fusion.2, bf16[2304,256]{1,0:T(8,128)(2,1)S(1)} %bitcast.80, bf16[1792,2304]{1,0:T(8,128)(2,1)S(1)} %bitcast.85), kind=kOutput, calls=%fused_computation.16 | convolution fusion | flops 1812332544 | bytes 11403264 | tf_op jit(solution)/shard_map/dot_general | solution.py:80
  14.1 2.3 %fusion.12 = (f32[256]{0:T(256)S(1)}, f32[256]{0:T(256)S(1)}, f32[1536,256]{1,0:T(8,128)S(1)}) fusion(f32[1536]{0:T(1024)S(1)} %broadcast_bitcast_fusion, f32[256]{0:T(256)S(1)} %copy-done.2, f32[1536,256]{1,0:T(8,128)S(1)} %fusion.6, bf16[2304,256]{1,0:T(8,128)(2,1)S(1)} %bitcast.79, bf16[1792,2304]{1,0:T(8,128)(2,1)S(1)} %bitcast.86), kind=kOutput, calls=%fused_computation.23 | convolution fusion | flops 1815477760 | bytes 11414528 | tf_op jit(solution)/shard_map/dot_general | solution.py:80
  16.4 0.2 add_convert_fusion.1
  16.8 0.2 select_reduce_fusion.4
  18.7 1.0 %pad_maximum_fusion = bf16[16,104,256]{2,1,0:T(8,128)(2,1)} fusion(bf16[16,8,256]{2,1,0:T(8,128)(2,1)S(1)} %broadcast_in_dim.441, bf16[16,96,256]{2,1,0:T(8,128)(2,1)S(1)} %broadcast_select_fusion), kind=kLoop, calls=%fused_computation.47 | loop fusion | flops 1703936 | bytes 1703936 | tf_op jit(solution)/shard_map/concatenate | solution.py:120
  19.6 6.6 %all-to-all-start = ((bf16[16,104,256]{2,1,0:T(8,128)(2,1)}), bf16[16,104,256]{2,1,0:T(8,128)(2,1)S(1)}, u32[]{:S(2)}, u32[]{:S(2)}) async-start(bf16[16,104,256]{2,1,0:T(8,128)(2,1)} %pad_maximum_fusion), calls=%async_computation | async-start | bytes 1703936 | tf_op jit(solution)/shard_map/all_to_all | solution.py:121
  26.6 20.5 %all-to-all-done = bf16[16,104,256]{2,1,0:T(8,128)(2,1)S(1)} async-done(((bf16[16,104,256]{2,1,0:T(8,128)(2,1)}), bf16[16,104,256]{2,1,0:T(8,128)(2,1)S(1)}, u32[]{:S(2)}, u32[]{:S(2)}) %all-to-all-start) | async-done | bytes 852000 | tf_op jit(solution)/shard_map/all_to_all | solution.py:121
  47.3 0.6 %gather_fusion = bf16[64,8,256]{2,1,0:T(8,128)(2,1)S(1)} fusion(bf16[192,8,256]{2,1,0:T(8,128)(2,1)S(1)} %bitcast.78, s32[1024]{0:T(1024)S(1)} %pad_clamp_fusion), kind=kCustom, calls=%fused_computation | custom fusion | bytes 524544 | tf_op jit(solution)/shard_map/jit(_take)/gather | solution.py:137
  47.9 0.1 select_select_fusion.1
  48.1 0.1 select_select_fusion
  48.2 0.9 %multiply_convert_fusion = bf16[2,32,8,256]{3,2,1,0:T(8,128)(2,1)} fusion(bf16[2,32,8,256]{3,2,1,0:T(8,128)(2,1)S(1)} %bitcast.82, f32[256]{0:T(256)S(1)} %copy-done.3, f32[256]{0:T(256)S(1)} %copy-done.4, f32[32,256]{1,0:T(8,128)S(1)} %select_select_fusion, f32[32,256]{1,0:T(8,128)S(1)} %select_select_fusion.1), kind=kLoop, calls=%fused_computation.49 | loop fusion | flops 1310720 | bytes 591872 | tf_op jit(solution)/shard_map/convert_element_type | solution.py:147
  (68 shorter events, 3.4 us)
Async XLA Ops:
  7.6 2.0 %copy-start = (bf16[3,3,3,256,256]{4,3,2,1,0:T(8,128)(2,1)S(1)}, bf16[3,3,3,256,256]{4,3,2,1,0:T(8,128)(2,1)}, u32[]{:S(2)}) copy-start(bf16[3,3,3,256,256]{4,3,2,1,0:T(8,128)(2,1)} %param.14) | copy-start | bytes 10616836
  12.0 2.1 %copy-start.2 = (f32[256]{0:T(256)S(1)}, f32[256]{0:T(256)}, u32[]{:S(2)}) copy-start(f32[256]{0:T(256)} %param.15) | copy-start | bytes 3076
  19.6 27.5 %all-to-all-start = ((bf16[16,104,256]{2,1,0:T(8,128)(2,1)}), bf16[16,104,256]{2,1,0:T(8,128)(2,1)S(1)}, u32[]{:S(2)}, u32[]{:S(2)}) async-start(bf16[16,104,256]{2,1,0:T(8,128)(2,1)} %pad_maximum_fusion), calls=%async_computation | async-start | bytes 1703936 | tf_op jit(solution)/shard_map/all_to_all | solution.py:121
  26.2 22.0 %copy-start.3 = (f32[256]{0:T(256)S(1)}, f32[256]{0:T(256)}, u32[]{:S(2)}) copy-start(f32[256]{0:T(256)} %param.17) | copy-start | bytes 3076
  26.3 22.0 %copy-start.4 = (f32[256]{0:T(256)S(1)}, f32[256]{0:T(256)}, u32[]{:S(2)}) copy-start(f32[256]{0:T(256)} %param.16) | copy-start | bytes 3076
  47.9 1.2 %copy-start.1 = (bf16[64,8,256]{2,1,0:T(8,128)(2,1)}, bf16[64,8,256]{2,1,0:T(8,128)(2,1)S(1)}, u32[]{:S(2)}) copy-start(bf16[64,8,256]{2,1,0:T(8,128)(2,1)S(1)} %gather_fusion) | copy-start | bytes 786436

commit v19 on v18

--- a/solution.py
+++ b/solution.py
@@ -66,7 +66,7 @@
     active = normalize(latents.astype(jnp.float32), live_frames, norm_scale, norm_offset).astype(
         jnp.bfloat16
     )
-    padded = jnp.pad(active, ((2, 0), (1, 1), (1, 1), (0, 0)))
+    padded = jnp.pad(active, ((0, 0), (1, 1), (1, 1), (0, 0)))
     unfolded = jnp.concatenate(
         [
             padded[:, row_tap : row_tap + frame_rows, col_tap : col_tap + columns]
@@ -74,17 +74,18 @@
             for col_tap in range(3)
         ],
         axis=-1,
-    ).reshape(frames + 2, frame_rows * columns, 9 * channels)
+    ).reshape(frames * frame_rows * columns, 9 * channels)
     kernel = conv_weight.reshape(3, 9 * channels, -1)
     spread_out = [
-        jnp.dot(
-            unfolded.reshape(-1, 9 * channels), kernel[frame_lag], preferred_element_type=jnp.float32
-        ).reshape(frames + 2, frame_rows * columns, -1)
+        jnp.pad(
+            jnp.dot(unfolded, kernel[frame_lag], preferred_element_type=jnp.float32).reshape(
+                frames, frame_rows * columns, -1
+            ),
+            ((2 - frame_lag, 0), (0, 0), (0, 0)),
+        )[:frames]
         for frame_lag in range(3)
     ]
-    conv = conv_bias + sum(
-        spread_out[frame_lag][frame_lag : frame_lag + frames] for frame_lag in range(3)
-    )
+    conv = conv_bias + sum(spread_out)
     conv = conv.reshape(frames, frame_rows, columns, -1)
     block_out = conv.astype(jnp.bfloat16)
     per_group = channels // GROUPS

time: 49.5 us -> 49.4 us (level)
    dot_general x3 -> x1, matrix products: 6.43 us -> 2 us  [local(): jnp.dot(unfolded, kernel[frame_lag], preferred_element_type=jnp.float32)]
    slice x0 -> x2, matrix products: none -> 4.21 us  [local(): jnp.pad(jnp.dot(unfolded, kernel[frame_lag], preferred_element_type=jnp.f...]
    unnamed x0 -> x1, other arithmetic: none -> 0.55 us
    unnamed x18 -> x23, local copies, waits for them, and re-layouts: 2.73 us -> 2.92 us
where the time goes in v19:
time: 49.4 us; the launch traced here: 49 us
  waiting for transfers between devices  20.5 us (41%)
  other arithmetic  8.31 us (17%)
  starting transfers between devices  6.61 us (13%)
  matrix products  6.22 us (13%)
  local copies, waits for them, and re-layouts  5.67 us (11%)
  between operations  1.71 us (3%)
    all_to_all x1, waiting for transfers between devices, local(): lax.all_to_all(outgoing, 'tile', split_axis=0, concat_axis=0, tiled=True)  20.5 us
    all_to_all x1, starting transfers between devices, local(): lax.all_to_all(outgoing, 'tile', split_axis=0, concat_axis=0, tiled=True)  6.61 us
    slice x2, matrix products, local(): jnp.pad(jnp.dot(unfolded, kernel[frame_lag], preferred_element_type=jnp.f...  4.21 us
    unnamed x23, local copies, waits for them, and re-layouts  2.92 us
    dot_general x1, matrix products, local(): jnp.dot(unfolded, kernel[frame_lag], preferred_element_type=jnp.float32)  2 us
    reduce_sum x2, other arithmetic, normalize(): second = jnp.sum(jnp.sum(flat * flat, axis=1) * live_mask, axis=0)  1.47 us
    convert_element_type x1, other arithmetic, local(): normalize(latents.astype(jnp.float32), live_frames, norm_scale, norm_offset)  1.24 us
  transfers between devices with their start and end apart: 1, of which 1 were waited for; matrix products, arithmetic and copies ran while one was open for 1% of the time, Pallas kernels for 0%

profile of v19, /device:TPU:9, one launch (start us, length us, event | category | flops | bytes accessed | tf_op | source)
XLA Modules:
  0.0 49.0 jit_solution(15876440031788191496)
XLA Ops:
  0.6 0.8 %pad_add_fusion = s32[2,16]{1,0:T(2,128)S(1)} fusion(s32[1,16]{1,0:T(1,128)} %bitcast.131, s32[1,16]{1,0:T(1,128)} %bitcast.132), kind=kLoop, calls=%fused_computation.91 | loop fusion | flops 32 | bytes 256 | tf_op jit(solution)/shard_map/stack | solution.py:50
  1.4 1.4 %fusion.18 = (f32[12,256]{1,0:T(8,128)S(1)}, f32[12,256]{1,0:T(8,128)S(1)}) fusion(bf16[12,16,8,256]{3,2,1,0:T(8,128)(2,1)} %param.9), kind=kLoop, calls=%fused_computation.32 | loop fusion | flops 1566720 | bytes 811008 | tf_op jit(solution)/shard_map/reduce_sum | solution.py:21
  2.8 0.6 %select_reduce_fusion = (f32[]{:T(128)}, f32[12]{0:T(128)S(1)}) fusion(s32[16]{0:T(128)S(1)} %get-tuple-element.58, pred[16]{0:T(512)(128)(4,1)S(1)} %iota_compare_fusion.3), kind=kLoop, calls=%fused_computation.55 | loop fusion | flops 947 | bytes 132 | tf_op jit(solution)/shard_map/reduce_sum | solution.py:19
  4.9 1.2 %fusion.17 = bf16[12,16,8,256]{3,2,1,0:T(8,128)(2,1)S(1)} fusion(bf16[12,16,8,256]{3,2,1,0:T(8,128)(2,1)S(1)} %copy-done, f32[256]{0:T(256)} %param.13, f32[256]{0:T(256)} %param.12, f32[256]{0:T(256)S(1)} %mul.163, f32[256]{0:T(256)S(1)} %sub.96), kind=kLoop, calls=%fused_computation.31 | loop fusion | flops 3932160 | bytes 1576960 | tf_op jit(solution)/shard_map/convert_element_type | solution.py:66
  6.2 0.2 fusion.21
  6.5 0.2 fusion.23
  6.7 0.2 fusion.24
  6.8 0.3 copy-done.3
  7.1 0.5 %constant_dynamic-update-slice_fusion = bf16[12,16,8,2304]{3,2,1,0:T(8,128)(2,1)S(1)} fusion(bf16[12,16,8,2304]{3,2,1,0:T(8,128)(2,1)S(1)} %fusion.24, f32[256]{0:T(256)S(1)} %copy-done.3, f32[256]{0:T(256)S(1)} %copy-done.4, f32[256]{0:T(256)S(1)} %mul.163, f32[256]{0:T(256)S(1)} %sub.96, bf16[12,16,8,256]{3,2,1,0:T(8,128)(2,1)S(1)} %copy-done), kind=kLoop, calls=%fused_computation.50 | loop fusion | flops 3932160 | bytes 1576960
  7.7 0.2 fusion.25
  7.9 0.2 fusion.26
  8.2 0.2 fusion.28
  8.4 1.5 %copy-done.1 = bf16[3,3,3,256,256]{4,3,2,1,0:T(8,128)(2,1)S(1)} copy-done((bf16[3,3,3,256,256]{4,3,2,1,0:T(8,128)(2,1)S(1)}, bf16[3,3,3,256,256]{4,3,2,1,0:T(8,128)(2,1)}, u32[]{:S(2)}) %copy-start.1) | copy-done | bytes 3538968
  9.9 0.4 fusion.37
  10.3 2.0 %fusion.2 = f32[12,128,256]{2,1,0:T(8,128)S(1)} fusion(bf16[2304,256,1]{1,0,2:T(8,128)(2,1)S(1)} %bitcast.94, bf16[12,16,8,2304]{3,2,1,0:T(8,128)(2,1)S(1)} %fusion.28), kind=kOutput, calls=%fused_computation.3 | convolution fusion | flops 1660944384 | bytes 9830400 | tf_op jit(solution)/shard_map/slice | solution.py:80
  12.3 2.0 %fusion = f32[12,128,256]{2,1,0:T(8,128)S(1)} fusion(bf16[2304,256,1]{1,0,2:T(8,128)(2,1)S(1)} %bitcast.93, bf16[12,16,8,2304]{3,2,1,0:T(8,128)(2,1)S(1)} %fusion.28), kind=kOutput, calls=%fused_computation.1 | convolution fusion | flops 1811939328 | bytes 9830400 | tf_op jit(solution)/shard_map/dot_general | solution.py:81
  14.3 2.2 %fusion.6 = (f32[256]{0:T(256)S(1)}, f32[256]{0:T(256)S(1)}, bf16[12,128,256]{2,1,0:T(8,128)(2,1)S(1)}) fusion(f32[12]{0:T(128)S(1)} %get-tuple-element.7, f32[12,128,256]{2,1,0:T(8,128)S(1)} %fusion, f32[12,128,256]{2,1,0:T(8,128)S(1)} %fusion.2, bf16[2304,256,1]{1,0,2:T(8,128)(2,1)S(1)} %bitcast.92, bf16[12,16,8,2304]{3,2,1,0:T(8,128)(2,1)S(1)} %fusion.28, ...), kind=kOutput, calls=%fused_computation.20 | convolution fusion | flops 1513881088 | bytes 12192816 | tf_op jit(solution)/shard_map/slice | solution.py:80
  16.7 0.2 select_reduce_fusion.4
  18.6 1.0 %pad_maximum_fusion = bf16[16,104,256]{2,1,0:T(8,128)(2,1)} fusion(bf16[16,8,256]{2,1,0:T(8,128)(2,1)S(1)} %broadcast_in_dim.441, bf16[16,96,256]{2,1,0:T(8,128)(2,1)S(1)} %broadcast_select_fusion), kind=kLoop, calls=%fused_computation.34 | loop fusion | flops 1703936 | bytes 1703936 | tf_op jit(solution)/shard_map/concatenate | solution.py:121
  19.5 6.6 %all-to-all-start = ((bf16[16,104,256]{2,1,0:T(8,128)(2,1)}), bf16[16,104,256]{2,1,0:T(8,128)(2,1)S(1)}, u32[]{:S(2)}, u32[]{:S(2)}) async-start(bf16[16,104,256]{2,1,0:T(8,128)(2,1)} %pad_maximum_fusion), calls=%async_computation | async-start | bytes 1703936 | tf_op jit(solution)/shard_map/all_to_all | solution.py:122
  26.5 20.5 %all-to-all-done = bf16[16,104,256]{2,1,0:T(8,128)(2,1)S(1)} async-done(((bf16[16,104,256]{2,1,0:T(8,128)(2,1)}), bf16[16,104,256]{2,1,0:T(8,128)(2,1)S(1)}, u32[]{:S(2)}, u32[]{:S(2)}) %all-to-all-start) | async-done | bytes 852000 | tf_op jit(solution)/shard_map/all_to_all | solution.py:122
  47.2 0.6 %gather_fusion = bf16[64,8,256]{2,1,0:T(8,128)(2,1)S(1)} fusion(bf16[192,8,256]{2,1,0:T(8,128)(2,1)S(1)} %bitcast.91, s32[1024]{0:T(1024)S(1)} %pad_clamp_fusion), kind=kCustom, calls=%fused_computation | custom fusion | bytes 524544 | tf_op jit(solution)/shard_map/jit(_take)/gather | solution.py:138
  47.8 0.1 select_select_fusion.1
  48.1 0.9 %multiply_convert_fusion = bf16[2,32,8,256]{3,2,1,0:T(8,128)(2,1)} fusion(bf16[2,32,8,256]{3,2,1,0:T(8,128)(2,1)S(1)} %bitcast.95, f32[256]{0:T(256)S(1)} %copy-done.5, f32[256]{0:T(256)S(1)} %copy-done.6, f32[32,256]{1,0:T(8,128)S(1)} %select_select_fusion, f32[32,256]{1,0:T(8,128)S(1)} %select_select_fusion.1), kind=kLoop, calls=%fused_computation.44 | loop fusion | flops 1310720 | bytes 591872 | tf_op jit(solution)/shard_map/convert_element_type | solution.py:148
  (72 shorter events, 3.4 us)
Async XLA Ops:
  0.6 4.3 %copy-start = (bf16[12,16,8,256]{3,2,1,0:T(8,128)(2,1)S(1)}, bf16[12,16,8,256]{3,2,1,0:T(8,128)(2,1)}, u32[]{:S(2)}) copy-start(bf16[12,16,8,256]{3,2,1,0:T(8,128)(2,1)} %param.9) | copy-start | bytes 2359300
  6.4 0.7 %copy-start.3 = (f32[256]{0:T(256)S(1)}, f32[256]{0:T(256)}, u32[]{:S(2)}) copy-start(f32[256]{0:T(256)} %param.13) | copy-start | bytes 3076
  6.5 0.7 %copy-start.4 = (f32[256]{0:T(256)S(1)}, f32[256]{0:T(256)}, u32[]{:S(2)}) copy-start(f32[256]{0:T(256)} %param.12) | copy-start | bytes 3076
  7.9 2.0 %copy-start.1 = (bf16[3,3,3,256,256]{4,3,2,1,0:T(8,128)(2,1)S(1)}, bf16[3,3,3,256,256]{4,3,2,1,0:T(8,128)(2,1)}, u32[]{:S(2)}) copy-start(bf16[3,3,3,256,256]{4,3,2,1,0:T(8,128)(2,1)} %param.14) | copy-start | bytes 10616836
  12.3 2.0 %copy-start.7 = (f32[256]{0:T(256)S(1)}, f32[256]{0:T(256)}, u32[]{:S(2)}) copy-start(f32[256]{0:T(256)} %param.15) | copy-start | bytes 3076
  19.5 27.5 %all-to-all-start = ((bf16[16,104,256]{2,1,0:T(8,128)(2,1)}), bf16[16,104,256]{2,1,0:T(8,128)(2,1)S(1)}, u32[]{:S(2)}, u32[]{:S(2)}) async-start(bf16[16,104,256]{2,1,0:T(8,128)(2,1)} %pad_maximum_fusion), calls=%async_computation | async-start | bytes 1703936 | tf_op jit(solution)/shard_map/all_to_all | solution.py:122
  26.1 22.0 %copy-start.5 = (f32[256]{0:T(256)S(1)}, f32[256]{0:T(256)}, u32[]{:S(2)}) copy-start(f32[256]{0:T(256)} %param.17) | copy-start | bytes 3076
  26.1 22.0 %copy-start.6 = (f32[256]{0:T(256)S(1)}, f32[256]{0:T(256)}, u32[]{:S(2)}) copy-start(f32[256]{0:T(256)} %param.16) | copy-start | bytes 3076
  47.8 1.2 %copy-start.2 = (bf16[64,8,256]{2,1,0:T(8,128)(2,1)}, bf16[64,8,256]{2,1,0:T(8,128)(2,1)S(1)}, u32[]{:S(2)}) copy-start(bf16[64,8,256]{2,1,0:T(8,128)(2,1)S(1)} %gather_fusion) | copy-start | bytes 786436

commit v20 on v19

--- a/solution.py
+++ b/solution.py
@@ -136,12 +136,11 @@
     take_from = (clip_id[None, :] * tile_rows + row_of) * per_dest + (within // NRB // classes)[None, :]
     rows_all = devices * tile_rows * per_dest
     block_mine = jnp.take(block_part.reshape(rows_all, columns, channels), take_from, axis=0, mode="clip")
-    tile_mean = jnp.broadcast_to(src_mean[0], (worker_tiles, channels))
-    tile_inverse = jnp.broadcast_to(src_inverse[0], (worker_tiles, channels))
+    src_stats = jnp.stack([src_mean, src_inverse], 1)
+    tile_stats = jnp.broadcast_to(src_stats[0], (worker_tiles, 2, channels))
     for source in range(1, devices):
-        hit = (clip_id == source)[:, None]
-        tile_mean = jnp.where(hit, src_mean[source], tile_mean)
-        tile_inverse = jnp.where(hit, src_inverse[source], tile_inverse)
+        tile_stats = jnp.where((clip_id == source)[:, None, None], src_stats[source], tile_stats)
+    tile_mean, tile_inverse = tile_stats[:, 0], tile_stats[:, 1]
     normed_mine = (block_mine.astype(jnp.float32) - tile_mean[None, :, None, :]) * tile_inverse[
         None, :, None, :
     ] * out_scale + out_offset

time: 49.4 us -> 49.2 us (level)
  no operation moved by 1% of the time
where the time goes in v20:
time: 49.2 us; the launch traced here: 48.9 us
  waiting for transfers between devices  20.5 us (42%)
  other arithmetic  8.2 us (17%)
  starting transfers between devices  6.61 us (13%)
  matrix products  6.22 us (13%)
  local copies, waits for them, and re-layouts  5.66 us (12%)
  between operations  1.71 us (3%)
    all_to_all x1, waiting for transfers between devices, local(): lax.all_to_all(outgoing, 'tile', split_axis=0, concat_axis=0, tiled=True)  20.5 us
    all_to_all x1, starting transfers between devices, local(): lax.all_to_all(outgoing, 'tile', split_axis=0, concat_axis=0, tiled=True)  6.61 us
    slice x2, matrix products, local(): jnp.pad(jnp.dot(unfolded, kernel[frame_lag], preferred_element_type=jnp.f...  4.21 us
    unnamed x23, local copies, waits for them, and re-layouts  2.92 us
    dot_general x1, matrix products, local(): jnp.dot(unfolded, kernel[frame_lag], preferred_element_type=jnp.float32)  2 us
    reduce_sum x2, other arithmetic, normalize(): second = jnp.sum(jnp.sum(flat * flat, axis=1) * live_mask, axis=0)  1.47 us
    convert_element_type x1, other arithmetic, local(): normalize(latents.astype(jnp.float32), live_frames, norm_scale, norm_offset)  1.24 us
  transfers between devices with their start and end apart: 1, of which 1 were waited for; matrix products, arithmetic and copies ran while one was open for 1% of the time, Pallas kernels for 0%

profile of v20, /device:TPU:9, one launch (start us, length us, event | category | flops | bytes accessed | tf_op | source)
XLA Modules:
  0.0 48.9 jit_solution(1595116224853113695)
XLA Ops:
  0.6 0.8 %pad_add_fusion = s32[2,16]{1,0:T(2,128)S(1)} fusion(s32[1,16]{1,0:T(1,128)} %bitcast.103, s32[1,16]{1,0:T(1,128)} %bitcast.104), kind=kLoop, calls=%fused_computation.154 | loop fusion | flops 32 | bytes 256 | tf_op jit(solution)/shard_map/stack | solution.py:50
  1.4 1.4 %fusion.18 = (f32[12,256]{1,0:T(8,128)S(1)}, f32[12,256]{1,0:T(8,128)S(1)}) fusion(bf16[12,16,8,256]{3,2,1,0:T(8,128)(2,1)} %param.9), kind=kLoop, calls=%fused_computation.32 | loop fusion | flops 1566720 | bytes 811008 | tf_op jit(solution)/shard_map/reduce_sum | solution.py:21
  2.8 0.6 %select_reduce_fusion = (f32[]{:T(128)}, f32[12]{0:T(128)S(1)}) fusion(s32[16]{0:T(128)S(1)} %get-tuple-element.44, pred[16]{0:T(512)(128)(4,1)S(1)} %iota_compare_fusion.3), kind=kLoop, calls=%fused_computation.86 | loop fusion | flops 947 | bytes 132 | tf_op jit(solution)/shard_map/reduce_sum | solution.py:19
  4.9 1.2 %fusion.17 = bf16[12,16,8,256]{3,2,1,0:T(8,128)(2,1)S(1)} fusion(bf16[12,16,8,256]{3,2,1,0:T(8,128)(2,1)S(1)} %copy-done, f32[256]{0:T(256)} %param.13, f32[256]{0:T(256)} %param.12, f32[256]{0:T(256)S(1)} %mul.165, f32[256]{0:T(256)S(1)} %sub.98), kind=kLoop, calls=%fused_computation.31 | loop fusion | flops 3932160 | bytes 1576960 | tf_op jit(solution)/shard_map/convert_element_type | solution.py:66
  6.2 0.2 fusion.21
  6.5 0.2 fusion.23
  6.7 0.2 fusion.24
  6.8 0.3 copy-done.3
  7.1 0.5 %constant_dynamic-update-slice_fusion = bf16[12,16,8,2304]{3,2,1,0:T(8,128)(2,1)S(1)} fusion(bf16[12,16,8,2304]{3,2,1,0:T(8,128)(2,1)S(1)} %fusion.24, f32[256]{0:T(256)S(1)} %copy-done.3, f32[256]{0:T(256)S(1)} %copy-done.4, f32[256]{0:T(256)S(1)} %mul.165, f32[256]{0:T(256)S(1)} %sub.98, bf16[12,16,8,256]{3,2,1,0:T(8,128)(2,1)S(1)} %copy-done), kind=kLoop, calls=%fused_computation.81 | loop fusion | flops 3932160 | bytes 1576960
  7.7 0.2 fusion.25
  7.9 0.2 fusion.26
  8.2 0.2 fusion.28
  8.4 1.5 %copy-done.1 = bf16[3,3,3,256,256]{4,3,2,1,0:T(8,128)(2,1)S(1)} copy-done((bf16[3,3,3,256,256]{4,3,2,1,0:T(8,128)(2,1)S(1)}, bf16[3,3,3,256,256]{4,3,2,1,0:T(8,128)(2,1)}, u32[]{:S(2)}) %copy-start.1) | copy-done | bytes 3538968
  9.9 0.4 fusion.68
  10.3 2.0 %fusion.2 = f32[12,128,256]{2,1,0:T(8,128)S(1)} fusion(bf16[2304,256,1]{1,0,2:T(8,128)(2,1)S(1)} %bitcast.98, bf16[12,16,8,2304]{3,2,1,0:T(8,128)(2,1)S(1)} %fusion.28), kind=kOutput, calls=%fused_computation.3 | convolution fusion | flops 1660944384 | bytes 9830400 | tf_op jit(solution)/shard_map/slice | solution.py:80
  12.3 2.0 %fusion = f32[12,128,256]{2,1,0:T(8,128)S(1)} fusion(bf16[2304,256,1]{1,0,2:T(8,128)(2,1)S(1)} %bitcast.97, bf16[12,16,8,2304]{3,2,1,0:T(8,128)(2,1)S(1)} %fusion.28), kind=kOutput, calls=%fused_computation.1 | convolution fusion | flops 1811939328 | bytes 9830400 | tf_op jit(solution)/shard_map/dot_general | solution.py:81
  14.3 2.2 %fusion.6 = (f32[256]{0:T(256)S(1)}, f32[256]{0:T(256)S(1)}, bf16[12,128,256]{2,1,0:T(8,128)(2,1)S(1)}) fusion(f32[12]{0:T(128)S(1)} %get-tuple-element.7, f32[12,128,256]{2,1,0:T(8,128)S(1)} %fusion, f32[12,128,256]{2,1,0:T(8,128)S(1)} %fusion.2, bf16[2304,256,1]{1,0,2:T(8,128)(2,1)S(1)} %bitcast.96, bf16[12,16,8,2304]{3,2,1,0:T(8,128)(2,1)S(1)} %fusion.28, ...), kind=kOutput, calls=%fused_computation.20 | convolution fusion | flops 1513881088 | bytes 12192816 | tf_op jit(solution)/shard_map/slice | solution.py:80
  16.7 0.2 select_reduce_fusion.4
  18.6 1.0 %pad_maximum_fusion = bf16[16,104,256]{2,1,0:T(8,128)(2,1)} fusion(bf16[16,8,256]{2,1,0:T(8,128)(2,1)S(1)} %broadcast_in_dim.282, bf16[16,96,256]{2,1,0:T(8,128)(2,1)S(1)} %broadcast_select_fusion), kind=kLoop, calls=%fused_computation.34 | loop fusion | flops 1703936 | bytes 1703936 | tf_op jit(solution)/shard_map/concatenate | solution.py:121
  19.5 6.6 %all-to-all-start = ((bf16[16,104,256]{2,1,0:T(8,128)(2,1)}), bf16[16,104,256]{2,1,0:T(8,128)(2,1)S(1)}, u32[]{:S(2)}, u32[]{:S(2)}) async-start(bf16[16,104,256]{2,1,0:T(8,128)(2,1)} %pad_maximum_fusion), calls=%async_computation | async-start | bytes 1703936 | tf_op jit(solution)/shard_map/all_to_all | solution.py:122
  26.5 20.5 %all-to-all-done = bf16[16,104,256]{2,1,0:T(8,128)(2,1)S(1)} async-done(((bf16[16,104,256]{2,1,0:T(8,128)(2,1)}), bf16[16,104,256]{2,1,0:T(8,128)(2,1)S(1)}, u32[]{:S(2)}, u32[]{:S(2)}) %all-to-all-start) | async-done | bytes 852000 | tf_op jit(solution)/shard_map/all_to_all | solution.py:122
  47.1 0.2 select_select_fusion
  47.4 0.6 %gather_fusion = bf16[64,8,256]{2,1,0:T(8,128)(2,1)S(1)} fusion(bf16[192,8,256]{2,1,0:T(8,128)(2,1)S(1)} %bitcast.95, s32[1024]{0:T(1024)S(1)} %pad_clamp_fusion), kind=kCustom, calls=%fused_computation | custom fusion | bytes 524544 | tf_op jit(solution)/shard_map/jit(_take)/gather | solution.py:138
  48.0 0.9 %multiply_convert_fusion = bf16[2,32,8,256]{3,2,1,0:T(8,128)(2,1)} fusion(bf16[2,32,8,256]{3,2,1,0:T(8,128)(2,1)S(1)} %bitcast.99, f32[256]{0:T(256)S(1)} %copy-done.5, f32[256]{0:T(256)S(1)} %copy-done.6, f32[32,256]{1,0:T(8,128)S(1)} %get-tuple-element.24, f32[32,256]{1,0:T(8,128)S(1)} %get-tuple-element.23), kind=kLoop, calls=%fused_computation.44 | loop fusion | flops 1310720 | bytes 591872 | tf_op jit(solution)/shard_map/convert_element_type | solution.py:147
  (72 shorter events, 3.3 us)
Async XLA Ops:
  0.6 4.3 %copy-start = (bf16[12,16,8,256]{3,2,1,0:T(8,128)(2,1)S(1)}, bf16[12,16,8,256]{3,2,1,0:T(8,128)(2,1)}, u32[]{:S(2)}) copy-start(bf16[12,16,8,256]{3,2,1,0:T(8,128)(2,1)} %param.9) | copy-start | bytes 2359300
  6.4 0.7 %copy-start.3 = (f32[256]{0:T(256)S(1)}, f32[256]{0:T(256)}, u32[]{:S(2)}) copy-start(f32[256]{0:T(256)} %param.13) | copy-start | bytes 3076
  6.5 0.7 %copy-start.4 = (f32[256]{0:T(256)S(1)}, f32[256]{0:T(256)}, u32[]{:S(2)}) copy-start(f32[256]{0:T(256)} %param.12) | copy-start | bytes 3076
  7.9 2.0 %copy-start.1 = (bf16[3,3,3,256,256]{4,3,2,1,0:T(8,128)(2,1)S(1)}, bf16[3,3,3,256,256]{4,3,2,1,0:T(8,128)(2,1)}, u32[]{:S(2)}) copy-start(bf16[3,3,3,256,256]{4,3,2,1,0:T(8,128)(2,1)} %param.14) | copy-start | bytes 10616836
  12.3 2.0 %copy-start.7 = (f32[256]{0:T(256)S(1)}, f32[256]{0:T(256)}, u32[]{:S(2)}) copy-start(f32[256]{0:T(256)} %param.15) | copy-start | bytes 3076
  19.5 27.5 %all-to-all-start = ((bf16[16,104,256]{2,1,0:T(8,128)(2,1)}), bf16[16,104,256]{2,1,0:T(8,128)(2,1)S(1)}, u32[]{:S(2)}, u32[]{:S(2)}) async-start(bf16[16,104,256]{2,1,0:T(8,128)(2,1)} %pad_maximum_fusion), calls=%async_computation | async-start | bytes 1703936 | tf_op jit(solution)/shard_map/all_to_all | solution.py:122
  26.1 21.9 %copy-start.5 = (f32[256]{0:T(256)S(1)}, f32[256]{0:T(256)}, u32[]{:S(2)}) copy-start(f32[256]{0:T(256)} %param.17) | copy-start | bytes 3076
  26.1 21.9 %copy-start.6 = (f32[256]{0:T(256)S(1)}, f32[256]{0:T(256)}, u32[]{:S(2)}) copy-start(f32[256]{0:T(256)} %param.16) | copy-start | bytes 3076
  48.0 0.9 %copy-start.2 = (bf16[64,8,256]{2,1,0:T(8,128)(2,1)}, bf16[64,8,256]{2,1,0:T(8,128)(2,1)S(1)}, u32[]{:S(2)}) copy-start(bf16[64,8,256]{2,1,0:T(8,128)(2,1)S(1)} %gather_fusion) | copy-start | bytes 786436
